TPU v7x, 32 devices: a whole 2x2x4 slice. The times are simulated.
32 devices in a mesh: slab: 2 (over y), genome: 4 (over x, core), group: 4 (over z).
Axes of the slice: x: 2, y: 2, z: 4, core: 2. Of those that a mesh axis runs over, the one named last changes fastest.
Arguments:
- genotypes: bfloat16 [640, 12288], P(None, ('slab', 'genome', 'group')), parts along dimension 1, may hold values from -6 to 6
Outputs:
- ld_score: float32 [12288], P(('slab', 'genome', 'group')), parts along dimension 0
There are 2 independent parts, one for each index of `slab`. A program takes and returns all parts, laid end to end along the dimension named above; each array names one. Nothing has to cross between parts.
All inputs are finite; a program needn't handle non-finite values.
Results may differ from a plain program's by a relative error of at most 0.0003.
Values may be sent and summed in bfloat16 or wider, within the bound.
No kernel may reach another device: no remote copies, remote signals or barrier semaphores. Data moves between devices by JAX's collectives and lax.ppermute only.
A program may use at most 64 MiB of HBM per device.

v0:
```python
import jax
import jax.numpy as jnp
from jax import lax
from jax.sharding import PartitionSpec as P


def passed_along(block, axis, distance):
    devices = range(lax.axis_size(axis))
    route = [(i - distance, i) for i in devices if i - distance in devices]
    return lax.ppermute(block, axis, route)


def per_device(genotypes):
    scaling = 1.0 / genotypes.shape[0]

    def squares(columns):
        band = (
            lax.dot_general(
                genotypes, columns, (((0,), (0,)), ((), ())), preferred_element_type=jnp.float32
            )
            * scaling
        )
        return jnp.sum(band * band, axis=1)

    gathered = lax.all_gather(genotypes, "group", axis=1, tiled=True)
    following = passed_along(gathered, "genome", -1)
    ld_score = squares(gathered) + squares(following)
    return ld_score


def solution(mesh):
    placed = (P(None, ("slab", "genome", "group")),)
    return jax.shard_map(
        per_device,
        mesh=mesh,
        in_specs=placed,
        out_specs=P(("slab", "genome", "group")),
        check_vma=False,
    )
```

profile of v0, /device:TPU:1, one launch (start us, length us, event | category | flops | bytes accessed | tf_op | source)
XLA Modules:
  0.0 89.7 jit_solution(2843091351955072725)
XLA Ops:
  6.5 0.0 all-gather.2.cloned.1.call-start
  6.5 0.0 copy-start
  6.5 0.7 all-gather.2.cloned.1.call-update
  7.3 47.5 %all-gather.2.cloned.1.call-done = bf16[640,1536]{1,0:T(8,128)(2,1)} async-done(((bf16[640,384]{1,0:T(8,128)(2,1)}), bf16[640,1536]{1,0:T(8,128)(2,1)}) %all-gather.2.cloned.1.call-update) | async-done | bytes 1966096 | tf_op jit(solution)/shard_map/all_gather | solution.py:25
  54.7 2.7 %collective-permute-start = (bf16[640,1536]{1,0:T(8,128)(2,1)}, bf16[640,1536]{1,0:T(8,128)(2,1)S(1)}, u32[]{:S(2)}, u32[]{:S(2)}) collective-permute-start(bf16[640,1536]{1,0:T(8,128)(2,1)} %all-gather.2.cloned.1.call-done), channel_id=1, source_target_pairs={{4,0},{8,4},{12,8},{5,1},{9,5},{13,9},{6,2},{10,6},{14,10},{7,3},{... | collective-permute-start | bytes 5898248 | tf_op jit(solution)/shard_map/ppermute | solution.py:10
  57.5 2.9 %fusion.2 = f32[384]{0:T(512)S(1)} fusion(bf16[640,384]{1,0:T(8,128)(2,1)} %param.1, bf16[640,1536]{1,0:T(8,128)(2,1)} %all-gather.2.cloned.1.call-done), kind=kOutput, calls=%fused_computation.4 | convolution fusion | flops 756743808 | bytes 2459136 | tf_op jit(solution)/shard_map/dot_general | solution.py:18
  60.4 20.7 %collective-permute-done = bf16[640,1536]{1,0:T(8,128)(2,1)S(1)} collective-permute-done((bf16[640,1536]{1,0:T(8,128)(2,1)}, bf16[640,1536]{1,0:T(8,128)(2,1)S(1)}, u32[]{:S(2)}, u32[]{:S(2)}) %collective-permute-start) | collective-permute-done | bytes 1966112 | tf_op jit(solution)/shard_map/ppermute | solution.py:10
  81.1 0.0 copy-done
  81.1 1.2 %fusion.3 = f32[384]{0:T(512)S(1)} fusion(bf16[640,384]{1,0:T(8,128)(2,1)S(1)} %copy-done, bf16[640,1536]{1,0:T(8,128)(2,1)S(1)} %collective-permute-done), kind=kOutput, calls=%fused_computation.5 | convolution fusion | flops 756743808 | bytes 2459136 | tf_op jit(solution)/shard_map/dot_general | solution.py:18
  82.2 0.6 add.3
Async XLA Ops:
  6.5 48.2 %all-gather.2.cloned.1.call-start = ((), (), s32[]{:S(2)}) async-start(), calls=%async_computation | async-start | bytes 2457600 | tf_op jit(solution)/shard_map/all_gather | solution.py:25
  6.5 74.5 %copy-start = (bf16[640,384]{1,0:T(8,128)(2,1)S(1)}, bf16[640,384]{1,0:T(8,128)(2,1)}, u32[]{:S(2)}) copy-start(bf16[640,384]{1,0:T(8,128)(2,1)} %param.1) | copy-start | bytes 1474564
  54.7 26.3 %collective-permute-start = (bf16[640,1536]{1,0:T(8,128)(2,1)}, bf16[640,1536]{1,0:T(8,128)(2,1)S(1)}, u32[]{:S(2)}, u32[]{:S(2)}) collective-permute-start(bf16[640,1536]{1,0:T(8,128)(2,1)} %all-gather.2.cloned.1.call-done), channel_id=1, source_target_pairs={{4,0},{8,4},{12,8},{5,1},{9,5},{13,9},{6,2},{10,6},{14,10},{7,3},{... | collective-permute-start | bytes 5898248 | tf_op jit(solution)/shard_map/ppermute | solution.py:10
Sparse Core Ops, SparseCore 0:
  9.0 45.7 all-gather.1
where the time goes:
time: 89.8 us; the launch traced here: 89.7 us
  waiting for transfers between devices  68.8 us (77%)
  between operations  13.4 us (15%)
  matrix products  4.09 us (5%)
  starting transfers between devices  2.75 us (3%)
    all_gather x1, waiting for transfers between devices, per_device(): gathered = lax.all_gather(genotypes, 'group', axis=1, tiled=True)  47.5 us
    ppermute x1, waiting for transfers between devices, passed_along(): return lax.ppermute(block, axis, route)  20.7 us
    dot_general x2, matrix products, squares(): lax.dot_general(genotypes, columns, (((0,), (0,)), ((), ())), preferred_e...  4.09 us
    ppermute x1, starting transfers between devices, passed_along(): return lax.ppermute(block, axis, route)  2.75 us
  transfers between devices with their start and end apart: 2, of which 2 were waited for; matrix products, arithmetic and copies ran while one was open for 3% of the time, Pallas kernels for 0%

commit v1 on v0

v1 whole, which is shorter than its diff:
```python
import jax
import jax.numpy as jnp
from jax import lax
from jax.sharding import PartitionSpec as P


def passed_along(block, axis, distance):
    devices = range(lax.axis_size(axis))
    route = [(i - distance, i) for i in devices if i - distance in devices]
    return lax.ppermute(block, axis, route)


def row_squares(rows, columns, scaling):
    band = (
        lax.dot_general(rows, columns, (((0,), (0,)), ((), ())), preferred_element_type=jnp.float32)
        * scaling
    )
    return jnp.sum(band * band, axis=1)


def general_plan(genotypes):
    scaling = 1.0 / genotypes.shape[0]
    gathered = lax.all_gather(genotypes, "group", axis=1, tiled=True)
    following = passed_along(gathered, "genome", -1)
    return row_squares(genotypes, gathered, scaling) + row_squares(genotypes, following, scaling)


def hub_plan(genotypes):
    scaling = 1.0 / genotypes.shape[0]
    own = genotypes
    adopt = lax.ppermute(own, "group", [(0, 1), (3, 2)])
    nbr = lax.ppermute(own, "group", [(1, 2), (2, 1)])
    far = lax.ppermute(adopt, "group", [(1, 2), (2, 1)])
    panel = [own, adopt, nbr, far]
    rows = [own, adopt]

    rows_next = [lax.ppermute(r, "genome", [(0, 0), (2, 2), (1, 3)]) for r in rows]
    panel_next = [lax.ppermute(c, "genome", [(1, 0), (3, 2), (2, 3)]) for c in panel]

    scores = []
    for r, rn in zip(rows, rows_next):
        within = sum(row_squares(r, c, scaling) for c in panel)
        following = sum(row_squares(rn, c, scaling) for c in panel_next)
        following = lax.ppermute(following, "genome", [(0, 0), (2, 2), (3, 1)])
        scores.append(within + following)

    at_hub = lax.ppermute(scores[0], "group", [(1, 1), (2, 2)])
    at_end = lax.ppermute(scores[1], "group", [(1, 0), (2, 3)])
    return at_hub + at_end


def solution(mesh):
    placed = (P(None, ("slab", "genome", "group")),)
    hub = mesh.shape["group"] == 4 and mesh.shape["genome"] == 4
    return jax.shard_map(
        hub_plan if hub else general_plan,
        mesh=mesh,
        in_specs=placed,
        out_specs=P(("slab", "genome", "group")),
        check_vma=False,
    )
```

time: 89.8 us -> 52.2 us (0.58)
  waiting for transfers between devices: 68.8 us -> 16.8 us
  starting transfers between devices: 2.75 us -> 24.6 us
  between operations: 13.4 us -> 0.24 us
  matrix products: 4.09 us -> 9.58 us
    all_gather x1 -> x0, waiting for transfers between devices: 47.5 us -> none  [per_device(): gathered = lax.all_gather(genotypes, 'group', axis=1, tiled=True)]
    ppermute x1 -> x13, starting transfers between devices: 2.75 us -> 24.6 us  [the longest x1 6.57 us: hub_plan(): adopt = lax.ppermute(own, 'group', [(0, 1), (3, 2)])]
    dot_general x2 -> x16, matrix products: 4.09 us -> 9.58 us  [row_squares(): lax.dot_general(rows, columns, (((0,), (0,)), ((), ())), preferred_elemen...]
    ppermute x1 -> x13, waiting for transfers between devices: 20.7 us -> 16.8 us  [the longest x1 12 us: hub_plan(): at_end = lax.ppermute(scores[1], 'group', [(1, 0), (2, 3)])]
  transfers between devices with their start and end apart: 2 -> 13, of which waited for: 2 -> 5; matrix products, arithmetic and copies ran while one was open for 3% -> 18% of each run, Pallas kernels for 0% -> 0%
where the time goes in v1:
time: 52.2 us; the launch traced here: 51.8 us
  starting transfers between devices  24.6 us (47%)
  waiting for transfers between devices  16.8 us (32%)
  matrix products  9.58 us (18%)
  other arithmetic  0.61 us (1%)
    ppermute x1, waiting for transfers between devices, hub_plan(): at_end = lax.ppermute(scores[1], 'group', [(1, 0), (2, 3)])  12 us
    dot_general x16, matrix products, row_squares(): lax.dot_general(rows, columns, (((0,), (0,)), ((), ())), preferred_elemen...  9.58 us
    ppermute x1, starting transfers between devices, hub_plan(): adopt = lax.ppermute(own, 'group', [(0, 1), (3, 2)])  6.57 us
    ppermute x2, starting transfers between devices, hub_plan(): lax.ppermute(r, 'genome', [(0, 0), (2, 2), (1, 3)])  6.29 us
    ppermute x4, starting transfers between devices, hub_plan(): lax.ppermute(c, 'genome', [(1, 0), (3, 2), (2, 3)])  5.68 us
    ppermute x2, starting transfers between devices, hub_plan(): following = lax.ppermute(following, 'genome', [(0, 0), (2, 2), (3, 1)])  2.58 us
    ppermute x2, waiting for transfers between devices, hub_plan(): following = lax.ppermute(following, 'genome', [(0, 0), (2, 2), (3, 1)])  2.4 us
    ppermute x1, waiting for transfers between devices, hub_plan(): adopt = lax.ppermute(own, 'group', [(0, 1), (3, 2)])  1.38 us
  transfers between devices with their start and end apart: 13, of which 5 were waited for; matrix products, arithmetic and copies ran while one was open for 18% of the time, Pallas kernels for 0%

profile of v1, /device:TPU:1, one launch (start us, length us, event | category | flops | bytes accessed | tf_op | source)
XLA Modules:
  0.0 51.8 jit_solution(14707600348277651622)
XLA Ops:
  0.0 0.8 %collective-permute-start.1 = (bf16[640,384]{1,0:T(8,128)(2,1)}, bf16[640,384]{1,0:T(8,128)(2,1)S(1)}, u32[]{:S(2)}, u32[]{:S(2)}) collective-permute-start(bf16[640,384]{1,0:T(8,128)(2,1)} %param.1), channel_id=1, source_target_pairs={{1,2},{2,1},{5,6},{6,5},{9,10},{10,9},{13,14},{14,13},{17,18},{18,... | collective-permute-start | bytes 1474568 | tf_op jit(solution)/shard_map/ppermute | solution.py:32
  0.8 6.6 %collective-permute-start = (bf16[640,384]{1,0:T(8,128)(2,1)}, bf16[640,384]{1,0:T(8,128)(2,1)S(1)}, u32[]{:S(2)}, u32[]{:S(2)}) collective-permute-start(bf16[640,384]{1,0:T(8,128)(2,1)} %param.1), channel_id=1, source_target_pairs={{0,1},{3,2},{4,5},{7,6},{8,9},{11,10},{12,13},{15,14},{16,17},{19,... | collective-permute-start | bytes 1474568 | tf_op jit(solution)/shard_map/ppermute | solution.py:31
  7.4 3.1 %collective-permute-start.3 = (bf16[640,384]{1,0:T(8,128)(2,1)}, bf16[640,384]{1,0:T(8,128)(2,1)S(1)}, u32[]{:S(2)}, u32[]{:S(2)}) collective-permute-start(bf16[640,384]{1,0:T(8,128)(2,1)} %param.1), channel_id=1, source_target_pairs={{0,0},{8,8},{4,12},{1,1},{9,9},{5,13},{2,2},{10,10},{6,14},{3,3},{... | collective-permute-start | bytes 1474568 | tf_op jit(solution)/shard_map/ppermute | solution.py:37
  10.6 1.7 %collective-permute-start.4 = (bf16[640,384]{1,0:T(8,128)(2,1)}, bf16[640,384]{1,0:T(8,128)(2,1)S(1)}, u32[]{:S(2)}, u32[]{:S(2)}) collective-permute-start(bf16[640,384]{1,0:T(8,128)(2,1)} %param.1), channel_id=1, source_target_pairs={{4,0},{12,8},{8,12},{5,1},{13,9},{9,13},{6,2},{14,10},{10,14},{7,3... | collective-permute-start | bytes 1474568 | tf_op jit(solution)/shard_map/ppermute | solution.py:38
  12.3 1.7 %fusion.16 = f32[384]{0:T(512)S(1)} fusion(bf16[640,384]{1,0:T(8,128)(2,1)} %param.1), kind=kOutput, calls=%fused_computation.32 | convolution fusion | flops 189185664 | bytes 493056 | tf_op jit(solution)/shard_map/dot_general | solution.py:15
  14.0 1.3 %collective-permute-start.6 = (bf16[640,384]{1,0:T(8,128)(2,1)S(1)}, bf16[640,384]{1,0:T(8,128)(2,1)S(1)}, u32[]{:S(2)}, u32[]{:S(2)}) collective-permute-start(bf16[640,384]{1,0:T(8,128)(2,1)S(1)} %collective-permute-done.1), channel_id=1, source_target_pairs={{4,0},{12,8},{8,12},{5,1},{13,9},{9,13},{6,2},{14,10},{10,14},{7,3... | collective-permute-start | bytes 1474568 | tf_op jit(solution)/shard_map/ppermute | solution.py:38
  15.3 0.5 %fusion.18 = f32[384]{0:T(512)S(1)} fusion(bf16[640,384]{1,0:T(8,128)(2,1)S(1)} %copy-done, bf16[640,384]{1,0:T(8,128)(2,1)S(1)} %collective-permute-done.1), kind=kOutput, calls=%fused_computation.34 | convolution fusion | flops 189185664 | bytes 984576 | tf_op jit(solution)/shard_map/dot_general | solution.py:15
  15.9 1.4 %collective-permute-done = bf16[640,384]{1,0:T(8,128)(2,1)S(1)} collective-permute-done((bf16[640,384]{1,0:T(8,128)(2,1)}, bf16[640,384]{1,0:T(8,128)(2,1)S(1)}, u32[]{:S(2)}, u32[]{:S(2)}) %collective-permute-start) | collective-permute-done | bytes 491552 | tf_op jit(solution)/shard_map/ppermute | solution.py:31
  17.8 3.1 %collective-permute-start.10 = (bf16[640,384]{1,0:T(8,128)(2,1)S(1)}, bf16[640,384]{1,0:T(8,128)(2,1)S(1)}, u32[]{:S(2)}, u32[]{:S(2)}) collective-permute-start(bf16[640,384]{1,0:T(8,128)(2,1)S(1)} %collective-permute-done), channel_id=1, source_target_pairs={{0,0},{8,8},{4,12},{1,1},{9,9},{5,13},{2,2},{10,10},{6,14},{3,3},{... | collective-permute-start | bytes 1474568 | tf_op jit(solution)/shard_map/ppermute | solution.py:37
  20.9 1.3 %collective-permute-start.5 = (bf16[640,384]{1,0:T(8,128)(2,1)S(1)}, bf16[640,384]{1,0:T(8,128)(2,1)S(1)}, u32[]{:S(2)}, u32[]{:S(2)}) collective-permute-start(bf16[640,384]{1,0:T(8,128)(2,1)S(1)} %collective-permute-done), channel_id=1, source_target_pairs={{4,0},{12,8},{8,12},{5,1},{13,9},{9,13},{6,2},{14,10},{10,14},{7,3... | collective-permute-start | bytes 1474568 | tf_op jit(solution)/shard_map/ppermute | solution.py:38
  22.3 0.5 %fusion.25 = f32[384]{0:T(512)S(1)} fusion(bf16[640,384]{1,0:T(8,128)(2,1)S(1)} %collective-permute-done), kind=kOutput, calls=%fused_computation.41 | convolution fusion | flops 189185664 | bytes 493056 | tf_op jit(solution)/shard_map/dot_general | solution.py:15
  22.8 0.5 %fusion.24 = f32[384]{0:T(512)S(1)} fusion(bf16[640,384]{1,0:T(8,128)(2,1)S(1)} %collective-permute-done, bf16[640,384]{1,0:T(8,128)(2,1)S(1)} %copy-done), kind=kOutput, calls=%fused_computation.40 | convolution fusion | flops 189185664 | bytes 984576 | tf_op jit(solution)/shard_map/dot_general | solution.py:15
  23.3 0.5 %fusion.17 = f32[384]{0:T(512)S(1)} fusion(bf16[640,384]{1,0:T(8,128)(2,1)S(1)} %copy-done, bf16[640,384]{1,0:T(8,128)(2,1)S(1)} %collective-permute-done), kind=kOutput, calls=%fused_computation.33 | convolution fusion | flops 189185664 | bytes 984576 | tf_op jit(solution)/shard_map/dot_general | solution.py:15
  23.9 0.7 %collective-permute-start.2 = (bf16[640,384]{1,0:T(8,128)(2,1)S(1)}, bf16[640,384]{1,0:T(8,128)(2,1)S(1)}, u32[]{:S(2)}, u32[]{:S(2)}) collective-permute-start(bf16[640,384]{1,0:T(8,128)(2,1)S(1)} %collective-permute-done), channel_id=1, source_target_pairs={{1,2},{2,1},{5,6},{6,5},{9,10},{10,9},{13,14},{14,13},{17,18},{18,... | collective-permute-start | bytes 1474568 | tf_op jit(solution)/shard_map/ppermute | solution.py:33
  24.6 0.5 %fusion.20 = f32[384]{0:T(512)S(1)} fusion(bf16[640,384]{1,0:T(8,128)(2,1)S(1)} %collective-permute-done.3, bf16[640,384]{1,0:T(8,128)(2,1)S(1)} %collective-permute-done.4), kind=kOutput, calls=%fused_computation.36 | convolution fusion | flops 189185664 | bytes 984576 | tf_op jit(solution)/shard_map/dot_general | solution.py:15
  25.1 0.5 %fusion.22 = f32[384]{0:T(512)S(1)} fusion(bf16[640,384]{1,0:T(8,128)(2,1)S(1)} %collective-permute-done.3, bf16[640,384]{1,0:T(8,128)(2,1)S(1)} %collective-permute-done.6), kind=kOutput, calls=%fused_computation.38 | convolution fusion | flops 189185664 | bytes 984576 | tf_op jit(solution)/shard_map/dot_general | solution.py:15
  25.6 1.0 %collective-permute-done.10 = bf16[640,384]{1,0:T(8,128)(2,1)S(1)} collective-permute-done((bf16[640,384]{1,0:T(8,128)(2,1)S(1)}, bf16[640,384]{1,0:T(8,128)(2,1)S(1)}, u32[]{:S(2)}, u32[]{:S(2)}) %collective-permute-start.10) | collective-permute-done | bytes 491552 | tf_op jit(solution)/shard_map/ppermute | solution.py:37
  26.6 0.5 %fusion.30 = f32[384]{0:T(512)S(1)} fusion(bf16[640,384]{1,0:T(8,128)(2,1)S(1)} %collective-permute-done.10, bf16[640,384]{1,0:T(8,128)(2,1)S(1)} %collective-permute-done.6), kind=kOutput, calls=%fused_computation.46 | convolution fusion | flops 189185664 | bytes 984576 | tf_op jit(solution)/shard_map/dot_general | solution.py:15
  27.2 0.5 %fusion.29 = f32[384]{0:T(512)S(1)} fusion(bf16[640,384]{1,0:T(8,128)(2,1)S(1)} %collective-permute-done.10, bf16[640,384]{1,0:T(8,128)(2,1)S(1)} %collective-permute-done.5), kind=kOutput, calls=%fused_computation.45 | convolution fusion | flops 189185664 | bytes 984576 | tf_op jit(solution)/shard_map/dot_general | solution.py:15
  27.7 0.5 %fusion.21 = f32[384]{0:T(512)S(1)} fusion(bf16[640,384]{1,0:T(8,128)(2,1)S(1)} %collective-permute-done.3, bf16[640,384]{1,0:T(8,128)(2,1)S(1)} %collective-permute-done.5), kind=kOutput, calls=%fused_computation.37 | convolution fusion | flops 189185664 | bytes 984576 | tf_op jit(solution)/shard_map/dot_general | solution.py:15
  28.2 1.3 %collective-permute-start.7 = (bf16[640,384]{1,0:T(8,128)(2,1)S(1)}, bf16[640,384]{1,0:T(8,128)(2,1)S(1)}, u32[]{:S(2)}, u32[]{:S(2)}) collective-permute-start(bf16[640,384]{1,0:T(8,128)(2,1)S(1)} %collective-permute-done.2), channel_id=1, source_target_pairs={{4,0},{12,8},{8,12},{5,1},{13,9},{9,13},{6,2},{14,10},{10,14},{7,3... | collective-permute-start | bytes 1474568 | tf_op jit(solution)/shard_map/ppermute | solution.py:38
  29.6 0.5 %fusion.27 = f32[384]{0:T(512)S(1)} fusion(bf16[640,384]{1,0:T(8,128)(2,1)S(1)} %collective-permute-done, bf16[640,384]{1,0:T(8,128)(2,1)S(1)} %collective-permute-done.2), kind=kOutput, calls=%fused_computation.43 | convolution fusion | flops 189185664 | bytes 984576 | tf_op jit(solution)/shard_map/dot_general | solution.py:15
  30.6 0.5 %fusion.28 = f32[384]{0:T(512)S(1)} fusion(bf16[640,384]{1,0:T(8,128)(2,1)S(1)} %collective-permute-done.10, bf16[640,384]{1,0:T(8,128)(2,1)S(1)} %collective-permute-done.4), kind=kOutput, calls=%fused_computation.44 | convolution fusion | flops 189185664 | bytes 984576 | tf_op jit(solution)/shard_map/dot_general | solution.py:15
  31.2 0.5 %fusion.31 = f32[384]{0:T(512)S(1)} fusion(bf16[640,384]{1,0:T(8,128)(2,1)S(1)} %collective-permute-done.10, bf16[640,384]{1,0:T(8,128)(2,1)S(1)} %collective-permute-done.7), kind=kOutput, calls=%fused_computation.47 | convolution fusion | flops 189185664 | bytes 984576 | tf_op jit(solution)/shard_map/dot_general | solution.py:15
  31.7 1.3 %collective-permute-start.11 = (f32[384]{0:T(512)S(1)}, f32[384]{0:T(512)S(1)}, u32[]{:S(2)}, u32[]{:S(2)}) collective-permute-start(f32[384]{0:T(512)S(1)} %add_add_fusion), channel_id=1, source_target_pairs={{0,0},{8,8},{12,4},{1,1},{9,9},{13,5},{2,2},{10,10},{14,6},{3,3},{... | collective-permute-start | bytes 4616 | tf_op jit(solution)/shard_map/ppermute | solution.py:44
  33.5 1.3 %collective-permute-start.8 = (f32[384]{0:T(512)S(1)}, f32[384]{0:T(512)S(1)}, u32[]{:S(2)}, u32[]{:S(2)}) collective-permute-start(f32[384]{0:T(512)S(1)} %add_add_fusion.2), channel_id=1, source_target_pairs={{0,0},{8,8},{12,4},{1,1},{9,9},{13,5},{2,2},{10,10},{14,6},{3,3},{... | collective-permute-start | bytes 4616 | tf_op jit(solution)/shard_map/ppermute | solution.py:44
  34.8 1.9 %collective-permute-done.11 = f32[384]{0:T(512)S(1)} collective-permute-done((f32[384]{0:T(512)S(1)}, f32[384]{0:T(512)S(1)}, u32[]{:S(2)}, u32[]{:S(2)}) %collective-permute-start.11) | collective-permute-done | bytes 1568 | tf_op jit(solution)/shard_map/ppermute | solution.py:44
  36.7 1.3 %collective-permute-start.12 = (f32[384]{0:T(512)S(1)}, f32[384]{0:T(512)S(1)}, u32[]{:S(2)}, u32[]{:S(2)}) collective-permute-start(f32[384]{0:T(512)S(1)} %add_add_fusion.1), channel_id=1, source_target_pairs={{1,0},{2,3},{5,4},{6,7},{9,8},{10,11},{13,12},{14,15},{17,16},{18,... | collective-permute-start | bytes 4616 | tf_op jit(solution)/shard_map/ppermute | solution.py:48
  38.0 0.5 %collective-permute-done.8 = f32[384]{0:T(512)S(1)} collective-permute-done((f32[384]{0:T(512)S(1)}, f32[384]{0:T(512)S(1)}, u32[]{:S(2)}, u32[]{:S(2)}) %collective-permute-start.8) | collective-permute-done | bytes 1568 | tf_op jit(solution)/shard_map/ppermute | solution.py:44
  38.5 0.6 %collective-permute-start.9 = (f32[384]{0:T(512)S(1)}, f32[384]{0:T(512)S(1)}, u32[]{:S(2)}, u32[]{:S(2)}) collective-permute-start(f32[384]{0:T(512)S(1)} %add_add_fusion.3), channel_id=1, source_target_pairs={{1,1},{2,2},{5,5},{6,6},{9,9},{10,10},{13,13},{14,14},{17,17},{18,... | collective-permute-start | bytes 4616 | tf_op jit(solution)/shard_map/ppermute | solution.py:47
  39.2 12.0 %collective-permute-done.12 = f32[384]{0:T(512)S(1)} collective-permute-done((f32[384]{0:T(512)S(1)}, f32[384]{0:T(512)S(1)}, u32[]{:S(2)}, u32[]{:S(2)}) %collective-permute-start.12) | collective-permute-done | bytes 1568 | tf_op jit(solution)/shard_map/ppermute | solution.py:48
  51.2 0.6 %add.59 = f32[384]{0:T(512)} add(f32[384]{0:T(512)S(1)} %collective-permute-done.9, f32[384]{0:T(512)S(1)} %collective-permute-done.12) | non-fusion elementwise | flops 384 | bytes 4608 | tf_op jit(solution)/shard_map/add | solution.py:49
  (17 shorter events, 1.6 us)
Async XLA Ops:
  0.0 15.3 %copy-start = (bf16[640,384]{1,0:T(8,128)(2,1)S(1)}, bf16[640,384]{1,0:T(8,128)(2,1)}, u32[]{:S(2)}) copy-start(bf16[640,384]{1,0:T(8,128)(2,1)} %param.1) | copy-start | bytes 1474564
  0.0 14.0 %collective-permute-start.1 = (bf16[640,384]{1,0:T(8,128)(2,1)}, bf16[640,384]{1,0:T(8,128)(2,1)S(1)}, u32[]{:S(2)}, u32[]{:S(2)}) collective-permute-start(bf16[640,384]{1,0:T(8,128)(2,1)} %param.1), channel_id=1, source_target_pairs={{1,2},{2,1},{5,6},{6,5},{9,10},{10,9},{13,14},{14,13},{17,18},{18,... | collective-permute-start | bytes 1474568 | tf_op jit(solution)/shard_map/ppermute | solution.py:32
  0.8 16.4 %collective-permute-start = (bf16[640,384]{1,0:T(8,128)(2,1)}, bf16[640,384]{1,0:T(8,128)(2,1)S(1)}, u32[]{:S(2)}, u32[]{:S(2)}) collective-permute-start(bf16[640,384]{1,0:T(8,128)(2,1)} %param.1), channel_id=1, source_target_pairs={{0,1},{3,2},{4,5},{7,6},{8,9},{11,10},{12,13},{15,14},{16,17},{19,... | collective-permute-start | bytes 1474568 | tf_op jit(solution)/shard_map/ppermute | solution.py:31
  7.4 16.5 %collective-permute-start.3 = (bf16[640,384]{1,0:T(8,128)(2,1)}, bf16[640,384]{1,0:T(8,128)(2,1)S(1)}, u32[]{:S(2)}, u32[]{:S(2)}) collective-permute-start(bf16[640,384]{1,0:T(8,128)(2,1)} %param.1), channel_id=1, source_target_pairs={{0,0},{8,8},{4,12},{1,1},{9,9},{5,13},{2,2},{10,10},{6,14},{3,3},{... | collective-permute-start | bytes 1474568 | tf_op jit(solution)/shard_map/ppermute | solution.py:37
  10.6 14.0 %collective-permute-start.4 = (bf16[640,384]{1,0:T(8,128)(2,1)}, bf16[640,384]{1,0:T(8,128)(2,1)S(1)}, u32[]{:S(2)}, u32[]{:S(2)}) collective-permute-start(bf16[640,384]{1,0:T(8,128)(2,1)} %param.1), channel_id=1, source_target_pairs={{4,0},{12,8},{8,12},{5,1},{13,9},{9,13},{6,2},{14,10},{10,14},{7,3... | collective-permute-start | bytes 1474568 | tf_op jit(solution)/shard_map/ppermute | solution.py:38
  14.0 11.1 %collective-permute-start.6 = (bf16[640,384]{1,0:T(8,128)(2,1)S(1)}, bf16[640,384]{1,0:T(8,128)(2,1)S(1)}, u32[]{:S(2)}, u32[]{:S(2)}) collective-permute-start(bf16[640,384]{1,0:T(8,128)(2,1)S(1)} %collective-permute-done.1), channel_id=1, source_target_pairs={{4,0},{12,8},{8,12},{5,1},{13,9},{9,13},{6,2},{14,10},{10,14},{7,3... | collective-permute-start | bytes 1474568 | tf_op jit(solution)/shard_map/ppermute | solution.py:38
  17.8 8.9 %collective-permute-start.10 = (bf16[640,384]{1,0:T(8,128)(2,1)S(1)}, bf16[640,384]{1,0:T(8,128)(2,1)S(1)}, u32[]{:S(2)}, u32[]{:S(2)}) collective-permute-start(bf16[640,384]{1,0:T(8,128)(2,1)S(1)} %collective-permute-done), channel_id=1, source_target_pairs={{0,0},{8,8},{4,12},{1,1},{9,9},{5,13},{2,2},{10,10},{6,14},{3,3},{... | collective-permute-start | bytes 1474568 | tf_op jit(solution)/shard_map/ppermute | solution.py:37
  20.9 6.3 %collective-permute-start.5 = (bf16[640,384]{1,0:T(8,128)(2,1)S(1)}, bf16[640,384]{1,0:T(8,128)(2,1)S(1)}, u32[]{:S(2)}, u32[]{:S(2)}) collective-permute-start(bf16[640,384]{1,0:T(8,128)(2,1)S(1)} %collective-permute-done), channel_id=1, source_target_pairs={{4,0},{12,8},{8,12},{5,1},{13,9},{9,13},{6,2},{14,10},{10,14},{7,3... | collective-permute-start | bytes 1474568 | tf_op jit(solution)/shard_map/ppermute | solution.py:38
  23.9 4.4 %collective-permute-start.2 = (bf16[640,384]{1,0:T(8,128)(2,1)S(1)}, bf16[640,384]{1,0:T(8,128)(2,1)S(1)}, u32[]{:S(2)}, u32[]{:S(2)}) collective-permute-start(bf16[640,384]{1,0:T(8,128)(2,1)S(1)} %collective-permute-done), channel_id=1, source_target_pairs={{1,2},{2,1},{5,6},{6,5},{9,10},{10,9},{13,14},{14,13},{17,18},{18,... | collective-permute-start | bytes 1474568 | tf_op jit(solution)/shard_map/ppermute | solution.py:33
  28.2 2.9 %collective-permute-start.7 = (bf16[640,384]{1,0:T(8,128)(2,1)S(1)}, bf16[640,384]{1,0:T(8,128)(2,1)S(1)}, u32[]{:S(2)}, u32[]{:S(2)}) collective-permute-start(bf16[640,384]{1,0:T(8,128)(2,1)S(1)} %collective-permute-done.2), channel_id=1, source_target_pairs={{4,0},{12,8},{8,12},{5,1},{13,9},{9,13},{6,2},{14,10},{10,14},{7,3... | collective-permute-start | bytes 1474568 | tf_op jit(solution)/shard_map/ppermute | solution.py:38
  31.7 5.0 %collective-permute-start.11 = (f32[384]{0:T(512)S(1)}, f32[384]{0:T(512)S(1)}, u32[]{:S(2)}, u32[]{:S(2)}) collective-permute-start(f32[384]{0:T(512)S(1)} %add_add_fusion), channel_id=1, source_target_pairs={{0,0},{8,8},{12,4},{1,1},{9,9},{13,5},{2,2},{10,10},{14,6},{3,3},{... | collective-permute-start | bytes 4616 | tf_op jit(solution)/shard_map/ppermute | solution.py:44
  33.5 5.0 %collective-permute-start.8 = (f32[384]{0:T(512)S(1)}, f32[384]{0:T(512)S(1)}, u32[]{:S(2)}, u32[]{:S(2)}) collective-permute-start(f32[384]{0:T(512)S(1)} %add_add_fusion.2), channel_id=1, source_target_pairs={{0,0},{8,8},{12,4},{1,1},{9,9},{13,5},{2,2},{10,10},{14,6},{3,3},{... | collective-permute-start | bytes 4616 | tf_op jit(solution)/shard_map/ppermute | solution.py:44
  36.7 14.5 %collective-permute-start.12 = (f32[384]{0:T(512)S(1)}, f32[384]{0:T(512)S(1)}, u32[]{:S(2)}, u32[]{:S(2)}) collective-permute-start(f32[384]{0:T(512)S(1)} %add_add_fusion.1), channel_id=1, source_target_pairs={{1,0},{2,3},{5,4},{6,7},{9,8},{10,11},{13,12},{14,15},{17,16},{18,... | collective-permute-start | bytes 4616 | tf_op jit(solution)/shard_map/ppermute | solution.py:48
  38.5 12.7 %collective-permute-start.9 = (f32[384]{0:T(512)S(1)}, f32[384]{0:T(512)S(1)}, u32[]{:S(2)}, u32[]{:S(2)}) collective-permute-start(f32[384]{0:T(512)S(1)} %add_add_fusion.3), channel_id=1, source_target_pairs={{1,1},{2,2},{5,5},{6,6},{9,9},{10,10},{13,13},{14,14},{17,17},{18,... | collective-permute-start | bytes 4616 | tf_op jit(solution)/shard_map/ppermute | solution.py:47

commit v2 on v1

--- a/solution.py
+++ b/solution.py
@@ -32,21 +32,18 @@
     nbr = lax.ppermute(own, "group", [(1, 2), (2, 1)])
     far = lax.ppermute(adopt, "group", [(1, 2), (2, 1)])
     panel = [own, adopt, nbr, far]
-    rows = [own, adopt]
 
-    rows_next = [lax.ppermute(r, "genome", [(0, 0), (2, 2), (1, 3)]) for r in rows]
-    panel_next = [lax.ppermute(c, "genome", [(1, 0), (3, 2), (2, 3)]) for c in panel]
-
-    scores = []
-    for r, rn in zip(rows, rows_next):
-        within = sum(row_squares(r, c, scaling) for c in panel)
-        following = sum(row_squares(rn, c, scaling) for c in panel_next)
-        following = lax.ppermute(following, "genome", [(0, 0), (2, 2), (3, 1)])
-        scores.append(within + following)
-
-    at_hub = lax.ppermute(scores[0], "group", [(1, 1), (2, 2)])
-    at_end = lax.ppermute(scores[1], "group", [(1, 0), (2, 3)])
-    return at_hub + at_end
+    onward = [(g, g + 1) for g in range(lax.axis_size("genome") - 1)]
+    backward = [(b, a) for a, b in onward]
+    rows = [own, adopt] + [lax.ppermute(r, "genome", onward) for r in (own, adopt)]
+    sums = [sum(row_squares(r, c, scaling) for c in panel) for r in rows]
+    following = lax.ppermute(jnp.concatenate(sums[2:]), "genome", backward)
+    width = own.shape[1]
+    at_hub = sums[0] + following[:width]
+    adopted = sums[1] + following[width:]
+    at_end = lax.ppermute(adopted, "group", [(1, 0), (2, 3)])
+    place = lax.axis_index("group")
+    return jnp.where((place == 1) | (place == 2), at_hub, at_end)
 
 
 def solution(mesh):

time: 52.2 us -> 43.6 us (0.84)
  starting transfers between devices: 24.6 us -> 17.1 us
  waiting for transfers between devices: 16.8 us -> 15.7 us
    ppermute x10 -> x4, starting transfers between devices: 16.5 us -> 11.7 us  [the longest x2 8.5 us: hub_plan(): lax.ppermute(r, 'genome', onward)]
    ppermute x10 -> x4, waiting for transfers between devices: 15.4 us -> 12 us  [the longest x1 8.03 us: hub_plan(): at_end = lax.ppermute(adopted, 'group', [(1, 0), (2, 3)])]
    ppermute x1, starting transfers between devices: 6.57 us -> 4.05 us  [hub_plan(): adopt = lax.ppermute(own, 'group', [(0, 1), (3, 2)])]
    ppermute x1, waiting for transfers between devices: 1.38 us -> 3.71 us  [hub_plan(): adopt = lax.ppermute(own, 'group', [(0, 1), (3, 2)])]
    add x5 -> x3, other arithmetic: 0.61 us -> 0.02 us  [the longest x2 0.01 us: hub_plan(): sums = [sum((row_squares(r, c, scaling) for c in panel)) for r in rows]]
    select_n x0 -> x1, other arithmetic: none -> 0.58 us  [hub_plan(): return jnp.where((place == 1) | (place == 2), at_hub, at_end)]
  transfers between devices with their start and end apart: 13 -> 7, of which waited for: 5 -> 4; matrix products, arithmetic and copies ran while one was open for 18% -> 20% of each run, Pallas kernels for 0% -> 0%
where the time goes in v2:
time: 43.6 us; the launch traced here: 43.3 us
  starting transfers between devices  17.1 us (39%)
  waiting for transfers between devices  15.7 us (36%)
  matrix products  9.68 us (22%)
  other arithmetic  0.61 us (1%)
    dot_general x16, matrix products, row_squares(): lax.dot_general(rows, columns, (((0,), (0,)), ((), ())), preferred_elemen...  9.68 us
    ppermute x2, starting transfers between devices, hub_plan(): lax.ppermute(r, 'genome', onward)  8.5 us
    ppermute x1, waiting for transfers between devices, hub_plan(): at_end = lax.ppermute(adopted, 'group', [(1, 0), (2, 3)])  8.03 us
    ppermute x1, starting transfers between devices, hub_plan(): adopt = lax.ppermute(own, 'group', [(0, 1), (3, 2)])  4.05 us
    ppermute x1, waiting for transfers between devices, hub_plan(): adopt = lax.ppermute(own, 'group', [(0, 1), (3, 2)])  3.71 us
    ppermute x1, waiting for transfers between devices, hub_plan(): following = lax.ppermute(jnp.concatenate(sums[2:]), 'genome', backward)  3.21 us
    ppermute x1, starting transfers between devices, hub_plan(): following = lax.ppermute(jnp.concatenate(sums[2:]), 'genome', backward)  1.92 us
    ppermute x1, starting transfers between devices, hub_plan(): at_end = lax.ppermute(adopted, 'group', [(1, 0), (2, 3)])  1.28 us
  transfers between devices with their start and end apart: 7, of which 4 were waited for; matrix products, arithmetic and copies ran while one was open for 20% of the time, Pallas kernels for 0%

profile of v2, /device:TPU:1, one launch (start us, length us, event | category | flops | bytes accessed | tf_op | source)
XLA Modules:
  0.0 43.3 jit_solution(6739280314579530441)
XLA Ops:
  0.0 4.0 %collective-permute-start = (bf16[640,384]{1,0:T(8,128)(2,1)}, bf16[640,384]{1,0:T(8,128)(2,1)S(1)}, u32[]{:S(2)}, u32[]{:S(2)}) collective-permute-start(bf16[640,384]{1,0:T(8,128)(2,1)} %param.1), channel_id=1, source_target_pairs={{0,1},{3,2},{4,5},{7,6},{8,9},{11,10},{12,13},{15,14},{16,17},{19,... | collective-permute-start | bytes 1474568 | tf_op jit(solution)/shard_map/ppermute | solution.py:31
  4.1 4.0 %collective-permute-start.3 = (bf16[640,384]{1,0:T(8,128)(2,1)}, bf16[640,384]{1,0:T(8,128)(2,1)S(1)}, u32[]{:S(2)}, u32[]{:S(2)}) collective-permute-start(bf16[640,384]{1,0:T(8,128)(2,1)} %param.1), channel_id=1, source_target_pairs={{0,4},{4,8},{8,12},{1,5},{5,9},{9,13},{2,6},{6,10},{10,14},{3,7},{... | collective-permute-start | bytes 1474568 | tf_op jit(solution)/shard_map/ppermute | solution.py:38
  8.0 0.7 %collective-permute-start.1 = (bf16[640,384]{1,0:T(8,128)(2,1)}, bf16[640,384]{1,0:T(8,128)(2,1)S(1)}, u32[]{:S(2)}, u32[]{:S(2)}) collective-permute-start(bf16[640,384]{1,0:T(8,128)(2,1)} %param.1), channel_id=1, source_target_pairs={{1,2},{2,1},{5,6},{6,5},{9,10},{10,9},{13,14},{14,13},{17,18},{18,... | collective-permute-start | bytes 1474568 | tf_op jit(solution)/shard_map/ppermute | solution.py:32
  8.7 0.0 copy-start
  8.7 1.8 %fusion.16 = f32[384]{0:T(512)S(1)} fusion(bf16[640,384]{1,0:T(8,128)(2,1)} %param.1), kind=kOutput, calls=%fused_computation.32 | convolution fusion | flops 189185664 | bytes 493056 | tf_op jit(solution)/shard_map/dot_general | solution.py:15
  10.5 3.7 %collective-permute-done = bf16[640,384]{1,0:T(8,128)(2,1)S(1)} collective-permute-done((bf16[640,384]{1,0:T(8,128)(2,1)}, bf16[640,384]{1,0:T(8,128)(2,1)S(1)}, u32[]{:S(2)}, u32[]{:S(2)}) %collective-permute-start) | collective-permute-done | bytes 491552 | tf_op jit(solution)/shard_map/ppermute | solution.py:31
  14.2 4.5 %collective-permute-start.4 = (bf16[640,384]{1,0:T(8,128)(2,1)S(1)}, bf16[640,384]{1,0:T(8,128)(2,1)S(1)}, u32[]{:S(2)}, u32[]{:S(2)}) collective-permute-start(bf16[640,384]{1,0:T(8,128)(2,1)S(1)} %collective-permute-done), channel_id=1, source_target_pairs={{0,4},{4,8},{8,12},{1,5},{5,9},{9,13},{2,6},{6,10},{10,14},{3,7},{... | collective-permute-start | bytes 1474568 | tf_op jit(solution)/shard_map/ppermute | solution.py:38
  18.8 0.7 %collective-permute-start.2 = (bf16[640,384]{1,0:T(8,128)(2,1)S(1)}, bf16[640,384]{1,0:T(8,128)(2,1)S(1)}, u32[]{:S(2)}, u32[]{:S(2)}) collective-permute-start(bf16[640,384]{1,0:T(8,128)(2,1)S(1)} %collective-permute-done), channel_id=1, source_target_pairs={{1,2},{2,1},{5,6},{6,5},{9,10},{10,9},{13,14},{14,13},{17,18},{18,... | collective-permute-start | bytes 1474568 | tf_op jit(solution)/shard_map/ppermute | solution.py:33
  19.5 0.0 collective-permute-done.3
  19.5 0.5 %fusion.20 = f32[384]{0:T(512)S(1)} fusion(bf16[640,384]{1,0:T(8,128)(2,1)S(1)} %collective-permute-done.3, bf16[640,384]{1,0:T(8,128)(2,1)S(1)} %copy-done), kind=kOutput, calls=%fused_computation.36 | convolution fusion | flops 189185664 | bytes 984576 | tf_op jit(solution)/shard_map/dot_general | solution.py:15
  20.0 0.5 %fusion.21 = f32[384]{0:T(512)S(1)} fusion(bf16[640,384]{1,0:T(8,128)(2,1)S(1)} %collective-permute-done.3, bf16[640,384]{1,0:T(8,128)(2,1)S(1)} %collective-permute-done), kind=kOutput, calls=%fused_computation.37 | convolution fusion | flops 189185664 | bytes 984576 | tf_op jit(solution)/shard_map/dot_general | solution.py:15
  20.5 0.0 collective-permute-done.1
  20.6 0.5 %fusion.22 = f32[384]{0:T(512)S(1)} fusion(bf16[640,384]{1,0:T(8,128)(2,1)S(1)} %collective-permute-done.3, bf16[640,384]{1,0:T(8,128)(2,1)S(1)} %collective-permute-done.1), kind=kOutput, calls=%fused_computation.38 | convolution fusion | flops 189185664 | bytes 984576 | tf_op jit(solution)/shard_map/dot_general | solution.py:15
  21.1 0.5 %fusion.30 = f32[384]{0:T(512)S(1)} fusion(bf16[640,384]{1,0:T(8,128)(2,1)S(1)} %collective-permute-done, bf16[640,384]{1,0:T(8,128)(2,1)S(1)} %collective-permute-done.1), kind=kOutput, calls=%fused_computation.46 | convolution fusion | flops 189185664 | bytes 984576 | tf_op jit(solution)/shard_map/dot_general | solution.py:15
  21.6 0.5 %fusion.28 = f32[384]{0:T(512)S(1)} fusion(bf16[640,384]{1,0:T(8,128)(2,1)S(1)} %collective-permute-done, bf16[640,384]{1,0:T(8,128)(2,1)S(1)} %copy-done), kind=kOutput, calls=%fused_computation.44 | convolution fusion | flops 189185664 | bytes 984576 | tf_op jit(solution)/shard_map/dot_general | solution.py:15
  22.1 0.5 %fusion.29 = f32[384]{0:T(512)S(1)} fusion(bf16[640,384]{1,0:T(8,128)(2,1)S(1)} %collective-permute-done), kind=kOutput, calls=%fused_computation.45 | convolution fusion | flops 189185664 | bytes 493056 | tf_op jit(solution)/shard_map/dot_general | solution.py:15
  22.7 0.5 %fusion.18 = f32[384]{0:T(512)S(1)} fusion(bf16[640,384]{1,0:T(8,128)(2,1)S(1)} %copy-done, bf16[640,384]{1,0:T(8,128)(2,1)S(1)} %collective-permute-done.1), kind=kOutput, calls=%fused_computation.34 | convolution fusion | flops 189185664 | bytes 984576 | tf_op jit(solution)/shard_map/dot_general | solution.py:15
  23.2 0.5 %fusion.17 = f32[384]{0:T(512)S(1)} fusion(bf16[640,384]{1,0:T(8,128)(2,1)S(1)} %copy-done, bf16[640,384]{1,0:T(8,128)(2,1)S(1)} %collective-permute-done), kind=kOutput, calls=%fused_computation.33 | convolution fusion | flops 189185664 | bytes 984576 | tf_op jit(solution)/shard_map/dot_general | solution.py:15
  23.7 0.8 %collective-permute-done.4 = bf16[640,384]{1,0:T(8,128)(2,1)S(1)} collective-permute-done((bf16[640,384]{1,0:T(8,128)(2,1)S(1)}, bf16[640,384]{1,0:T(8,128)(2,1)S(1)}, u32[]{:S(2)}, u32[]{:S(2)}) %collective-permute-start.4) | collective-permute-done | bytes 491552 | tf_op jit(solution)/shard_map/ppermute | solution.py:38
  24.5 0.5 %fusion.26 = f32[384]{0:T(512)S(1)} fusion(bf16[640,384]{1,0:T(8,128)(2,1)S(1)} %collective-permute-done.4, bf16[640,384]{1,0:T(8,128)(2,1)S(1)} %collective-permute-done.1), kind=kOutput, calls=%fused_computation.42 | convolution fusion | flops 189185664 | bytes 984576 | tf_op jit(solution)/shard_map/dot_general | solution.py:15
  25.0 0.5 %fusion.24 = f32[384]{0:T(512)S(1)} fusion(bf16[640,384]{1,0:T(8,128)(2,1)S(1)} %collective-permute-done.4, bf16[640,384]{1,0:T(8,128)(2,1)S(1)} %copy-done), kind=kOutput, calls=%fused_computation.40 | convolution fusion | flops 189185664 | bytes 984576 | tf_op jit(solution)/shard_map/dot_general | solution.py:15
  25.6 0.5 %fusion.25 = f32[384]{0:T(512)S(1)} fusion(bf16[640,384]{1,0:T(8,128)(2,1)S(1)} %collective-permute-done.4, bf16[640,384]{1,0:T(8,128)(2,1)S(1)} %collective-permute-done), kind=kOutput, calls=%fused_computation.41 | convolution fusion | flops 189185664 | bytes 984576 | tf_op jit(solution)/shard_map/dot_general | solution.py:15
  26.1 0.0 collective-permute-done.2
  26.1 0.5 %fusion.27 = f32[384]{0:T(512)S(1)} fusion(bf16[640,384]{1,0:T(8,128)(2,1)S(1)} %collective-permute-done.4, bf16[640,384]{1,0:T(8,128)(2,1)S(1)} %collective-permute-done.2), kind=kOutput, calls=%fused_computation.43 | convolution fusion | flops 189185664 | bytes 984576 | tf_op jit(solution)/shard_map/dot_general | solution.py:15
  26.7 0.5 %fusion.23 = f32[384]{0:T(512)S(1)} fusion(bf16[640,384]{1,0:T(8,128)(2,1)S(1)} %collective-permute-done.3, bf16[640,384]{1,0:T(8,128)(2,1)S(1)} %collective-permute-done.2), kind=kOutput, calls=%fused_computation.39 | convolution fusion | flops 189185664 | bytes 984576 | tf_op jit(solution)/shard_map/dot_general | solution.py:15
  27.2 1.9 %collective-permute-start.5 = (f32[768]{0:T(1024)S(1)}, f32[768]{0:T(1024)S(1)}, u32[]{:S(2)}, u32[]{:S(2)}) collective-permute-start(f32[768]{0:T(1024)S(1)} %pad_maximum_fusion), channel_id=1, source_target_pairs={{4,0},{8,4},{12,8},{5,1},{9,5},{13,9},{6,2},{10,6},{14,10},{7,3},{... | collective-permute-start | bytes 9224 | tf_op jit(solution)/shard_map/ppermute | solution.py:40
  29.2 0.5 %fusion.31 = f32[384]{0:T(512)S(1)} fusion(bf16[640,384]{1,0:T(8,128)(2,1)S(1)} %collective-permute-done, bf16[640,384]{1,0:T(8,128)(2,1)S(1)} %collective-permute-done.2), kind=kOutput, calls=%fused_computation.47 | convolution fusion | flops 189185664 | bytes 984576 | tf_op jit(solution)/shard_map/dot_general | solution.py:15
  29.7 3.2 %collective-permute-done.5 = f32[768]{0:T(1024)S(1)} collective-permute-done((f32[768]{0:T(1024)S(1)}, f32[768]{0:T(1024)S(1)}, u32[]{:S(2)}, u32[]{:S(2)}) %collective-permute-start.5) | collective-permute-done | bytes 3104 | tf_op jit(solution)/shard_map/ppermute | solution.py:40
  32.9 1.3 %collective-permute-start.6 = (f32[384]{0:T(512)S(1)}, f32[384]{0:T(512)S(1)}, u32[]{:S(2)}, u32[]{:S(2)}) collective-permute-start(f32[384]{0:T(512)S(1)} %slice_add_fusion), channel_id=1, source_target_pairs={{1,0},{2,3},{5,4},{6,7},{9,8},{10,11},{13,12},{14,15},{17,16},{18,... | collective-permute-start | bytes 4616 | tf_op jit(solution)/shard_map/ppermute | solution.py:44
  34.2 0.5 %fusion.19 = f32[384]{0:T(512)S(1)} fusion(bf16[640,384]{1,0:T(8,128)(2,1)S(1)} %copy-done, bf16[640,384]{1,0:T(8,128)(2,1)S(1)} %collective-permute-done.2), kind=kOutput, calls=%fused_computation.35 | convolution fusion | flops 189185664 | bytes 984576 | tf_op jit(solution)/shard_map/dot_general | solution.py:15
  34.7 8.0 %collective-permute-done.6 = f32[384]{0:T(512)S(1)} collective-permute-done((f32[384]{0:T(512)S(1)}, f32[384]{0:T(512)S(1)}, u32[]{:S(2)}, u32[]{:S(2)}) %collective-permute-start.6) | collective-permute-done | bytes 1568 | tf_op jit(solution)/shard_map/ppermute | solution.py:44
  42.8 0.6 %add_select_fusion = f32[384]{0:T(512)} fusion(f32[384]{0:T(512)S(1)} %collective-permute-done.6, f32[768]{0:T(1024)S(1)} %collective-permute-done.5, f32[384]{0:T(512)S(1)} %fusion.19, f32[384]{0:T(512)S(1)} %fusion.18, f32[384]{0:T(512)S(1)} %fusion.16, f32[384]{0:T(512)S(1)} %fusion.17, pred[]{:T(512)S(6)} %or.3), kind=kLoop, calls=%fused_computation.50 | loop fusion | flops 1920 | bytes 10753 | tf_op jit(solution)/shard_map/jit(_where)/select_n | solution.py:46
  (5 shorter events, 0.0 us)
Async XLA Ops:
  0.0 14.2 %collective-permute-start = (bf16[640,384]{1,0:T(8,128)(2,1)}, bf16[640,384]{1,0:T(8,128)(2,1)S(1)}, u32[]{:S(2)}, u32[]{:S(2)}) collective-permute-start(bf16[640,384]{1,0:T(8,128)(2,1)} %param.1), channel_id=1, source_target_pairs={{0,1},{3,2},{4,5},{7,6},{8,9},{11,10},{12,13},{15,14},{16,17},{19,... | collective-permute-start | bytes 1474568 | tf_op jit(solution)/shard_map/ppermute | solution.py:31
  4.1 15.4 %collective-permute-start.3 = (bf16[640,384]{1,0:T(8,128)(2,1)}, bf16[640,384]{1,0:T(8,128)(2,1)S(1)}, u32[]{:S(2)}, u32[]{:S(2)}) collective-permute-start(bf16[640,384]{1,0:T(8,128)(2,1)} %param.1), channel_id=1, source_target_pairs={{0,4},{4,8},{8,12},{1,5},{5,9},{9,13},{2,6},{6,10},{10,14},{3,7},{... | collective-permute-start | bytes 1474568 | tf_op jit(solution)/shard_map/ppermute | solution.py:38
  8.0 12.5 %collective-permute-start.1 = (bf16[640,384]{1,0:T(8,128)(2,1)}, bf16[640,384]{1,0:T(8,128)(2,1)S(1)}, u32[]{:S(2)}, u32[]{:S(2)}) collective-permute-start(bf16[640,384]{1,0:T(8,128)(2,1)} %param.1), channel_id=1, source_target_pairs={{1,2},{2,1},{5,6},{6,5},{9,10},{10,9},{13,14},{14,13},{17,18},{18,... | collective-permute-start | bytes 1474568 | tf_op jit(solution)/shard_map/ppermute | solution.py:32
  8.7 10.7 %copy-start = (bf16[640,384]{1,0:T(8,128)(2,1)S(1)}, bf16[640,384]{1,0:T(8,128)(2,1)}, u32[]{:S(2)}) copy-start(bf16[640,384]{1,0:T(8,128)(2,1)} %param.1) | copy-start | bytes 1474564
  14.2 10.3 %collective-permute-start.4 = (bf16[640,384]{1,0:T(8,128)(2,1)S(1)}, bf16[640,384]{1,0:T(8,128)(2,1)S(1)}, u32[]{:S(2)}, u32[]{:S(2)}) collective-permute-start(bf16[640,384]{1,0:T(8,128)(2,1)S(1)} %collective-permute-done), channel_id=1, source_target_pairs={{0,4},{4,8},{8,12},{1,5},{5,9},{9,13},{2,6},{6,10},{10,14},{3,7},{... | collective-permute-start | bytes 1474568 | tf_op jit(solution)/shard_map/ppermute | solution.py:38
  18.8 7.4 %collective-permute-start.2 = (bf16[640,384]{1,0:T(8,128)(2,1)S(1)}, bf16[640,384]{1,0:T(8,128)(2,1)S(1)}, u32[]{:S(2)}, u32[]{:S(2)}) collective-permute-start(bf16[640,384]{1,0:T(8,128)(2,1)S(1)} %collective-permute-done), channel_id=1, source_target_pairs={{1,2},{2,1},{5,6},{6,5},{9,10},{10,9},{13,14},{14,13},{17,18},{18,... | collective-permute-start | bytes 1474568 | tf_op jit(solution)/shard_map/ppermute | solution.py:33
  27.2 5.7 %collective-permute-start.5 = (f32[768]{0:T(1024)S(1)}, f32[768]{0:T(1024)S(1)}, u32[]{:S(2)}, u32[]{:S(2)}) collective-permute-start(f32[768]{0:T(1024)S(1)} %pad_maximum_fusion), channel_id=1, source_target_pairs={{4,0},{8,4},{12,8},{5,1},{9,5},{13,9},{6,2},{10,6},{14,10},{7,3},{... | collective-permute-start | bytes 9224 | tf_op jit(solution)/shard_map/ppermute | solution.py:40
  32.9 9.8 %collective-permute-start.6 = (f32[384]{0:T(512)S(1)}, f32[384]{0:T(512)S(1)}, u32[]{:S(2)}, u32[]{:S(2)}) collective-permute-start(f32[384]{0:T(512)S(1)} %slice_add_fusion), channel_id=1, source_target_pairs={{1,0},{2,3},{5,4},{6,7},{9,8},{10,11},{13,12},{14,15},{17,16},{18,... | collective-permute-start | bytes 4616 | tf_op jit(solution)/shard_map/ppermute | solution.py:44

commit v3 on v2

--- a/solution.py
+++ b/solution.py
@@ -35,7 +35,10 @@
 
     onward = [(g, g + 1) for g in range(lax.axis_size("genome") - 1)]
     backward = [(b, a) for a, b in onward]
-    rows = [own, adopt] + [lax.ppermute(r, "genome", onward) for r in (own, adopt)]
+    prev_own = lax.ppermute(own, "genome", onward)
+    relay, _ = lax.optimization_barrier((prev_own, adopt))
+    prev_adopt = lax.ppermute(relay, "group", [(0, 1), (3, 2)])
+    rows = [own, adopt, prev_own, prev_adopt]
     sums = [sum(row_squares(r, c, scaling) for c in panel) for r in rows]
     following = lax.ppermute(jnp.concatenate(sums[2:]), "genome", backward)
     width = own.shape[1]

time: 43.6 us -> 50.1 us (1.15)
  waiting for transfers between devices: 15.7 us -> 22.5 us
    ppermute x2, waiting for transfers between devices: 0.77 us -> 5.7 us  [the longest x1 5.35 us: hub_plan(): prev_adopt = lax.ppermute(relay, 'group', [(0, 1), (3, 2)])]
    ppermute x1, waiting for transfers between devices: 3.71 us -> 7.7 us  [hub_plan(): adopt = lax.ppermute(own, 'group', [(0, 1), (3, 2)])]
    ppermute x1, waiting for transfers between devices: 3.21 us -> 1.97 us  [hub_plan(): following = lax.ppermute(jnp.concatenate(sums[2:]), 'genome', backward)]
    ppermute x1, waiting for transfers between devices: 8.03 us -> 7.16 us  [hub_plan(): at_end = lax.ppermute(adopted, 'group', [(1, 0), (2, 3)])]
    ppermute x1, starting transfers between devices: 4.05 us -> 3.23 us  [hub_plan(): adopt = lax.ppermute(own, 'group', [(0, 1), (3, 2)])]
  transfers between devices with their start and end apart: 7 -> 7, of which waited for: 4 -> 5; matrix products, arithmetic and copies ran while one was open for 20% -> 15% of each run, Pallas kernels for 0% -> 0%
where the time goes in v3:
time: 50.1 us; the launch traced here: 49.8 us
  waiting for transfers between devices  22.5 us (45%)
  starting transfers between devices  16.8 us (34%)
  matrix products  9.69 us (19%)
  other arithmetic  0.61 us (1%)
    dot_general x16, matrix products, row_squares(): lax.dot_general(rows, columns, (((0,), (0,)), ((), ())), preferred_elemen...  9.69 us
    ppermute x1, waiting for transfers between devices, hub_plan(): adopt = lax.ppermute(own, 'group', [(0, 1), (3, 2)])  7.7 us
    ppermute x1, waiting for transfers between devices, hub_plan(): at_end = lax.ppermute(adopted, 'group', [(1, 0), (2, 3)])  7.16 us
    ppermute x1, waiting for transfers between devices, hub_plan(): prev_adopt = lax.ppermute(relay, 'group', [(0, 1), (3, 2)])  5.35 us
    ppermute x1, starting transfers between devices, hub_plan(): prev_own = lax.ppermute(own, 'genome', onward)  4.5 us
    ppermute x1, starting transfers between devices, hub_plan(): prev_adopt = lax.ppermute(relay, 'group', [(0, 1), (3, 2)])  4.02 us
    ppermute x1, starting transfers between devices, hub_plan(): adopt = lax.ppermute(own, 'group', [(0, 1), (3, 2)])  3.23 us
    ppermute x1, starting transfers between devices, hub_plan(): following = lax.ppermute(jnp.concatenate(sums[2:]), 'genome', backward)  2.41 us
  transfers between devices with their start and end apart: 7, of which 5 were waited for; matrix products, arithmetic and copies ran while one was open for 15% of the time, Pallas kernels for 0%

profile of v3, /device:TPU:1, one launch (start us, length us, event | category | flops | bytes accessed | tf_op | source)
XLA Modules:
  0.0 49.8 jit_solution(6118844742869984220)
XLA Ops:
  0.0 4.5 %collective-permute-start.3 = (bf16[640,384]{1,0:T(8,128)(2,1)}, bf16[640,384]{1,0:T(8,128)(2,1)S(1)}, u32[]{:S(2)}, u32[]{:S(2)}) collective-permute-start(bf16[640,384]{1,0:T(8,128)(2,1)} %param.1), channel_id=1, source_target_pairs={{0,4},{4,8},{8,12},{1,5},{5,9},{9,13},{2,6},{6,10},{10,14},{3,7},{... | collective-permute-start | bytes 1474568 | tf_op jit(solution)/shard_map/ppermute | solution.py:38
  4.5 3.2 %collective-permute-start = (bf16[640,384]{1,0:T(8,128)(2,1)}, bf16[640,384]{1,0:T(8,128)(2,1)S(1)}, u32[]{:S(2)}, u32[]{:S(2)}) collective-permute-start(bf16[640,384]{1,0:T(8,128)(2,1)} %param.1), channel_id=1, source_target_pairs={{0,1},{3,2},{4,5},{7,6},{8,9},{11,10},{12,13},{15,14},{16,17},{19,... | collective-permute-start | bytes 1474568 | tf_op jit(solution)/shard_map/ppermute | solution.py:31
  7.7 0.7 %collective-permute-start.1 = (bf16[640,384]{1,0:T(8,128)(2,1)}, bf16[640,384]{1,0:T(8,128)(2,1)S(1)}, u32[]{:S(2)}, u32[]{:S(2)}) collective-permute-start(bf16[640,384]{1,0:T(8,128)(2,1)} %param.1), channel_id=1, source_target_pairs={{1,2},{2,1},{5,6},{6,5},{9,10},{10,9},{13,14},{14,13},{17,18},{18,... | collective-permute-start | bytes 1474568 | tf_op jit(solution)/shard_map/ppermute | solution.py:32
  8.5 0.0 copy-start
  8.5 1.8 %fusion.16 = f32[384]{0:T(512)S(1)} fusion(bf16[640,384]{1,0:T(8,128)(2,1)} %param.1), kind=kOutput, calls=%fused_computation.32 | convolution fusion | flops 189185664 | bytes 493056 | tf_op jit(solution)/shard_map/dot_general | solution.py:15
  10.2 0.4 collective-permute-done.3
  10.6 7.7 %collective-permute-done = bf16[640,384]{1,0:T(8,128)(2,1)S(1)} collective-permute-done((bf16[640,384]{1,0:T(8,128)(2,1)}, bf16[640,384]{1,0:T(8,128)(2,1)S(1)}, u32[]{:S(2)}, u32[]{:S(2)}) %collective-permute-start) | collective-permute-done | bytes 491552 | tf_op jit(solution)/shard_map/ppermute | solution.py:31
  18.3 4.0 %collective-permute-start.4 = (bf16[640,384]{1,0:T(8,128)(2,1)S(1)}, bf16[640,384]{1,0:T(8,128)(2,1)S(1)}, u32[]{:S(2)}, u32[]{:S(2)}) collective-permute-start(bf16[640,384]{1,0:T(8,128)(2,1)S(1)} %collective-permute-done.3), channel_id=1, source_target_pairs={{0,1},{3,2},{4,5},{7,6},{8,9},{11,10},{12,13},{15,14},{16,17},{19,... | collective-permute-start | bytes 1474568 | tf_op jit(solution)/shard_map/ppermute | solution.py:40
  22.3 0.5 %fusion.20 = f32[384]{0:T(512)S(1)} fusion(bf16[640,384]{1,0:T(8,128)(2,1)S(1)} %collective-permute-done.3, bf16[640,384]{1,0:T(8,128)(2,1)S(1)} %copy-done), kind=kOutput, calls=%fused_computation.36 | convolution fusion | flops 189185664 | bytes 984576 | tf_op jit(solution)/shard_map/dot_general | solution.py:15
  22.9 0.0 collective-permute-done.1
  22.9 0.5 %fusion.22 = f32[384]{0:T(512)S(1)} fusion(bf16[640,384]{1,0:T(8,128)(2,1)S(1)} %collective-permute-done.3, bf16[640,384]{1,0:T(8,128)(2,1)S(1)} %collective-permute-done.1), kind=kOutput, calls=%fused_computation.38 | convolution fusion | flops 189185664 | bytes 984576 | tf_op jit(solution)/shard_map/dot_general | solution.py:15
  23.4 0.5 %fusion.18 = f32[384]{0:T(512)S(1)} fusion(bf16[640,384]{1,0:T(8,128)(2,1)S(1)} %copy-done, bf16[640,384]{1,0:T(8,128)(2,1)S(1)} %collective-permute-done.1), kind=kOutput, calls=%fused_computation.34 | convolution fusion | flops 189185664 | bytes 984576 | tf_op jit(solution)/shard_map/dot_general | solution.py:15
  23.9 0.5 %fusion.30 = f32[384]{0:T(512)S(1)} fusion(bf16[640,384]{1,0:T(8,128)(2,1)S(1)} %collective-permute-done, bf16[640,384]{1,0:T(8,128)(2,1)S(1)} %collective-permute-done.1), kind=kOutput, calls=%fused_computation.46 | convolution fusion | flops 189185664 | bytes 984576 | tf_op jit(solution)/shard_map/dot_general | solution.py:15
  24.5 0.5 %fusion.29 = f32[384]{0:T(512)S(1)} fusion(bf16[640,384]{1,0:T(8,128)(2,1)S(1)} %collective-permute-done), kind=kOutput, calls=%fused_computation.45 | convolution fusion | flops 189185664 | bytes 493056 | tf_op jit(solution)/shard_map/dot_general | solution.py:15
  25.0 0.7 %collective-permute-start.2 = (bf16[640,384]{1,0:T(8,128)(2,1)S(1)}, bf16[640,384]{1,0:T(8,128)(2,1)S(1)}, u32[]{:S(2)}, u32[]{:S(2)}) collective-permute-start(bf16[640,384]{1,0:T(8,128)(2,1)S(1)} %collective-permute-done), channel_id=1, source_target_pairs={{1,2},{2,1},{5,6},{6,5},{9,10},{10,9},{13,14},{14,13},{17,18},{18,... | collective-permute-start | bytes 1474568 | tf_op jit(solution)/shard_map/ppermute | solution.py:33
  25.7 0.5 %fusion.28 = f32[384]{0:T(512)S(1)} fusion(bf16[640,384]{1,0:T(8,128)(2,1)S(1)} %collective-permute-done, bf16[640,384]{1,0:T(8,128)(2,1)S(1)} %copy-done), kind=kOutput, calls=%fused_computation.44 | convolution fusion | flops 189185664 | bytes 984576 | tf_op jit(solution)/shard_map/dot_general | solution.py:15
  26.2 0.5 %fusion.21 = f32[384]{0:T(512)S(1)} fusion(bf16[640,384]{1,0:T(8,128)(2,1)S(1)} %collective-permute-done.3, bf16[640,384]{1,0:T(8,128)(2,1)S(1)} %collective-permute-done), kind=kOutput, calls=%fused_computation.37 | convolution fusion | flops 189185664 | bytes 984576 | tf_op jit(solution)/shard_map/dot_general | solution.py:15
  26.7 0.5 %fusion.17 = f32[384]{0:T(512)S(1)} fusion(bf16[640,384]{1,0:T(8,128)(2,1)S(1)} %copy-done, bf16[640,384]{1,0:T(8,128)(2,1)S(1)} %collective-permute-done), kind=kOutput, calls=%fused_computation.33 | convolution fusion | flops 189185664 | bytes 984576 | tf_op jit(solution)/shard_map/dot_general | solution.py:15
  27.3 0.0 collective-permute-done.2
  27.3 0.5 %fusion.23 = f32[384]{0:T(512)S(1)} fusion(bf16[640,384]{1,0:T(8,128)(2,1)S(1)} %collective-permute-done.3, bf16[640,384]{1,0:T(8,128)(2,1)S(1)} %collective-permute-done.2), kind=kOutput, calls=%fused_computation.39 | convolution fusion | flops 189185664 | bytes 984576 | tf_op jit(solution)/shard_map/dot_general | solution.py:15
  27.8 5.3 %collective-permute-done.4 = bf16[640,384]{1,0:T(8,128)(2,1)S(1)} collective-permute-done((bf16[640,384]{1,0:T(8,128)(2,1)S(1)}, bf16[640,384]{1,0:T(8,128)(2,1)S(1)}, u32[]{:S(2)}, u32[]{:S(2)}) %collective-permute-start.4) | collective-permute-done | bytes 491552 | tf_op jit(solution)/shard_map/ppermute | solution.py:40
  33.2 0.5 %fusion.26 = f32[384]{0:T(512)S(1)} fusion(bf16[640,384]{1,0:T(8,128)(2,1)S(1)} %collective-permute-done.4, bf16[640,384]{1,0:T(8,128)(2,1)S(1)} %collective-permute-done.1), kind=kOutput, calls=%fused_computation.42 | convolution fusion | flops 189185664 | bytes 984576 | tf_op jit(solution)/shard_map/dot_general | solution.py:15
  33.7 0.5 %fusion.25 = f32[384]{0:T(512)S(1)} fusion(bf16[640,384]{1,0:T(8,128)(2,1)S(1)} %collective-permute-done.4, bf16[640,384]{1,0:T(8,128)(2,1)S(1)} %collective-permute-done), kind=kOutput, calls=%fused_computation.41 | convolution fusion | flops 189185664 | bytes 984576 | tf_op jit(solution)/shard_map/dot_general | solution.py:15
  34.3 0.5 %fusion.24 = f32[384]{0:T(512)S(1)} fusion(bf16[640,384]{1,0:T(8,128)(2,1)S(1)} %collective-permute-done.4, bf16[640,384]{1,0:T(8,128)(2,1)S(1)} %copy-done), kind=kOutput, calls=%fused_computation.40 | convolution fusion | flops 189185664 | bytes 984576 | tf_op jit(solution)/shard_map/dot_general | solution.py:15
  34.8 0.5 %fusion.27 = f32[384]{0:T(512)S(1)} fusion(bf16[640,384]{1,0:T(8,128)(2,1)S(1)} %collective-permute-done.4, bf16[640,384]{1,0:T(8,128)(2,1)S(1)} %collective-permute-done.2), kind=kOutput, calls=%fused_computation.43 | convolution fusion | flops 189185664 | bytes 984576 | tf_op jit(solution)/shard_map/dot_general | solution.py:15
  35.3 2.4 %collective-permute-start.5 = (f32[768]{0:T(1024)S(1)}, f32[768]{0:T(1024)S(1)}, u32[]{:S(2)}, u32[]{:S(2)}) collective-permute-start(f32[768]{0:T(1024)S(1)} %pad_maximum_fusion), channel_id=1, source_target_pairs={{4,0},{8,4},{12,8},{5,1},{9,5},{13,9},{6,2},{10,6},{14,10},{7,3},{... | collective-permute-start | bytes 9224 | tf_op jit(solution)/shard_map/ppermute | solution.py:43
  37.8 0.5 %fusion.31 = f32[384]{0:T(512)S(1)} fusion(bf16[640,384]{1,0:T(8,128)(2,1)S(1)} %collective-permute-done, bf16[640,384]{1,0:T(8,128)(2,1)S(1)} %collective-permute-done.2), kind=kOutput, calls=%fused_computation.47 | convolution fusion | flops 189185664 | bytes 984576 | tf_op jit(solution)/shard_map/dot_general | solution.py:15
  38.3 2.0 %collective-permute-done.5 = f32[768]{0:T(1024)S(1)} collective-permute-done((f32[768]{0:T(1024)S(1)}, f32[768]{0:T(1024)S(1)}, u32[]{:S(2)}, u32[]{:S(2)}) %collective-permute-start.5) | collective-permute-done | bytes 3104 | tf_op jit(solution)/shard_map/ppermute | solution.py:43
  40.3 1.3 %collective-permute-start.6 = (f32[384]{0:T(512)S(1)}, f32[384]{0:T(512)S(1)}, u32[]{:S(2)}, u32[]{:S(2)}) collective-permute-start(f32[384]{0:T(512)S(1)} %slice_add_fusion), channel_id=1, source_target_pairs={{1,0},{2,3},{5,4},{6,7},{9,8},{10,11},{13,12},{14,15},{17,16},{18,... | collective-permute-start | bytes 4616 | tf_op jit(solution)/shard_map/ppermute | solution.py:47
  41.6 0.5 %fusion.19 = f32[384]{0:T(512)S(1)} fusion(bf16[640,384]{1,0:T(8,128)(2,1)S(1)} %copy-done, bf16[640,384]{1,0:T(8,128)(2,1)S(1)} %collective-permute-done.2), kind=kOutput, calls=%fused_computation.35 | convolution fusion | flops 189185664 | bytes 984576 | tf_op jit(solution)/shard_map/dot_general | solution.py:15
  42.1 7.2 %collective-permute-done.6 = f32[384]{0:T(512)S(1)} collective-permute-done((f32[384]{0:T(512)S(1)}, f32[384]{0:T(512)S(1)}, u32[]{:S(2)}, u32[]{:S(2)}) %collective-permute-start.6) | collective-permute-done | bytes 1568 | tf_op jit(solution)/shard_map/ppermute | solution.py:47
  49.3 0.6 %add_select_fusion = f32[384]{0:T(512)} fusion(f32[384]{0:T(512)S(1)} %collective-permute-done.6, f32[768]{0:T(1024)S(1)} %collective-permute-done.5, f32[384]{0:T(512)S(1)} %fusion.19, f32[384]{0:T(512)S(1)} %fusion.18, f32[384]{0:T(512)S(1)} %fusion.16, f32[384]{0:T(512)S(1)} %fusion.17, pred[]{:T(512)S(6)} %or.3), kind=kLoop, calls=%fused_computation.50 | loop fusion | flops 1920 | bytes 10753 | tf_op jit(solution)/shard_map/jit(_where)/select_n | solution.py:49
  (5 shorter events, 0.0 us)
Async XLA Ops:
  0.0 10.6 %collective-permute-start.3 = (bf16[640,384]{1,0:T(8,128)(2,1)}, bf16[640,384]{1,0:T(8,128)(2,1)S(1)}, u32[]{:S(2)}, u32[]{:S(2)}) collective-permute-start(bf16[640,384]{1,0:T(8,128)(2,1)} %param.1), channel_id=1, source_target_pairs={{0,4},{4,8},{8,12},{1,5},{5,9},{9,13},{2,6},{6,10},{10,14},{3,7},{... | collective-permute-start | bytes 1474568 | tf_op jit(solution)/shard_map/ppermute | solution.py:38
  4.5 13.8 %collective-permute-start = (bf16[640,384]{1,0:T(8,128)(2,1)}, bf16[640,384]{1,0:T(8,128)(2,1)S(1)}, u32[]{:S(2)}, u32[]{:S(2)}) collective-permute-start(bf16[640,384]{1,0:T(8,128)(2,1)} %param.1), channel_id=1, source_target_pairs={{0,1},{3,2},{4,5},{7,6},{8,9},{11,10},{12,13},{15,14},{16,17},{19,... | collective-permute-start | bytes 1474568 | tf_op jit(solution)/shard_map/ppermute | solution.py:31
  7.7 15.1 %collective-permute-start.1 = (bf16[640,384]{1,0:T(8,128)(2,1)}, bf16[640,384]{1,0:T(8,128)(2,1)S(1)}, u32[]{:S(2)}, u32[]{:S(2)}) collective-permute-start(bf16[640,384]{1,0:T(8,128)(2,1)} %param.1), channel_id=1, source_target_pairs={{1,2},{2,1},{5,6},{6,5},{9,10},{10,9},{13,14},{14,13},{17,18},{18,... | collective-permute-start | bytes 1474568 | tf_op jit(solution)/shard_map/ppermute | solution.py:32
  8.5 13.9 %copy-start = (bf16[640,384]{1,0:T(8,128)(2,1)S(1)}, bf16[640,384]{1,0:T(8,128)(2,1)}, u32[]{:S(2)}) copy-start(bf16[640,384]{1,0:T(8,128)(2,1)} %param.1) | copy-start | bytes 1474564
  18.3 14.9 %collective-permute-start.4 = (bf16[640,384]{1,0:T(8,128)(2,1)S(1)}, bf16[640,384]{1,0:T(8,128)(2,1)S(1)}, u32[]{:S(2)}, u32[]{:S(2)}) collective-permute-start(bf16[640,384]{1,0:T(8,128)(2,1)S(1)} %collective-permute-done.3), channel_id=1, source_target_pairs={{0,1},{3,2},{4,5},{7,6},{8,9},{11,10},{12,13},{15,14},{16,17},{19,... | collective-permute-start | bytes 1474568 | tf_op jit(solution)/shard_map/ppermute | solution.py:40
  25.0 2.3 %collective-permute-start.2 = (bf16[640,384]{1,0:T(8,128)(2,1)S(1)}, bf16[640,384]{1,0:T(8,128)(2,1)S(1)}, u32[]{:S(2)}, u32[]{:S(2)}) collective-permute-start(bf16[640,384]{1,0:T(8,128)(2,1)S(1)} %collective-permute-done), channel_id=1, source_target_pairs={{1,2},{2,1},{5,6},{6,5},{9,10},{10,9},{13,14},{14,13},{17,18},{18,... | collective-permute-start | bytes 1474568 | tf_op jit(solution)/shard_map/ppermute | solution.py:33
  35.3 4.9 %collective-permute-start.5 = (f32[768]{0:T(1024)S(1)}, f32[768]{0:T(1024)S(1)}, u32[]{:S(2)}, u32[]{:S(2)}) collective-permute-start(f32[768]{0:T(1024)S(1)} %pad_maximum_fusion), channel_id=1, source_target_pairs={{4,0},{8,4},{12,8},{5,1},{9,5},{13,9},{6,2},{10,6},{14,10},{7,3},{... | collective-permute-start | bytes 9224 | tf_op jit(solution)/shard_map/ppermute | solution.py:43
  40.3 9.0 %collective-permute-start.6 = (f32[384]{0:T(512)S(1)}, f32[384]{0:T(512)S(1)}, u32[]{:S(2)}, u32[]{:S(2)}) collective-permute-start(f32[384]{0:T(512)S(1)} %slice_add_fusion), channel_id=1, source_target_pairs={{1,0},{2,3},{5,4},{6,7},{9,8},{10,11},{13,12},{14,15},{17,16},{18,... | collective-permute-start | bytes 4616 | tf_op jit(solution)/shard_map/ppermute | solution.py:47

commit v4 on v2

--- a/solution.py
+++ b/solution.py
@@ -31,14 +31,17 @@
     adopt = lax.ppermute(own, "group", [(0, 1), (3, 2)])
     nbr = lax.ppermute(own, "group", [(1, 2), (2, 1)])
     far = lax.ppermute(adopt, "group", [(1, 2), (2, 1)])
-    panel = [own, adopt, nbr, far]
+    early = jnp.concatenate([own, adopt, nbr], axis=1)
 
     onward = [(g, g + 1) for g in range(lax.axis_size("genome") - 1)]
     backward = [(b, a) for a, b in onward]
-    rows = [own, adopt] + [lax.ppermute(r, "genome", onward) for r in (own, adopt)]
-    sums = [sum(row_squares(r, c, scaling) for c in panel) for r in rows]
+    prev = [lax.ppermute(r, "genome", onward) for r in (own, adopt)]
+    width = own.shape[1]
+    sums = []
+    for rows in (jnp.concatenate([own, adopt], axis=1), jnp.concatenate(prev, axis=1)):
+        total = row_squares(rows, early, scaling) + row_squares(rows, far, scaling)
+        sums += [total[:width], total[width:]]
     following = lax.ppermute(jnp.concatenate(sums[2:]), "genome", backward)
-    width = own.shape[1]
     at_hub = sums[0] + following[:width]
     adopted = sums[1] + following[width:]
     at_end = lax.ppermute(adopted, "group", [(1, 0), (2, 3)])

time: 43.6 us -> 41.5 us (0.952)
  matrix products: 9.68 us -> 5.04 us
  local copies, waits for them, and re-layouts: 0.01 us -> 1.48 us
  waiting for transfers between devices: 15.7 us -> 16.8 us
    dot_general x16 -> x4, matrix products: 9.68 us -> 5.04 us  [row_squares(): lax.dot_general(rows, columns, (((0,), (0,)), ((), ())), preferred_elemen...]
    ppermute x2, waiting for transfers between devices: 0.77 us -> 3.6 us  [hub_plan(): prev = [lax.ppermute(r, 'genome', onward) for r in (own, adopt)]]
    ppermute x1, waiting for transfers between devices: 8.03 us -> 5.83 us  [hub_plan(): at_end = lax.ppermute(adopted, 'group', [(1, 0), (2, 3)])]
    unnamed x2, local copies, waits for them, and re-layouts: 0.01 us -> 1.17 us
    ppermute x1, waiting for transfers between devices: 3.71 us -> 4.37 us  [hub_plan(): adopt = lax.ppermute(own, 'group', [(0, 1), (3, 2)])]
  transfers between devices with their start and end apart: 7 -> 7, of which waited for: 4 -> 4; matrix products, arithmetic and copies ran while one was open for 20% -> 14% of each run, Pallas kernels for 0% -> 0%
where the time goes in v4:
time: 41.5 us; the launch traced here: 41.2 us
  starting transfers between devices  17.1 us (41%)
  waiting for transfers between devices  16.8 us (40%)
  matrix products  5.04 us (12%)
  local copies, waits for them, and re-layouts  1.48 us (4%)
  other arithmetic  0.6 us (1%)
    ppermute x2, starting transfers between devices, hub_plan(): prev = [lax.ppermute(r, 'genome', onward) for r in (own, adopt)]  8.51 us
    ppermute x1, waiting for transfers between devices, hub_plan(): at_end = lax.ppermute(adopted, 'group', [(1, 0), (2, 3)])  5.83 us
    dot_general x4, matrix products, row_squares(): lax.dot_general(rows, columns, (((0,), (0,)), ((), ())), preferred_elemen...  5.04 us
    ppermute x1, waiting for transfers between devices, hub_plan(): adopt = lax.ppermute(own, 'group', [(0, 1), (3, 2)])  4.37 us
    ppermute x1, starting transfers between devices, hub_plan(): adopt = lax.ppermute(own, 'group', [(0, 1), (3, 2)])  4.05 us
    ppermute x2, waiting for transfers between devices, hub_plan(): prev = [lax.ppermute(r, 'genome', onward) for r in (own, adopt)]  3.6 us
    ppermute x1, waiting for transfers between devices, hub_plan(): following = lax.ppermute(jnp.concatenate(sums[2:]), 'genome', backward)  3.03 us
    ppermute x1, starting transfers between devices, hub_plan(): following = lax.ppermute(jnp.concatenate(sums[2:]), 'genome', backward)  1.92 us
  transfers between devices with their start and end apart: 7, of which 4 were waited for; matrix products, arithmetic and copies ran while one was open for 14% of the time, Pallas kernels for 0%

profile of v4, /device:TPU:1, one launch (start us, length us, event | category | flops | bytes accessed | tf_op | source)
XLA Modules:
  0.0 41.2 jit_solution(15861974089042913920)
XLA Ops:
  0.0 4.0 %collective-permute-start = (bf16[640,384]{1,0:T(8,128)(2,1)}, bf16[640,384]{1,0:T(8,128)(2,1)S(1)}, u32[]{:S(2)}, u32[]{:S(2)}) collective-permute-start(bf16[640,384]{1,0:T(8,128)(2,1)} %param.1), channel_id=1, source_target_pairs={{0,1},{3,2},{4,5},{7,6},{8,9},{11,10},{12,13},{15,14},{16,17},{19,... | collective-permute-start | bytes 1474568 | tf_op jit(solution)/shard_map/ppermute | solution.py:31
  4.1 4.0 %collective-permute-start.3 = (bf16[640,384]{1,0:T(8,128)(2,1)}, bf16[640,384]{1,0:T(8,128)(2,1)S(1)}, u32[]{:S(2)}, u32[]{:S(2)}) collective-permute-start(bf16[640,384]{1,0:T(8,128)(2,1)} %param.1), channel_id=1, source_target_pairs={{0,4},{4,8},{8,12},{1,5},{5,9},{9,13},{2,6},{6,10},{10,14},{3,7},{... | collective-permute-start | bytes 1474568 | tf_op jit(solution)/shard_map/ppermute | solution.py:38
  8.0 0.7 %collective-permute-start.1 = (bf16[640,384]{1,0:T(8,128)(2,1)}, bf16[640,384]{1,0:T(8,128)(2,1)S(1)}, u32[]{:S(2)}, u32[]{:S(2)}) collective-permute-start(bf16[640,384]{1,0:T(8,128)(2,1)} %param.1), channel_id=1, source_target_pairs={{1,2},{2,1},{5,6},{6,5},{9,10},{10,9},{13,14},{14,13},{17,18},{18,... | collective-permute-start | bytes 1474568 | tf_op jit(solution)/shard_map/ppermute | solution.py:32
  8.7 1.1 %constant_dynamic-update-slice_fusion.1 = (bf16[640,768]{1,0:T(8,128)(2,1)S(1)}, bf16[640,1152]{1,0:T(8,128)(2,1)S(1)}) fusion(bf16[640,384]{1,0:T(8,128)(2,1)} %param.1), kind=kLoop, calls=%fused_computation.13 | loop fusion | bytes 1474560
  9.8 4.4 %collective-permute-done = bf16[640,384]{1,0:T(8,128)(2,1)S(1)} collective-permute-done((bf16[640,384]{1,0:T(8,128)(2,1)}, bf16[640,384]{1,0:T(8,128)(2,1)S(1)}, u32[]{:S(2)}, u32[]{:S(2)}) %collective-permute-start) | collective-permute-done | bytes 491552 | tf_op jit(solution)/shard_map/ppermute | solution.py:31
  14.2 0.7 %collective-permute-start.2 = (bf16[640,384]{1,0:T(8,128)(2,1)S(1)}, bf16[640,384]{1,0:T(8,128)(2,1)S(1)}, u32[]{:S(2)}, u32[]{:S(2)}) collective-permute-start(bf16[640,384]{1,0:T(8,128)(2,1)S(1)} %collective-permute-done), channel_id=1, source_target_pairs={{1,2},{2,1},{5,6},{6,5},{9,10},{10,9},{13,14},{14,13},{17,18},{18,... | collective-permute-start | bytes 1474568 | tf_op jit(solution)/shard_map/ppermute | solution.py:33
  14.9 4.6 %collective-permute-start.4 = (bf16[640,384]{1,0:T(8,128)(2,1)S(1)}, bf16[640,384]{1,0:T(8,128)(2,1)S(1)}, u32[]{:S(2)}, u32[]{:S(2)}) collective-permute-start(bf16[640,384]{1,0:T(8,128)(2,1)S(1)} %collective-permute-done), channel_id=1, source_target_pairs={{0,4},{4,8},{8,12},{1,5},{5,9},{9,13},{2,6},{6,10},{10,14},{3,7},{... | collective-permute-start | bytes 1474568 | tf_op jit(solution)/shard_map/ppermute | solution.py:38
  19.5 0.0 collective-permute-done.3
  19.5 0.1 constant_dynamic-update-slice_fusion.6
  19.5 0.2 constant_dynamic-update-slice_fusion
  19.7 0.0 collective-permute-done.1
  19.7 0.1 constant_dynamic-update-slice_fusion.2
  19.8 1.8 %fusion.2 = f32[768]{0:T(1024)S(1)} fusion(bf16[640,768]{1,0:T(8,128)(2,1)S(1)} %get-tuple-element.5, bf16[640,1152]{1,0:T(8,128)(2,1)S(1)} %constant_dynamic-update-slice_fusion.2), kind=kOutput, calls=%fused_computation.4 | convolution fusion | flops 1135115520 | bytes 2460672 | tf_op jit(solution)/shard_map/dot_general | solution.py:15
  21.6 3.6 %collective-permute-done.4 = bf16[640,384]{1,0:T(8,128)(2,1)S(1)} collective-permute-done((bf16[640,384]{1,0:T(8,128)(2,1)S(1)}, bf16[640,384]{1,0:T(8,128)(2,1)S(1)}, u32[]{:S(2)}, u32[]{:S(2)}) %collective-permute-start.4) | collective-permute-done | bytes 491552 | tf_op jit(solution)/shard_map/ppermute | solution.py:38
  25.2 0.1 constant_dynamic-update-slice_fusion.5
  25.3 1.8 %fusion.3 = f32[768]{0:T(1024)S(1)} fusion(bf16[640,768]{1,0:T(8,128)(2,1)S(1)} %constant_dynamic-update-slice_fusion.5, bf16[640,1152]{1,0:T(8,128)(2,1)S(1)} %constant_dynamic-update-slice_fusion.2), kind=kOutput, calls=%fused_computation.5 | convolution fusion | flops 1135115520 | bytes 2460672 | tf_op jit(solution)/shard_map/dot_general | solution.py:15
  27.1 0.0 collective-permute-done.2
  27.1 0.7 %fusion.7 = f32[768]{0:T(1024)S(1)} fusion(bf16[640,768]{1,0:T(8,128)(2,1)S(1)} %constant_dynamic-update-slice_fusion.5, bf16[640,384]{1,0:T(8,128)(2,1)S(1)} %collective-permute-done.2), kind=kOutput, calls=%fused_computation.11 | convolution fusion | flops 378371328 | bytes 1477632 | tf_op jit(solution)/shard_map/dot_general | solution.py:15
  27.8 1.9 %collective-permute-start.5 = (f32[768]{0:T(1024)S(1)}, f32[768]{0:T(1024)S(1)}, u32[]{:S(2)}, u32[]{:S(2)}) collective-permute-start(f32[768]{0:T(1024)S(1)} %add.13), channel_id=1, source_target_pairs={{4,0},{8,4},{12,8},{5,1},{9,5},{13,9},{6,2},{10,6},{14,10},{7,3},{... | collective-permute-start | bytes 9224 | tf_op jit(solution)/shard_map/ppermute | solution.py:44
  29.8 0.7 %fusion.6 = f32[768]{0:T(1024)S(1)} fusion(bf16[640,768]{1,0:T(8,128)(2,1)S(1)} %get-tuple-element.5, bf16[640,384]{1,0:T(8,128)(2,1)S(1)} %collective-permute-done.2), kind=kOutput, calls=%fused_computation.10 | convolution fusion | flops 378371328 | bytes 1477632 | tf_op jit(solution)/shard_map/dot_general | solution.py:15
  30.5 3.0 %collective-permute-done.5 = f32[768]{0:T(1024)S(1)} collective-permute-done((f32[768]{0:T(1024)S(1)}, f32[768]{0:T(1024)S(1)}, u32[]{:S(2)}, u32[]{:S(2)}) %collective-permute-start.5) | collective-permute-done | bytes 3104 | tf_op jit(solution)/shard_map/ppermute | solution.py:44
  33.5 1.3 %collective-permute-start.6 = (f32[384]{0:T(512)S(1)}, f32[384]{0:T(512)S(1)}, u32[]{:S(2)}, u32[]{:S(2)}) collective-permute-start(f32[384]{0:T(512)S(1)} %slice_add_fusion), channel_id=1, source_target_pairs={{1,0},{2,3},{5,4},{6,7},{9,8},{10,11},{13,12},{14,15},{17,16},{18,... | collective-permute-start | bytes 4616 | tf_op jit(solution)/shard_map/ppermute | solution.py:47
  34.8 5.8 %collective-permute-done.6 = f32[384]{0:T(512)S(1)} collective-permute-done((f32[384]{0:T(512)S(1)}, f32[384]{0:T(512)S(1)}, u32[]{:S(2)}, u32[]{:S(2)}) %collective-permute-start.6) | collective-permute-done | bytes 1568 | tf_op jit(solution)/shard_map/ppermute | solution.py:47
  40.6 0.6 %add_select_fusion = f32[384]{0:T(512)} fusion(f32[384]{0:T(512)S(1)} %collective-permute-done.6, f32[768]{0:T(1024)S(1)} %collective-permute-done.5, f32[768]{0:T(1024)S(1)} %add.12, pred[]{:T(512)S(6)} %or.3), kind=kLoop, calls=%fused_computation.20 | loop fusion | flops 768 | bytes 6145 | tf_op jit(solution)/shard_map/jit(_where)/select_n | solution.py:49
  (3 shorter events, 0.0 us)
Async XLA Ops:
  0.0 14.2 %collective-permute-start = (bf16[640,384]{1,0:T(8,128)(2,1)}, bf16[640,384]{1,0:T(8,128)(2,1)S(1)}, u32[]{:S(2)}, u32[]{:S(2)}) collective-permute-start(bf16[640,384]{1,0:T(8,128)(2,1)} %param.1), channel_id=1, source_target_pairs={{0,1},{3,2},{4,5},{7,6},{8,9},{11,10},{12,13},{15,14},{16,17},{19,... | collective-permute-start | bytes 1474568 | tf_op jit(solution)/shard_map/ppermute | solution.py:31
  4.1 15.4 %collective-permute-start.3 = (bf16[640,384]{1,0:T(8,128)(2,1)}, bf16[640,384]{1,0:T(8,128)(2,1)S(1)}, u32[]{:S(2)}, u32[]{:S(2)}) collective-permute-start(bf16[640,384]{1,0:T(8,128)(2,1)} %param.1), channel_id=1, source_target_pairs={{0,4},{4,8},{8,12},{1,5},{5,9},{9,13},{2,6},{6,10},{10,14},{3,7},{... | collective-permute-start | bytes 1474568 | tf_op jit(solution)/shard_map/ppermute | solution.py:38
  8.0 11.7 %collective-permute-start.1 = (bf16[640,384]{1,0:T(8,128)(2,1)}, bf16[640,384]{1,0:T(8,128)(2,1)S(1)}, u32[]{:S(2)}, u32[]{:S(2)}) collective-permute-start(bf16[640,384]{1,0:T(8,128)(2,1)} %param.1), channel_id=1, source_target_pairs={{1,2},{2,1},{5,6},{6,5},{9,10},{10,9},{13,14},{14,13},{17,18},{18,... | collective-permute-start | bytes 1474568 | tf_op jit(solution)/shard_map/ppermute | solution.py:32
  14.2 12.9 %collective-permute-start.2 = (bf16[640,384]{1,0:T(8,128)(2,1)S(1)}, bf16[640,384]{1,0:T(8,128)(2,1)S(1)}, u32[]{:S(2)}, u32[]{:S(2)}) collective-permute-start(bf16[640,384]{1,0:T(8,128)(2,1)S(1)} %collective-permute-done), channel_id=1, source_target_pairs={{1,2},{2,1},{5,6},{6,5},{9,10},{10,9},{13,14},{14,13},{17,18},{18,... | collective-permute-start | bytes 1474568 | tf_op jit(solution)/shard_map/ppermute | solution.py:33
  14.9 10.3 %collective-permute-start.4 = (bf16[640,384]{1,0:T(8,128)(2,1)S(1)}, bf16[640,384]{1,0:T(8,128)(2,1)S(1)}, u32[]{:S(2)}, u32[]{:S(2)}) collective-permute-start(bf16[640,384]{1,0:T(8,128)(2,1)S(1)} %collective-permute-done), channel_id=1, source_target_pairs={{0,4},{4,8},{8,12},{1,5},{5,9},{9,13},{2,6},{6,10},{10,14},{3,7},{... | collective-permute-start | bytes 1474568 | tf_op jit(solution)/shard_map/ppermute | solution.py:38
  27.8 5.7 %collective-permute-start.5 = (f32[768]{0:T(1024)S(1)}, f32[768]{0:T(1024)S(1)}, u32[]{:S(2)}, u32[]{:S(2)}) collective-permute-start(f32[768]{0:T(1024)S(1)} %add.13), channel_id=1, source_target_pairs={{4,0},{8,4},{12,8},{5,1},{9,5},{13,9},{6,2},{10,6},{14,10},{7,3},{... | collective-permute-start | bytes 9224 | tf_op jit(solution)/shard_map/ppermute | solution.py:44
  33.5 7.1 %collective-permute-start.6 = (f32[384]{0:T(512)S(1)}, f32[384]{0:T(512)S(1)}, u32[]{:S(2)}, u32[]{:S(2)}) collective-permute-start(f32[384]{0:T(512)S(1)} %slice_add_fusion), channel_id=1, source_target_pairs={{1,0},{2,3},{5,4},{6,7},{9,8},{10,11},{13,12},{14,15},{17,16},{18,... | collective-permute-start | bytes 4616 | tf_op jit(solution)/shard_map/ppermute | solution.py:47

commit v5 on v3

--- a/solution.py
+++ b/solution.py
@@ -31,17 +31,20 @@
     adopt = lax.ppermute(own, "group", [(0, 1), (3, 2)])
     nbr = lax.ppermute(own, "group", [(1, 2), (2, 1)])
     far = lax.ppermute(adopt, "group", [(1, 2), (2, 1)])
-    panel = [own, adopt, nbr, far]
+    early = jnp.concatenate([own, adopt, nbr], axis=1)
 
     onward = [(g, g + 1) for g in range(lax.axis_size("genome") - 1)]
     backward = [(b, a) for a, b in onward]
     prev_own = lax.ppermute(own, "genome", onward)
     relay, _ = lax.optimization_barrier((prev_own, adopt))
     prev_adopt = lax.ppermute(relay, "group", [(0, 1), (3, 2)])
-    rows = [own, adopt, prev_own, prev_adopt]
-    sums = [sum(row_squares(r, c, scaling) for c in panel) for r in rows]
+    width = own.shape[1]
+    pair = jnp.concatenate([own, adopt], axis=1)
+    total = row_squares(pair, early, scaling) + row_squares(pair, far, scaling)
+    sums = [total[:width], total[width:]]
+    for rows in (prev_own, prev_adopt):
+        sums.append(row_squares(rows, early, scaling) + row_squares(rows, far, scaling))
     following = lax.ppermute(jnp.concatenate(sums[2:]), "genome", backward)
-    width = own.shape[1]
     at_hub = sums[0] + following[:width]
     adopted = sums[1] + following[width:]
     at_end = lax.ppermute(adopted, "group", [(1, 0), (2, 3)])

time: 50.1 us -> 41.6 us (0.83)
  waiting for transfers between devices: 22.5 us -> 14.5 us
  matrix products: 9.69 us -> 5.69 us
  starting transfers between devices: 16.8 us -> 19.1 us
  local copies, waits for them, and re-layouts: 0.01 us -> 1.35 us
    dot_general x16 -> x6, matrix products: 9.69 us -> 5.69 us  [row_squares(): lax.dot_general(rows, columns, (((0,), (0,)), ((), ())), preferred_elemen...]
    ppermute x1, waiting for transfers between devices: 7.16 us -> 3.39 us  [hub_plan(): at_end = lax.ppermute(adopted, 'group', [(1, 0), (2, 3)])]
    ppermute x1, waiting for transfers between devices: 7.7 us -> 4.37 us  [hub_plan(): adopt = lax.ppermute(own, 'group', [(0, 1), (3, 2)])]
    ppermute x1, starting transfers between devices: 2.41 us -> 4.38 us  [hub_plan(): following = lax.ppermute(jnp.concatenate(sums[2:]), 'genome', backward)]
    unnamed x2 -> x1, local copies, waits for them, and re-layouts: 0.01 us -> 1.12 us
    ppermute x1, starting transfers between devices: 3.23 us -> 4.05 us  [hub_plan(): adopt = lax.ppermute(own, 'group', [(0, 1), (3, 2)])]
    ppermute x1, starting transfers between devices: 4.5 us -> 3.96 us  [hub_plan(): prev_own = lax.ppermute(own, 'genome', onward)]
  transfers between devices with their start and end apart: 7 -> 7, of which waited for: 5 -> 4; matrix products, arithmetic and copies ran while one was open for 15% -> 15% of each run, Pallas kernels for 0% -> 0%
where the time goes in v5:
time: 41.6 us; the launch traced here: 41.3 us
  starting transfers between devices  19.1 us (46%)
  waiting for transfers between devices  14.5 us (35%)
  matrix products  5.69 us (14%)
  local copies, waits for them, and re-layouts  1.35 us (3%)
  other arithmetic  0.61 us (1%)
    dot_general x6, matrix products, row_squares(): lax.dot_general(rows, columns, (((0,), (0,)), ((), ())), preferred_elemen...  5.69 us
    ppermute x1, waiting for transfers between devices, hub_plan(): prev_adopt = lax.ppermute(relay, 'group', [(0, 1), (3, 2)])  5.05 us
    ppermute x1, starting transfers between devices, hub_plan(): following = lax.ppermute(jnp.concatenate(sums[2:]), 'genome', backward)  4.38 us
    ppermute x1, waiting for transfers between devices, hub_plan(): adopt = lax.ppermute(own, 'group', [(0, 1), (3, 2)])  4.37 us
    ppermute x1, starting transfers between devices, hub_plan(): adopt = lax.ppermute(own, 'group', [(0, 1), (3, 2)])  4.05 us
    ppermute x1, starting transfers between devices, hub_plan(): prev_adopt = lax.ppermute(relay, 'group', [(0, 1), (3, 2)])  4.02 us
    ppermute x1, starting transfers between devices, hub_plan(): prev_own = lax.ppermute(own, 'genome', onward)  3.96 us
    ppermute x1, waiting for transfers between devices, hub_plan(): at_end = lax.ppermute(adopted, 'group', [(1, 0), (2, 3)])  3.39 us
  transfers between devices with their start and end apart: 7, of which 4 were waited for; matrix products, arithmetic and copies ran while one was open for 15% of the time, Pallas kernels for 0%

profile of v5, /device:TPU:1, one launch (start us, length us, event | category | flops | bytes accessed | tf_op | source)
XLA Modules:
  0.0 41.3 jit_solution(18151292097709258558)
XLA Ops:
  0.0 4.0 %collective-permute-start = (bf16[640,384]{1,0:T(8,128)(2,1)}, bf16[640,384]{1,0:T(8,128)(2,1)S(1)}, u32[]{:S(2)}, u32[]{:S(2)}) collective-permute-start(bf16[640,384]{1,0:T(8,128)(2,1)} %param.1), channel_id=1, source_target_pairs={{0,1},{3,2},{4,5},{7,6},{8,9},{11,10},{12,13},{15,14},{16,17},{19,... | collective-permute-start | bytes 1474568 | tf_op jit(solution)/shard_map/ppermute | solution.py:31
  4.1 4.0 %collective-permute-start.3 = (bf16[640,384]{1,0:T(8,128)(2,1)}, bf16[640,384]{1,0:T(8,128)(2,1)S(1)}, u32[]{:S(2)}, u32[]{:S(2)}) collective-permute-start(bf16[640,384]{1,0:T(8,128)(2,1)} %param.1), channel_id=1, source_target_pairs={{0,4},{4,8},{8,12},{1,5},{5,9},{9,13},{2,6},{6,10},{10,14},{3,7},{... | collective-permute-start | bytes 1474568 | tf_op jit(solution)/shard_map/ppermute | solution.py:38
  8.0 0.7 %collective-permute-start.1 = (bf16[640,384]{1,0:T(8,128)(2,1)}, bf16[640,384]{1,0:T(8,128)(2,1)S(1)}, u32[]{:S(2)}, u32[]{:S(2)}) collective-permute-start(bf16[640,384]{1,0:T(8,128)(2,1)} %param.1), channel_id=1, source_target_pairs={{1,2},{2,1},{5,6},{6,5},{9,10},{10,9},{13,14},{14,13},{17,18},{18,... | collective-permute-start | bytes 1474568 | tf_op jit(solution)/shard_map/ppermute | solution.py:32
  8.7 1.1 %constant_dynamic-update-slice_fusion.1 = (bf16[640,768]{1,0:T(8,128)(2,1)S(1)}, bf16[640,1152]{1,0:T(8,128)(2,1)S(1)}) fusion(bf16[640,384]{1,0:T(8,128)(2,1)} %param.1), kind=kLoop, calls=%fused_computation.19 | loop fusion | bytes 1474560
  9.8 4.4 %collective-permute-done = bf16[640,384]{1,0:T(8,128)(2,1)S(1)} collective-permute-done((bf16[640,384]{1,0:T(8,128)(2,1)}, bf16[640,384]{1,0:T(8,128)(2,1)S(1)}, u32[]{:S(2)}, u32[]{:S(2)}) %collective-permute-start) | collective-permute-done | bytes 491552 | tf_op jit(solution)/shard_map/ppermute | solution.py:31
  14.2 0.0 collective-permute-done.3
  14.2 4.0 %collective-permute-start.4 = (bf16[640,384]{1,0:T(8,128)(2,1)S(1)}, bf16[640,384]{1,0:T(8,128)(2,1)S(1)}, u32[]{:S(2)}, u32[]{:S(2)}) collective-permute-start(bf16[640,384]{1,0:T(8,128)(2,1)S(1)} %collective-permute-done.3), channel_id=1, source_target_pairs={{0,1},{3,2},{4,5},{7,6},{8,9},{11,10},{12,13},{15,14},{16,17},{19,... | collective-permute-start | bytes 1474568 | tf_op jit(solution)/shard_map/ppermute | solution.py:40
  18.2 0.7 %collective-permute-start.2 = (bf16[640,384]{1,0:T(8,128)(2,1)S(1)}, bf16[640,384]{1,0:T(8,128)(2,1)S(1)}, u32[]{:S(2)}, u32[]{:S(2)}) collective-permute-start(bf16[640,384]{1,0:T(8,128)(2,1)S(1)} %collective-permute-done), channel_id=1, source_target_pairs={{1,2},{2,1},{5,6},{6,5},{9,10},{10,9},{13,14},{14,13},{17,18},{18,... | collective-permute-start | bytes 1474568 | tf_op jit(solution)/shard_map/ppermute | solution.py:33
  18.9 0.2 constant_dynamic-update-slice_fusion
  19.1 0.0 collective-permute-done.1
  19.1 0.1 constant_dynamic-update-slice_fusion.2
  19.2 1.8 %fusion.3 = f32[768]{0:T(1024)S(1)} fusion(bf16[640,768]{1,0:T(8,128)(2,1)S(1)} %get-tuple-element.7, bf16[640,1152]{1,0:T(8,128)(2,1)S(1)} %constant_dynamic-update-slice_fusion.2), kind=kOutput, calls=%fused_computation.6 | convolution fusion | flops 1135115520 | bytes 2460672 | tf_op jit(solution)/shard_map/dot_general | solution.py:15
  21.0 1.1 %fusion.5 = f32[384]{0:T(512)S(1)} fusion(bf16[640,1152]{1,0:T(8,128)(2,1)S(1)} %constant_dynamic-update-slice_fusion.2, bf16[640,384]{1,0:T(8,128)(2,1)S(1)} %collective-permute-done.3), kind=kOutput, calls=%fused_computation.9 | convolution fusion | flops 567557760 | bytes 1967616 | tf_op jit(solution)/shard_map/dot_general | solution.py:15
  22.1 5.0 %collective-permute-done.4 = bf16[640,384]{1,0:T(8,128)(2,1)S(1)} collective-permute-done((bf16[640,384]{1,0:T(8,128)(2,1)S(1)}, bf16[640,384]{1,0:T(8,128)(2,1)S(1)}, u32[]{:S(2)}, u32[]{:S(2)}) %collective-permute-start.4) | collective-permute-done | bytes 491552 | tf_op jit(solution)/shard_map/ppermute | solution.py:40
  27.2 1.0 %fusion.6 = f32[384]{0:T(512)S(1)} fusion(bf16[640,384]{1,0:T(8,128)(2,1)S(1)} %collective-permute-done.4, bf16[640,1152]{1,0:T(8,128)(2,1)S(1)} %constant_dynamic-update-slice_fusion.2), kind=kOutput, calls=%fused_computation.10 | convolution fusion | flops 567557760 | bytes 1967616 | tf_op jit(solution)/shard_map/dot_general | solution.py:15
  28.2 0.0 collective-permute-done.2
  28.2 0.5 %fusion.11 = f32[384]{0:T(512)S(1)} fusion(bf16[640,384]{1,0:T(8,128)(2,1)S(1)} %collective-permute-done.4, bf16[640,384]{1,0:T(8,128)(2,1)S(1)} %collective-permute-done.2), kind=kOutput, calls=%fused_computation.17 | convolution fusion | flops 189185664 | bytes 984576 | tf_op jit(solution)/shard_map/dot_general | solution.py:15
  28.8 0.5 %fusion.10 = f32[384]{0:T(512)S(1)} fusion(bf16[640,384]{1,0:T(8,128)(2,1)S(1)} %collective-permute-done.3, bf16[640,384]{1,0:T(8,128)(2,1)S(1)} %collective-permute-done.2), kind=kOutput, calls=%fused_computation.16 | convolution fusion | flops 189185664 | bytes 984576 | tf_op jit(solution)/shard_map/dot_general | solution.py:15
  29.3 4.4 %collective-permute-start.5 = (f32[768]{0:T(1024)S(1)}, f32[768]{0:T(1024)S(1)}, u32[]{:S(2)}, u32[]{:S(2)}) collective-permute-start(f32[768]{0:T(1024)S(1)} %pad_maximum_fusion), channel_id=1, source_target_pairs={{4,0},{8,4},{12,8},{5,1},{9,5},{13,9},{6,2},{10,6},{14,10},{7,3},{... | collective-permute-start | bytes 9224 | tf_op jit(solution)/shard_map/ppermute | solution.py:47
  33.7 0.7 %fusion.7 = f32[768]{0:T(1024)S(1)} fusion(bf16[640,768]{1,0:T(8,128)(2,1)S(1)} %get-tuple-element.7, bf16[640,384]{1,0:T(8,128)(2,1)S(1)} %collective-permute-done.2), kind=kOutput, calls=%fused_computation.11 | convolution fusion | flops 378371328 | bytes 1477632 | tf_op jit(solution)/shard_map/dot_general | solution.py:15
  34.4 1.7 %collective-permute-done.5 = f32[768]{0:T(1024)S(1)} collective-permute-done((f32[768]{0:T(1024)S(1)}, f32[768]{0:T(1024)S(1)}, u32[]{:S(2)}, u32[]{:S(2)}) %collective-permute-start.5) | collective-permute-done | bytes 3104 | tf_op jit(solution)/shard_map/ppermute | solution.py:47
  36.1 1.3 %collective-permute-start.6 = (f32[384]{0:T(512)S(1)}, f32[384]{0:T(512)S(1)}, u32[]{:S(2)}, u32[]{:S(2)}) collective-permute-start(f32[384]{0:T(512)S(1)} %slice_add_fusion), channel_id=1, source_target_pairs={{1,0},{2,3},{5,4},{6,7},{9,8},{10,11},{13,12},{14,15},{17,16},{18,... | collective-permute-start | bytes 4616 | tf_op jit(solution)/shard_map/ppermute | solution.py:50
  37.4 3.4 %collective-permute-done.6 = f32[384]{0:T(512)S(1)} collective-permute-done((f32[384]{0:T(512)S(1)}, f32[384]{0:T(512)S(1)}, u32[]{:S(2)}, u32[]{:S(2)}) %collective-permute-start.6) | collective-permute-done | bytes 1568 | tf_op jit(solution)/shard_map/ppermute | solution.py:50
  40.8 0.6 %add_select_fusion = f32[384]{0:T(512)} fusion(f32[384]{0:T(512)S(1)} %collective-permute-done.6, f32[768]{0:T(1024)S(1)} %collective-permute-done.5, f32[768]{0:T(1024)S(1)} %add.15, pred[]{:T(512)S(6)} %or.3), kind=kLoop, calls=%fused_computation.25 | loop fusion | flops 768 | bytes 6145 | tf_op jit(solution)/shard_map/jit(_where)/select_n | solution.py:52
  (5 shorter events, 0.0 us)
Async XLA Ops:
  0.0 14.2 %collective-permute-start = (bf16[640,384]{1,0:T(8,128)(2,1)}, bf16[640,384]{1,0:T(8,128)(2,1)S(1)}, u32[]{:S(2)}, u32[]{:S(2)}) collective-permute-start(bf16[640,384]{1,0:T(8,128)(2,1)} %param.1), channel_id=1, source_target_pairs={{0,1},{3,2},{4,5},{7,6},{8,9},{11,10},{12,13},{15,14},{16,17},{19,... | collective-permute-start | bytes 1474568 | tf_op jit(solution)/shard_map/ppermute | solution.py:31
  4.1 10.2 %collective-permute-start.3 = (bf16[640,384]{1,0:T(8,128)(2,1)}, bf16[640,384]{1,0:T(8,128)(2,1)S(1)}, u32[]{:S(2)}, u32[]{:S(2)}) collective-permute-start(bf16[640,384]{1,0:T(8,128)(2,1)} %param.1), channel_id=1, source_target_pairs={{0,4},{4,8},{8,12},{1,5},{5,9},{9,13},{2,6},{6,10},{10,14},{3,7},{... | collective-permute-start | bytes 1474568 | tf_op jit(solution)/shard_map/ppermute | solution.py:38
  8.0 11.1 %collective-permute-start.1 = (bf16[640,384]{1,0:T(8,128)(2,1)}, bf16[640,384]{1,0:T(8,128)(2,1)S(1)}, u32[]{:S(2)}, u32[]{:S(2)}) collective-permute-start(bf16[640,384]{1,0:T(8,128)(2,1)} %param.1), channel_id=1, source_target_pairs={{1,2},{2,1},{5,6},{6,5},{9,10},{10,9},{13,14},{14,13},{17,18},{18,... | collective-permute-start | bytes 1474568 | tf_op jit(solution)/shard_map/ppermute | solution.py:32
  14.2 12.9 %collective-permute-start.4 = (bf16[640,384]{1,0:T(8,128)(2,1)S(1)}, bf16[640,384]{1,0:T(8,128)(2,1)S(1)}, u32[]{:S(2)}, u32[]{:S(2)}) collective-permute-start(bf16[640,384]{1,0:T(8,128)(2,1)S(1)} %collective-permute-done.3), channel_id=1, source_target_pairs={{0,1},{3,2},{4,5},{7,6},{8,9},{11,10},{12,13},{15,14},{16,17},{19,... | collective-permute-start | bytes 1474568 | tf_op jit(solution)/shard_map/ppermute | solution.py:40
  18.2 10.0 %collective-permute-start.2 = (bf16[640,384]{1,0:T(8,128)(2,1)S(1)}, bf16[640,384]{1,0:T(8,128)(2,1)S(1)}, u32[]{:S(2)}, u32[]{:S(2)}) collective-permute-start(bf16[640,384]{1,0:T(8,128)(2,1)S(1)} %collective-permute-done), channel_id=1, source_target_pairs={{1,2},{2,1},{5,6},{6,5},{9,10},{10,9},{13,14},{14,13},{17,18},{18,... | collective-permute-start | bytes 1474568 | tf_op jit(solution)/shard_map/ppermute | solution.py:33
  29.3 6.8 %collective-permute-start.5 = (f32[768]{0:T(1024)S(1)}, f32[768]{0:T(1024)S(1)}, u32[]{:S(2)}, u32[]{:S(2)}) collective-permute-start(f32[768]{0:T(1024)S(1)} %pad_maximum_fusion), channel_id=1, source_target_pairs={{4,0},{8,4},{12,8},{5,1},{9,5},{13,9},{6,2},{10,6},{14,10},{7,3},{... | collective-permute-start | bytes 9224 | tf_op jit(solution)/shard_map/ppermute | solution.py:47
  36.1 4.7 %collective-permute-start.6 = (f32[384]{0:T(512)S(1)}, f32[384]{0:T(512)S(1)}, u32[]{:S(2)}, u32[]{:S(2)}) collective-permute-start(f32[384]{0:T(512)S(1)} %slice_add_fusion), channel_id=1, source_target_pairs={{1,0},{2,3},{5,4},{6,7},{9,8},{10,11},{13,12},{14,15},{17,16},{18,... | collective-permute-start | bytes 4616 | tf_op jit(solution)/shard_map/ppermute | solution.py:50

commit v6 on v4

--- a/solution.py
+++ b/solution.py
@@ -35,12 +35,12 @@
 
     onward = [(g, g + 1) for g in range(lax.axis_size("genome") - 1)]
     backward = [(b, a) for a, b in onward]
-    prev = [lax.ppermute(r, "genome", onward) for r in (own, adopt)]
+    prev_own, prev_adopt = [lax.ppermute(r, "genome", onward) for r in (own, adopt)]
     width = own.shape[1]
-    sums = []
-    for rows in (jnp.concatenate([own, adopt], axis=1), jnp.concatenate(prev, axis=1)):
-        total = row_squares(rows, early, scaling) + row_squares(rows, far, scaling)
-        sums += [total[:width], total[width:]]
+    held = jnp.concatenate([own, adopt, prev_own], axis=1)
+    total = row_squares(held, early, scaling) + row_squares(held, far, scaling)
+    sums = [total[:width], total[width:2 * width], total[2 * width:]]
+    sums.append(row_squares(prev_adopt, early, scaling) + row_squares(prev_adopt, far, scaling))
     following = lax.ppermute(jnp.concatenate(sums[2:]), "genome", backward)
     at_hub = sums[0] + following[:width]
     adopted = sums[1] + following[width:]

time: 41.5 us -> 42.1 us (1.014)
  waiting for transfers between devices: 16.8 us -> 17.4 us
    ppermute x2, waiting for transfers between devices: 3.6 us -> 2.03 us  [hub_plan(): lax.ppermute(r, 'genome', onward)]
    ppermute x1, waiting for transfers between devices: 5.83 us -> 7.18 us  [hub_plan(): at_end = lax.ppermute(adopted, 'group', [(1, 0), (2, 3)])]
    ppermute x1, waiting for transfers between devices: 3.03 us -> 3.75 us  [hub_plan(): following = lax.ppermute(jnp.concatenate(sums[2:]), 'genome', backward)]
    unnamed x2 -> x3, local copies, waits for them, and re-layouts: 1.17 us -> 1.28 us
  transfers between devices with their start and end apart: 7 -> 7, of which waited for: 4 -> 4; matrix products, arithmetic and copies ran while one was open for 14% -> 12% of each run, Pallas kernels for 0% -> 0%
where the time goes in v6:
time: 42.1 us; the launch traced here: 41.8 us
  waiting for transfers between devices  17.4 us (41%)
  starting transfers between devices  17.1 us (41%)
  matrix products  5.06 us (12%)
  local copies, waits for them, and re-layouts  1.45 us (3%)
  other arithmetic  0.6 us (1%)
    ppermute x2, starting transfers between devices, hub_plan(): lax.ppermute(r, 'genome', onward)  8.51 us
    ppermute x1, waiting for transfers between devices, hub_plan(): at_end = lax.ppermute(adopted, 'group', [(1, 0), (2, 3)])  7.18 us
    dot_general x4, matrix products, row_squares(): lax.dot_general(rows, columns, (((0,), (0,)), ((), ())), preferred_elemen...  5.06 us
    ppermute x1, waiting for transfers between devices, hub_plan(): adopt = lax.ppermute(own, 'group', [(0, 1), (3, 2)])  4.4 us
    ppermute x1, starting transfers between devices, hub_plan(): adopt = lax.ppermute(own, 'group', [(0, 1), (3, 2)])  4.05 us
    ppermute x1, waiting for transfers between devices, hub_plan(): following = lax.ppermute(jnp.concatenate(sums[2:]), 'genome', backward)  3.75 us
    ppermute x2, waiting for transfers between devices, hub_plan(): lax.ppermute(r, 'genome', onward)  2.03 us
    ppermute x1, starting transfers between devices, hub_plan(): following = lax.ppermute(jnp.concatenate(sums[2:]), 'genome', backward)  1.92 us
  transfers between devices with their start and end apart: 7, of which 4 were waited for; matrix products, arithmetic and copies ran while one was open for 12% of the time, Pallas kernels for 0%

profile of v6, /device:TPU:1, one launch (start us, length us, event | category | flops | bytes accessed | tf_op | source)
XLA Modules:
  0.0 41.8 jit_solution(2490565987819474442)
XLA Ops:
  0.0 4.0 %collective-permute-start = (bf16[640,384]{1,0:T(8,128)(2,1)}, bf16[640,384]{1,0:T(8,128)(2,1)S(1)}, u32[]{:S(2)}, u32[]{:S(2)}) collective-permute-start(bf16[640,384]{1,0:T(8,128)(2,1)} %param.1), channel_id=1, source_target_pairs={{0,1},{3,2},{4,5},{7,6},{8,9},{11,10},{12,13},{15,14},{16,17},{19,... | collective-permute-start | bytes 1474568 | tf_op jit(solution)/shard_map/ppermute | solution.py:31
  4.1 0.7 %collective-permute-start.2 = (bf16[640,384]{1,0:T(8,128)(2,1)}, bf16[640,384]{1,0:T(8,128)(2,1)S(1)}, u32[]{:S(2)}, u32[]{:S(2)}) collective-permute-start(bf16[640,384]{1,0:T(8,128)(2,1)} %param.1), channel_id=1, source_target_pairs={{1,2},{2,1},{5,6},{6,5},{9,10},{10,9},{13,14},{14,13},{17,18},{18,... | collective-permute-start | bytes 1474568 | tf_op jit(solution)/shard_map/ppermute | solution.py:32
  4.8 4.0 %collective-permute-start.1 = (bf16[640,384]{1,0:T(8,128)(2,1)}, bf16[640,384]{1,0:T(8,128)(2,1)S(1)}, u32[]{:S(2)}, u32[]{:S(2)}) collective-permute-start(bf16[640,384]{1,0:T(8,128)(2,1)} %param.1), channel_id=1, source_target_pairs={{0,4},{4,8},{8,12},{1,5},{5,9},{9,13},{2,6},{6,10},{10,14},{3,7},{... | collective-permute-start | bytes 1474568 | tf_op jit(solution)/shard_map/ppermute | solution.py:38
  8.7 1.1 %constant_dynamic-update-slice_fusion.2 = bf16[640,1152]{1,0:T(8,128)(2,1)S(1)} fusion(bf16[640,384]{1,0:T(8,128)(2,1)} %param.1), kind=kLoop, calls=%fused_computation.14 | loop fusion | bytes 983040
  9.8 4.4 %collective-permute-done = bf16[640,384]{1,0:T(8,128)(2,1)S(1)} collective-permute-done((bf16[640,384]{1,0:T(8,128)(2,1)}, bf16[640,384]{1,0:T(8,128)(2,1)S(1)}, u32[]{:S(2)}, u32[]{:S(2)}) %collective-permute-start) | collective-permute-done | bytes 491552 | tf_op jit(solution)/shard_map/ppermute | solution.py:31
  14.2 0.1 constant_dynamic-update-slice_fusion.1
  14.3 0.1 copy.6
  14.4 0.7 %collective-permute-start.3 = (bf16[640,384]{1,0:T(8,128)(2,1)S(1)}, bf16[640,384]{1,0:T(8,128)(2,1)S(1)}, u32[]{:S(2)}, u32[]{:S(2)}) collective-permute-start(bf16[640,384]{1,0:T(8,128)(2,1)S(1)} %collective-permute-done), channel_id=1, source_target_pairs={{1,2},{2,1},{5,6},{6,5},{9,10},{10,9},{13,14},{14,13},{17,18},{18,... | collective-permute-start | bytes 1474568 | tf_op jit(solution)/shard_map/ppermute | solution.py:33
  15.1 4.6 %collective-permute-start.4 = (bf16[640,384]{1,0:T(8,128)(2,1)S(1)}, bf16[640,384]{1,0:T(8,128)(2,1)S(1)}, u32[]{:S(2)}, u32[]{:S(2)}) collective-permute-start(bf16[640,384]{1,0:T(8,128)(2,1)S(1)} %collective-permute-done), channel_id=1, source_target_pairs={{0,4},{4,8},{8,12},{1,5},{5,9},{9,13},{2,6},{6,10},{10,14},{3,7},{... | collective-permute-start | bytes 1474568 | tf_op jit(solution)/shard_map/ppermute | solution.py:38
  19.7 0.0 collective-permute-done.2
  19.7 0.1 constant_dynamic-update-slice_fusion.3
  19.8 0.0 collective-permute-done.1
  19.8 0.1 constant_dynamic-update-slice_fusion
  19.9 2.5 %fusion.3 = f32[1152]{0:T(1024)S(1)} fusion(bf16[640,1152]{1,0:T(8,128)(2,1)S(1)} %constant_dynamic-update-slice_fusion, bf16[640,1152]{1,0:T(8,128)(2,1)S(1)} %constant_dynamic-update-slice_fusion.3), kind=kOutput, calls=%fused_computation.6 | convolution fusion | flops 1702673280 | bytes 2953728 | tf_op jit(solution)/shard_map/dot_general | solution.py:15
  22.4 0.0 collective-permute-done.3
  22.4 1.0 %fusion.4 = f32[1152]{0:T(1024)S(1)} fusion(bf16[640,1152]{1,0:T(8,128)(2,1)S(1)} %constant_dynamic-update-slice_fusion, bf16[640,384]{1,0:T(8,128)(2,1)S(1)} %collective-permute-done.3), kind=kOutput, calls=%fused_computation.7 | convolution fusion | flops 567556992 | bytes 1970688 | tf_op jit(solution)/shard_map/dot_general | solution.py:15
  23.4 2.0 %collective-permute-done.4 = bf16[640,384]{1,0:T(8,128)(2,1)S(1)} collective-permute-done((bf16[640,384]{1,0:T(8,128)(2,1)S(1)}, bf16[640,384]{1,0:T(8,128)(2,1)S(1)}, u32[]{:S(2)}, u32[]{:S(2)}) %collective-permute-start.4) | collective-permute-done | bytes 491552 | tf_op jit(solution)/shard_map/ppermute | solution.py:38
  25.4 1.1 %fusion.5 = f32[384]{0:T(512)S(1)} fusion(bf16[640,1152]{1,0:T(8,128)(2,1)S(1)} %constant_dynamic-update-slice_fusion.3, bf16[640,384]{1,0:T(8,128)(2,1)S(1)} %collective-permute-done.4), kind=kOutput, calls=%fused_computation.8 | convolution fusion | flops 567557760 | bytes 1967616 | tf_op jit(solution)/shard_map/dot_general | solution.py:15
  26.5 0.5 %fusion.7 = f32[384]{0:T(512)S(1)} fusion(bf16[640,384]{1,0:T(8,128)(2,1)S(1)} %collective-permute-done.4, bf16[640,384]{1,0:T(8,128)(2,1)S(1)} %collective-permute-done.3), kind=kOutput, calls=%fused_computation.11 | convolution fusion | flops 189185664 | bytes 984576 | tf_op jit(solution)/shard_map/dot_general | solution.py:15
  27.0 1.9 %collective-permute-start.5 = (f32[768]{0:T(1024)S(1)}, f32[768]{0:T(1024)S(1)}, u32[]{:S(2)}, u32[]{:S(2)}) collective-permute-start(f32[768]{0:T(1024)S(1)} %pad_maximum_fusion), channel_id=1, source_target_pairs={{4,0},{8,4},{12,8},{5,1},{9,5},{13,9},{6,2},{10,6},{14,10},{7,3},{... | collective-permute-start | bytes 9224 | tf_op jit(solution)/shard_map/ppermute | solution.py:44
  29.0 3.7 %collective-permute-done.5 = f32[768]{0:T(1024)S(1)} collective-permute-done((f32[768]{0:T(1024)S(1)}, f32[768]{0:T(1024)S(1)}, u32[]{:S(2)}, u32[]{:S(2)}) %collective-permute-start.5) | collective-permute-done | bytes 3104 | tf_op jit(solution)/shard_map/ppermute | solution.py:44
  32.7 1.3 %collective-permute-start.6 = (f32[384]{0:T(512)S(1)}, f32[384]{0:T(512)S(1)}, u32[]{:S(2)}, u32[]{:S(2)}) collective-permute-start(f32[384]{0:T(512)S(1)} %slice_add_fusion), channel_id=1, source_target_pairs={{1,0},{2,3},{5,4},{6,7},{9,8},{10,11},{13,12},{14,15},{17,16},{18,... | collective-permute-start | bytes 4616 | tf_op jit(solution)/shard_map/ppermute | solution.py:47
  34.0 7.2 %collective-permute-done.6 = f32[384]{0:T(512)S(1)} collective-permute-done((f32[384]{0:T(512)S(1)}, f32[384]{0:T(512)S(1)}, u32[]{:S(2)}, u32[]{:S(2)}) %collective-permute-start.6) | collective-permute-done | bytes 1568 | tf_op jit(solution)/shard_map/ppermute | solution.py:47
  41.2 0.6 %fusion.8 = f32[384]{0:T(512)} fusion(f32[384]{0:T(512)S(1)} %collective-permute-done.6, f32[1152]{0:T(1024)S(1)} %add.12, f32[768]{0:T(1024)S(1)} %collective-permute-done.5, pred[]{:T(512)S(6)} %or.3), kind=kLoop, calls=%fused_computation.21 | loop fusion | flops 768 | bytes 6145 | tf_op jit(solution)/shard_map/jit(_where)/select_n | solution.py:49
  (5 shorter events, 0.0 us)
Async XLA Ops:
  0.0 14.2 %collective-permute-start = (bf16[640,384]{1,0:T(8,128)(2,1)}, bf16[640,384]{1,0:T(8,128)(2,1)S(1)}, u32[]{:S(2)}, u32[]{:S(2)}) collective-permute-start(bf16[640,384]{1,0:T(8,128)(2,1)} %param.1), channel_id=1, source_target_pairs={{0,1},{3,2},{4,5},{7,6},{8,9},{11,10},{12,13},{15,14},{16,17},{19,... | collective-permute-start | bytes 1474568 | tf_op jit(solution)/shard_map/ppermute | solution.py:31
  4.1 15.6 %collective-permute-start.2 = (bf16[640,384]{1,0:T(8,128)(2,1)}, bf16[640,384]{1,0:T(8,128)(2,1)S(1)}, u32[]{:S(2)}, u32[]{:S(2)}) collective-permute-start(bf16[640,384]{1,0:T(8,128)(2,1)} %param.1), channel_id=1, source_target_pairs={{1,2},{2,1},{5,6},{6,5},{9,10},{10,9},{13,14},{14,13},{17,18},{18,... | collective-permute-start | bytes 1474568 | tf_op jit(solution)/shard_map/ppermute | solution.py:32
  4.8 15.0 %collective-permute-start.1 = (bf16[640,384]{1,0:T(8,128)(2,1)}, bf16[640,384]{1,0:T(8,128)(2,1)S(1)}, u32[]{:S(2)}, u32[]{:S(2)}) collective-permute-start(bf16[640,384]{1,0:T(8,128)(2,1)} %param.1), channel_id=1, source_target_pairs={{0,4},{4,8},{8,12},{1,5},{5,9},{9,13},{2,6},{6,10},{10,14},{3,7},{... | collective-permute-start | bytes 1474568 | tf_op jit(solution)/shard_map/ppermute | solution.py:38
  14.4 8.0 %collective-permute-start.3 = (bf16[640,384]{1,0:T(8,128)(2,1)S(1)}, bf16[640,384]{1,0:T(8,128)(2,1)S(1)}, u32[]{:S(2)}, u32[]{:S(2)}) collective-permute-start(bf16[640,384]{1,0:T(8,128)(2,1)S(1)} %collective-permute-done), channel_id=1, source_target_pairs={{1,2},{2,1},{5,6},{6,5},{9,10},{10,9},{13,14},{14,13},{17,18},{18,... | collective-permute-start | bytes 1474568 | tf_op jit(solution)/shard_map/ppermute | solution.py:33
  15.1 10.3 %collective-permute-start.4 = (bf16[640,384]{1,0:T(8,128)(2,1)S(1)}, bf16[640,384]{1,0:T(8,128)(2,1)S(1)}, u32[]{:S(2)}, u32[]{:S(2)}) collective-permute-start(bf16[640,384]{1,0:T(8,128)(2,1)S(1)} %collective-permute-done), channel_id=1, source_target_pairs={{0,4},{4,8},{8,12},{1,5},{5,9},{9,13},{2,6},{6,10},{10,14},{3,7},{... | collective-permute-start | bytes 1474568 | tf_op jit(solution)/shard_map/ppermute | solution.py:38
  27.0 5.7 %collective-permute-start.5 = (f32[768]{0:T(1024)S(1)}, f32[768]{0:T(1024)S(1)}, u32[]{:S(2)}, u32[]{:S(2)}) collective-permute-start(f32[768]{0:T(1024)S(1)} %pad_maximum_fusion), channel_id=1, source_target_pairs={{4,0},{8,4},{12,8},{5,1},{9,5},{13,9},{6,2},{10,6},{14,10},{7,3},{... | collective-permute-start | bytes 9224 | tf_op jit(solution)/shard_map/ppermute | solution.py:44
  32.7 8.5 %collective-permute-start.6 = (f32[384]{0:T(512)S(1)}, f32[384]{0:T(512)S(1)}, u32[]{:S(2)}, u32[]{:S(2)}) collective-permute-start(f32[384]{0:T(512)S(1)} %slice_add_fusion), channel_id=1, source_target_pairs={{1,0},{2,3},{5,4},{6,7},{9,8},{10,11},{13,12},{14,15},{17,16},{18,... | collective-permute-start | bytes 4616 | tf_op jit(solution)/shard_map/ppermute | solution.py:47

commit v7 on v6

--- a/solution.py
+++ b/solution.py
@@ -28,9 +28,13 @@
 def hub_plan(genotypes):
     scaling = 1.0 / genotypes.shape[0]
     own = genotypes
-    adopt = lax.ppermute(own, "group", [(0, 1), (3, 2)])
+    cut = min(256, own.shape[1])
+    pieces = [own[:, :cut], own[:, cut:]] if cut < own.shape[1] else [own]
+    adopt_parts = [lax.ppermute(p, "group", [(0, 1), (3, 2)]) for p in pieces]
     nbr = lax.ppermute(own, "group", [(1, 2), (2, 1)])
-    far = lax.ppermute(adopt, "group", [(1, 2), (2, 1)])
+    far_parts = [lax.ppermute(p, "group", [(1, 2), (2, 1)]) for p in adopt_parts]
+    adopt = jnp.concatenate(adopt_parts, axis=1) if len(adopt_parts) > 1 else adopt_parts[0]
+    far = jnp.concatenate(far_parts, axis=1) if len(far_parts) > 1 else far_parts[0]
     early = jnp.concatenate([own, adopt, nbr], axis=1)
 
     onward = [(g, g + 1) for g in range(lax.axis_size("genome") - 1)]

time: 42.1 us -> 46.4 us (1.10)
  starting transfers between devices: 17.1 us -> 19.1 us
  local copies, waits for them, and re-layouts: 1.45 us -> 3.42 us
    ppermute x1, waiting for transfers between devices: 7.18 us -> 10.7 us  [hub_plan(): at_end = lax.ppermute(adopted, 'group', [(1, 0), (2, 3)])]
    ppermute x2 -> x4, waiting for transfers between devices: 4.4 us -> 1.85 us  [the longest x2 1.85 us: hub_plan(): adopt_parts = [lax.ppermute(p, 'group', [(0, 1), (3, 2)]) for p in pieces]]
    ppermute x2 -> x4, starting transfers between devices: 4.74 us -> 6.69 us  [the longest x2 5.35 us: hub_plan(): adopt_parts = [lax.ppermute(p, 'group', [(0, 1), (3, 2)]) for p in pieces]]
    slice x0 -> x2, local copies, waits for them, and re-layouts: none -> 1.92 us  [hub_plan(): pieces = [own[:, :cut], own[:, cut:]] if cut < own.shape[1] else [own]]
    ppermute x2, waiting for transfers between devices: 2.03 us -> 1.25 us  [hub_plan(): lax.ppermute(r, 'genome', onward)]
    unnamed x3 -> x5, local copies, waits for them, and re-layouts: 1.28 us -> 1.29 us
  transfers between devices with their start and end apart: 7 -> 9, of which waited for: 4 -> 4; matrix products, arithmetic and copies ran while one was open for 12% -> 13% of each run, Pallas kernels for 0% -> 0%
where the time goes in v7:
time: 46.4 us; the launch traced here: 46 us
  starting transfers between devices  19.1 us (41%)
  waiting for transfers between devices  17.5 us (38%)
  matrix products  5.05 us (11%)
  local copies, waits for them, and re-layouts  3.42 us (7%)
  other arithmetic  0.66 us (1%)
    ppermute x1, waiting for transfers between devices, hub_plan(): at_end = lax.ppermute(adopted, 'group', [(1, 0), (2, 3)])  10.7 us
    ppermute x2, starting transfers between devices, hub_plan(): lax.ppermute(r, 'genome', onward)  8.51 us
    ppermute x2, starting transfers between devices, hub_plan(): adopt_parts = [lax.ppermute(p, 'group', [(0, 1), (3, 2)]) for p in pieces]  5.35 us
    dot_general x4, matrix products, row_squares(): lax.dot_general(rows, columns, (((0,), (0,)), ((), ())), preferred_elemen...  5.05 us
    ppermute x1, waiting for transfers between devices, hub_plan(): following = lax.ppermute(jnp.concatenate(sums[2:]), 'genome', backward)  3.74 us
    slice x2, local copies, waits for them, and re-layouts, hub_plan(): pieces = [own[:, :cut], own[:, cut:]] if cut < own.shape[1] else [own]  1.92 us
    ppermute x1, starting transfers between devices, hub_plan(): following = lax.ppermute(jnp.concatenate(sums[2:]), 'genome', backward)  1.92 us
    ppermute x2, waiting for transfers between devices, hub_plan(): adopt_parts = [lax.ppermute(p, 'group', [(0, 1), (3, 2)]) for p in pieces]  1.85 us
  transfers between devices with their start and end apart: 9, of which 4 were waited for; matrix products, arithmetic and copies ran while one was open for 13% of the time, Pallas kernels for 0%

profile of v7, /device:TPU:1, one launch (start us, length us, event | category | flops | bytes accessed | tf_op | source)
XLA Modules:
  0.0 46.0 jit_solution(4238684302058729189)
XLA Ops:
  0.0 1.0 %slice.21 = bf16[640,256]{1,0:T(8,128)(2,1)S(1)} slice(bf16[640,384]{1,0:T(8,128)(2,1)} %param.1), slice={[0:640], [0:256]} | slice | bytes 655360 | tf_op jit(solution)/shard_map/slice | solution.py:32
  1.0 4.0 %collective-permute-start = (bf16[640,256]{1,0:T(8,128)(2,1)S(1)}, bf16[640,256]{1,0:T(8,128)(2,1)S(1)}, u32[]{:S(2)}, u32[]{:S(2)}) collective-permute-start(bf16[640,256]{1,0:T(8,128)(2,1)S(1)} %slice.21), channel_id=1, source_target_pairs={{0,1},{3,2},{4,5},{7,6},{8,9},{11,10},{12,13},{15,14},{16,17},{19,... | collective-permute-start | bytes 983048 | tf_op jit(solution)/shard_map/ppermute | solution.py:33
  5.1 0.9 %slice.22 = bf16[640,128]{1,0:T(8,128)(2,1)S(1)} slice(bf16[640,384]{1,0:T(8,128)(2,1)} %param.1), slice={[0:640], [256:384]} | slice | bytes 327680 | tf_op jit(solution)/shard_map/slice | solution.py:32
  6.0 1.3 %collective-permute-start.1 = (bf16[640,128]{1,0:T(8,128)(2,1)S(1)}, bf16[640,128]{1,0:T(8,128)(2,1)S(1)}, u32[]{:S(2)}, u32[]{:S(2)}) collective-permute-start(bf16[640,128]{1,0:T(8,128)(2,1)S(1)} %slice.22), channel_id=1, source_target_pairs={{0,1},{3,2},{4,5},{7,6},{8,9},{11,10},{12,13},{15,14},{16,17},{19,... | collective-permute-start | bytes 491528 | tf_op jit(solution)/shard_map/ppermute | solution.py:33
  7.3 0.7 %collective-permute-start.3 = (bf16[640,384]{1,0:T(8,128)(2,1)}, bf16[640,384]{1,0:T(8,128)(2,1)S(1)}, u32[]{:S(2)}, u32[]{:S(2)}) collective-permute-start(bf16[640,384]{1,0:T(8,128)(2,1)} %param.1), channel_id=1, source_target_pairs={{1,2},{2,1},{5,6},{6,5},{9,10},{10,9},{13,14},{14,13},{17,18},{18,... | collective-permute-start | bytes 1474568 | tf_op jit(solution)/shard_map/ppermute | solution.py:34
  8.0 4.0 %collective-permute-start.2 = (bf16[640,384]{1,0:T(8,128)(2,1)}, bf16[640,384]{1,0:T(8,128)(2,1)S(1)}, u32[]{:S(2)}, u32[]{:S(2)}) collective-permute-start(bf16[640,384]{1,0:T(8,128)(2,1)} %param.1), channel_id=1, source_target_pairs={{0,4},{4,8},{8,12},{1,5},{5,9},{9,13},{2,6},{6,10},{10,14},{3,7},{... | collective-permute-start | bytes 1474568 | tf_op jit(solution)/shard_map/ppermute | solution.py:42
  12.0 1.1 %constant_dynamic-update-slice_fusion.3 = bf16[640,1152]{1,0:T(8,128)(2,1)S(1)} fusion(bf16[640,384]{1,0:T(8,128)(2,1)} %param.1), kind=kLoop, calls=%fused_computation.16 | loop fusion | bytes 983040
  13.1 1.8 %collective-permute-done.1 = bf16[640,128]{1,0:T(8,128)(2,1)S(1)} collective-permute-done((bf16[640,128]{1,0:T(8,128)(2,1)S(1)}, bf16[640,128]{1,0:T(8,128)(2,1)S(1)}, u32[]{:S(2)}, u32[]{:S(2)}) %collective-permute-start.1) | collective-permute-done | bytes 163872 | tf_op jit(solution)/shard_map/ppermute | solution.py:33
  14.9 0.7 %collective-permute-start.5 = (bf16[640,128]{1,0:T(8,128)(2,1)S(1)}, bf16[640,128]{1,0:T(8,128)(2,1)S(1)}, u32[]{:S(2)}, u32[]{:S(2)}) collective-permute-start(bf16[640,128]{1,0:T(8,128)(2,1)S(1)} %collective-permute-done.1), channel_id=1, source_target_pairs={{1,2},{2,1},{5,6},{6,5},{9,10},{10,9},{13,14},{14,13},{17,18},{18,... | collective-permute-start | bytes 491528 | tf_op jit(solution)/shard_map/ppermute | solution.py:35
  15.6 0.0 collective-permute-done
  15.7 0.1 copy.5
  15.8 0.1 pad_maximum_fusion
  15.8 4.6 %collective-permute-start.6 = (bf16[640,384]{1,0:T(8,128)(2,1)S(1)}, bf16[640,384]{1,0:T(8,128)(2,1)S(1)}, u32[]{:S(2)}, u32[]{:S(2)}) collective-permute-start(bf16[640,384]{1,0:T(8,128)(2,1)S(1)} %pad_maximum_fusion), channel_id=1, source_target_pairs={{0,4},{4,8},{8,12},{1,5},{5,9},{9,13},{2,6},{6,10},{10,14},{3,7},{... | collective-permute-start | bytes 1474568 | tf_op jit(solution)/shard_map/ppermute | solution.py:42
  20.4 0.7 %collective-permute-start.4 = (bf16[640,256]{1,0:T(8,128)(2,1)S(1)}, bf16[640,256]{1,0:T(8,128)(2,1)S(1)}, u32[]{:S(2)}, u32[]{:S(2)}) collective-permute-start(bf16[640,256]{1,0:T(8,128)(2,1)S(1)} %collective-permute-done), channel_id=1, source_target_pairs={{1,2},{2,1},{5,6},{6,5},{9,10},{10,9},{13,14},{14,13},{17,18},{18,... | collective-permute-start | bytes 983048 | tf_op jit(solution)/shard_map/ppermute | solution.py:35
  21.1 0.0 collective-permute-done.3
  21.1 0.1 constant_dynamic-update-slice_fusion.4
  21.2 0.0 collective-permute-done.2
  21.2 0.1 constant_dynamic-update-slice_fusion
  21.3 2.5 %fusion.3 = f32[1152]{0:T(1024)S(1)} fusion(bf16[640,1152]{1,0:T(8,128)(2,1)S(1)} %constant_dynamic-update-slice_fusion, bf16[640,1152]{1,0:T(8,128)(2,1)S(1)} %constant_dynamic-update-slice_fusion.4), kind=kOutput, calls=%fused_computation.6 | convolution fusion | flops 1702673280 | bytes 2953728 | tf_op jit(solution)/shard_map/dot_general | solution.py:15
  23.8 0.0 collective-permute-done.4
  23.8 0.0 collective-permute-done.5
  23.9 1.0 %fusion.4 = f32[1152]{0:T(1024)S(1)} fusion(bf16[640,1152]{1,0:T(8,128)(2,1)S(1)} %constant_dynamic-update-slice_fusion, bf16[640,384]{1,0:T(8,128)(2,1)S(1)} %constant_dynamic-update-slice_fusion.8), kind=kOutput, calls=%fused_computation.7 | convolution fusion | flops 567556992 | bytes 1970688 | tf_op jit(solution)/shard_map/dot_general | solution.py:15
  24.9 1.2 %collective-permute-done.6 = bf16[640,384]{1,0:T(8,128)(2,1)S(1)} collective-permute-done((bf16[640,384]{1,0:T(8,128)(2,1)S(1)}, bf16[640,384]{1,0:T(8,128)(2,1)S(1)}, u32[]{:S(2)}, u32[]{:S(2)}) %collective-permute-start.6) | collective-permute-done | bytes 491552 | tf_op jit(solution)/shard_map/ppermute | solution.py:42
  26.2 1.0 %fusion.5 = f32[384]{0:T(512)S(1)} fusion(bf16[640,384]{1,0:T(8,128)(2,1)S(1)} %collective-permute-done.6, bf16[640,1152]{1,0:T(8,128)(2,1)S(1)} %constant_dynamic-update-slice_fusion.4), kind=kOutput, calls=%fused_computation.8 | convolution fusion | flops 567557760 | bytes 1967616 | tf_op jit(solution)/shard_map/dot_general | solution.py:15
  27.2 0.5 %fusion.7 = f32[384]{0:T(512)S(1)} fusion(bf16[640,384]{1,0:T(8,128)(2,1)S(1)} %collective-permute-done.6, bf16[640,384]{1,0:T(8,128)(2,1)S(1)} %constant_dynamic-update-slice_fusion.8), kind=kOutput, calls=%fused_computation.11 | convolution fusion | flops 189185664 | bytes 984576 | tf_op jit(solution)/shard_map/dot_general | solution.py:15
  27.8 1.9 %collective-permute-start.7 = (f32[768]{0:T(1024)S(1)}, f32[768]{0:T(1024)S(1)}, u32[]{:S(2)}, u32[]{:S(2)}) collective-permute-start(f32[768]{0:T(1024)S(1)} %pad_maximum_fusion.1), channel_id=1, source_target_pairs={{4,0},{8,4},{12,8},{5,1},{9,5},{13,9},{6,2},{10,6},{14,10},{7,3},{... | collective-permute-start | bytes 9224 | tf_op jit(solution)/shard_map/ppermute | solution.py:48
  29.7 3.7 %collective-permute-done.7 = f32[768]{0:T(1024)S(1)} collective-permute-done((f32[768]{0:T(1024)S(1)}, f32[768]{0:T(1024)S(1)}, u32[]{:S(2)}, u32[]{:S(2)}) %collective-permute-start.7) | collective-permute-done | bytes 3104 | tf_op jit(solution)/shard_map/ppermute | solution.py:48
  33.4 1.3 %collective-permute-start.8 = (f32[384]{0:T(512)S(1)}, f32[384]{0:T(512)S(1)}, u32[]{:S(2)}, u32[]{:S(2)}) collective-permute-start(f32[384]{0:T(512)S(1)} %slice_add_fusion), channel_id=1, source_target_pairs={{1,0},{2,3},{5,4},{6,7},{9,8},{10,11},{13,12},{14,15},{17,16},{18,... | collective-permute-start | bytes 4616 | tf_op jit(solution)/shard_map/ppermute | solution.py:51
  34.7 10.7 %collective-permute-done.8 = f32[384]{0:T(512)S(1)} collective-permute-done((f32[384]{0:T(512)S(1)}, f32[384]{0:T(512)S(1)}, u32[]{:S(2)}, u32[]{:S(2)}) %collective-permute-start.8) | collective-permute-done | bytes 1568 | tf_op jit(solution)/shard_map/ppermute | solution.py:51
  45.4 0.6 %fusion.8 = f32[384]{0:T(512)} fusion(f32[384]{0:T(512)S(1)} %collective-permute-done.8, f32[1152]{0:T(1024)S(1)} %add.12, f32[768]{0:T(1024)S(1)} %collective-permute-done.7, pred[]{:T(512)S(6)} %or.3), kind=kLoop, calls=%fused_computation.26 | loop fusion | flops 768 | bytes 6145 | tf_op jit(solution)/shard_map/jit(_where)/select_n | solution.py:53
  (9 shorter events, 0.2 us)
Async XLA Ops:
  1.0 14.6 %collective-permute-start = (bf16[640,256]{1,0:T(8,128)(2,1)S(1)}, bf16[640,256]{1,0:T(8,128)(2,1)S(1)}, u32[]{:S(2)}, u32[]{:S(2)}) collective-permute-start(bf16[640,256]{1,0:T(8,128)(2,1)S(1)} %slice.21), channel_id=1, source_target_pairs={{0,1},{3,2},{4,5},{7,6},{8,9},{11,10},{12,13},{15,14},{16,17},{19,... | collective-permute-start | bytes 983048 | tf_op jit(solution)/shard_map/ppermute | solution.py:33
  6.0 8.9 %collective-permute-start.1 = (bf16[640,128]{1,0:T(8,128)(2,1)S(1)}, bf16[640,128]{1,0:T(8,128)(2,1)S(1)}, u32[]{:S(2)}, u32[]{:S(2)}) collective-permute-start(bf16[640,128]{1,0:T(8,128)(2,1)S(1)} %slice.22), channel_id=1, source_target_pairs={{0,1},{3,2},{4,5},{7,6},{8,9},{11,10},{12,13},{15,14},{16,17},{19,... | collective-permute-start | bytes 491528 | tf_op jit(solution)/shard_map/ppermute | solution.py:33
  7.3 13.8 %collective-permute-start.3 = (bf16[640,384]{1,0:T(8,128)(2,1)}, bf16[640,384]{1,0:T(8,128)(2,1)S(1)}, u32[]{:S(2)}, u32[]{:S(2)}) collective-permute-start(bf16[640,384]{1,0:T(8,128)(2,1)} %param.1), channel_id=1, source_target_pairs={{1,2},{2,1},{5,6},{6,5},{9,10},{10,9},{13,14},{14,13},{17,18},{18,... | collective-permute-start | bytes 1474568 | tf_op jit(solution)/shard_map/ppermute | solution.py:34
  8.0 13.2 %collective-permute-start.2 = (bf16[640,384]{1,0:T(8,128)(2,1)}, bf16[640,384]{1,0:T(8,128)(2,1)S(1)}, u32[]{:S(2)}, u32[]{:S(2)}) collective-permute-start(bf16[640,384]{1,0:T(8,128)(2,1)} %param.1), channel_id=1, source_target_pairs={{0,4},{4,8},{8,12},{1,5},{5,9},{9,13},{2,6},{6,10},{10,14},{3,7},{... | collective-permute-start | bytes 1474568 | tf_op jit(solution)/shard_map/ppermute | solution.py:42
  14.9 8.9 %collective-permute-start.5 = (bf16[640,128]{1,0:T(8,128)(2,1)S(1)}, bf16[640,128]{1,0:T(8,128)(2,1)S(1)}, u32[]{:S(2)}, u32[]{:S(2)}) collective-permute-start(bf16[640,128]{1,0:T(8,128)(2,1)S(1)} %collective-permute-done.1), channel_id=1, source_target_pairs={{1,2},{2,1},{5,6},{6,5},{9,10},{10,9},{13,14},{14,13},{17,18},{18,... | collective-permute-start | bytes 491528 | tf_op jit(solution)/shard_map/ppermute | solution.py:35
  15.8 10.3 %collective-permute-start.6 = (bf16[640,384]{1,0:T(8,128)(2,1)S(1)}, bf16[640,384]{1,0:T(8,128)(2,1)S(1)}, u32[]{:S(2)}, u32[]{:S(2)}) collective-permute-start(bf16[640,384]{1,0:T(8,128)(2,1)S(1)} %pad_maximum_fusion), channel_id=1, source_target_pairs={{0,4},{4,8},{8,12},{1,5},{5,9},{9,13},{2,6},{6,10},{10,14},{3,7},{... | collective-permute-start | bytes 1474568 | tf_op jit(solution)/shard_map/ppermute | solution.py:42
  20.4 3.4 %collective-permute-start.4 = (bf16[640,256]{1,0:T(8,128)(2,1)S(1)}, bf16[640,256]{1,0:T(8,128)(2,1)S(1)}, u32[]{:S(2)}, u32[]{:S(2)}) collective-permute-start(bf16[640,256]{1,0:T(8,128)(2,1)S(1)} %collective-permute-done), channel_id=1, source_target_pairs={{1,2},{2,1},{5,6},{6,5},{9,10},{10,9},{13,14},{14,13},{17,18},{18,... | collective-permute-start | bytes 983048 | tf_op jit(solution)/shard_map/ppermute | solution.py:35
  27.8 5.7 %collective-permute-start.7 = (f32[768]{0:T(1024)S(1)}, f32[768]{0:T(1024)S(1)}, u32[]{:S(2)}, u32[]{:S(2)}) collective-permute-start(f32[768]{0:T(1024)S(1)} %pad_maximum_fusion.1), channel_id=1, source_target_pairs={{4,0},{8,4},{12,8},{5,1},{9,5},{13,9},{6,2},{10,6},{14,10},{7,3},{... | collective-permute-start | bytes 9224 | tf_op jit(solution)/shard_map/ppermute | solution.py:48
  33.4 12.0 %collective-permute-start.8 = (f32[384]{0:T(512)S(1)}, f32[384]{0:T(512)S(1)}, u32[]{:S(2)}, u32[]{:S(2)}) collective-permute-start(f32[384]{0:T(512)S(1)} %slice_add_fusion), channel_id=1, source_target_pairs={{1,0},{2,3},{5,4},{6,7},{9,8},{10,11},{13,12},{14,15},{17,16},{18,... | collective-permute-start | bytes 4616 | tf_op jit(solution)/shard_map/ppermute | solution.py:51

commit v8 on v4

--- a/solution.py
+++ b/solution.py
@@ -33,15 +33,17 @@
     far = lax.ppermute(adopt, "group", [(1, 2), (2, 1)])
     early = jnp.concatenate([own, adopt, nbr], axis=1)
 
-    onward = [(g, g + 1) for g in range(lax.axis_size("genome") - 1)]
+    both = ("genome", "group")
+    line = lax.axis_size("group")
+    onward = [(g * line + z, (g + 1) * line + z) for g in range(lax.axis_size("genome") - 1) for z in (1, 2)]
     backward = [(b, a) for a, b in onward]
-    prev = [lax.ppermute(r, "genome", onward) for r in (own, adopt)]
+    prev = [lax.ppermute(r, both, onward) for r in (own, adopt)]
     width = own.shape[1]
     sums = []
     for rows in (jnp.concatenate([own, adopt], axis=1), jnp.concatenate(prev, axis=1)):
         total = row_squares(rows, early, scaling) + row_squares(rows, far, scaling)
         sums += [total[:width], total[width:]]
-    following = lax.ppermute(jnp.concatenate(sums[2:]), "genome", backward)
+    following = lax.ppermute(jnp.concatenate(sums[2:]), both, backward)
     at_hub = sums[0] + following[:width]
     adopted = sums[1] + following[width:]
     at_end = lax.ppermute(adopted, "group", [(1, 0), (2, 3)])

time: 41.5 us -> 41.5 us (level)
  waiting for transfers between devices: 16.8 us -> 25.2 us
  starting transfers between devices: 17.1 us -> 8.76 us
    ppermute x1, waiting for transfers between devices: 5.83 us -> 17.5 us  [hub_plan(): at_end = lax.ppermute(adopted, 'group', [(1, 0), (2, 3)])]
    ppermute x3, starting transfers between devices: 10.4 us -> 2.05 us  [the longest x2 1.38 us: hub_plan(): prev = [lax.ppermute(r, both, onward) for r in (own, adopt)]]
    ppermute x3, waiting for transfers between devices: 6.63 us -> 0.01 us  [the longest x2 0.01 us: hub_plan(): prev = [lax.ppermute(r, both, onward) for r in (own, adopt)]]
    ppermute x1, waiting for transfers between devices: 4.37 us -> 7.64 us  [hub_plan(): adopt = lax.ppermute(own, 'group', [(0, 1), (3, 2)])]
  transfers between devices with their start and end apart: 7 -> 7, of which waited for: 4 -> 2; matrix products, arithmetic and copies ran while one was open for 14% -> 14% of each run, Pallas kernels for 0% -> 0%
where the time goes in v8:
time: 41.5 us; the launch traced here: 41.2 us
  waiting for transfers between devices  25.2 us (61%)
  starting transfers between devices  8.76 us (21%)
  matrix products  5.04 us (12%)
  local copies, waits for them, and re-layouts  1.48 us (4%)
  other arithmetic  0.6 us (1%)
    ppermute x1, waiting for transfers between devices, hub_plan(): at_end = lax.ppermute(adopted, 'group', [(1, 0), (2, 3)])  17.5 us
    ppermute x1, waiting for transfers between devices, hub_plan(): adopt = lax.ppermute(own, 'group', [(0, 1), (3, 2)])  7.64 us
    dot_general x4, matrix products, row_squares(): lax.dot_general(rows, columns, (((0,), (0,)), ((), ())), preferred_elemen...  5.04 us
    ppermute x1, starting transfers between devices, hub_plan(): adopt = lax.ppermute(own, 'group', [(0, 1), (3, 2)])  4.05 us
    ppermute x2, starting transfers between devices, hub_plan(): prev = [lax.ppermute(r, both, onward) for r in (own, adopt)]  1.38 us
    ppermute x1, starting transfers between devices, hub_plan(): at_end = lax.ppermute(adopted, 'group', [(1, 0), (2, 3)])  1.29 us
    unnamed x2, local copies, waits for them, and re-layouts  1.17 us
  transfers between devices with their start and end apart: 7, of which 2 were waited for; matrix products, arithmetic and copies ran while one was open for 14% of the time, Pallas kernels for 0%

profile of v8, /device:TPU:1, one launch (start us, length us, event | category | flops | bytes accessed | tf_op | source)
XLA Modules:
  0.0 41.2 jit_solution(13780140336077731509)
XLA Ops:
  0.0 4.0 %collective-permute-start = (bf16[640,384]{1,0:T(8,128)(2,1)}, bf16[640,384]{1,0:T(8,128)(2,1)S(1)}, u32[]{:S(2)}, u32[]{:S(2)}) collective-permute-start(bf16[640,384]{1,0:T(8,128)(2,1)} %param.1), channel_id=1, source_target_pairs={{0,1},{3,2},{4,5},{7,6},{8,9},{11,10},{12,13},{15,14},{16,17},{19,... | collective-permute-start | bytes 1474568 | tf_op jit(solution)/shard_map/ppermute | solution.py:31
  4.1 0.7 %collective-permute-start.3 = (bf16[640,384]{1,0:T(8,128)(2,1)}, bf16[640,384]{1,0:T(8,128)(2,1)S(1)}, u32[]{:S(2)}, u32[]{:S(2)}) collective-permute-start(bf16[640,384]{1,0:T(8,128)(2,1)} %param.1), channel_id=1, source_target_pairs={{1,5},{2,6},{5,9},{6,10},{9,13},{10,14},{17,21},{18,22},{21,25},{2... | collective-permute-start | bytes 1474568 | tf_op jit(solution)/shard_map/ppermute | solution.py:40
  4.8 0.7 %collective-permute-start.1 = (bf16[640,384]{1,0:T(8,128)(2,1)}, bf16[640,384]{1,0:T(8,128)(2,1)S(1)}, u32[]{:S(2)}, u32[]{:S(2)}) collective-permute-start(bf16[640,384]{1,0:T(8,128)(2,1)} %param.1), channel_id=1, source_target_pairs={{1,2},{2,1},{5,6},{6,5},{9,10},{10,9},{13,14},{14,13},{17,18},{18,... | collective-permute-start | bytes 1474568 | tf_op jit(solution)/shard_map/ppermute | solution.py:32
  5.5 1.1 %constant_dynamic-update-slice_fusion.1 = (bf16[640,768]{1,0:T(8,128)(2,1)S(1)}, bf16[640,1152]{1,0:T(8,128)(2,1)S(1)}) fusion(bf16[640,384]{1,0:T(8,128)(2,1)} %param.1), kind=kLoop, calls=%fused_computation.13 | loop fusion | bytes 1474560
  6.6 7.6 %collective-permute-done = bf16[640,384]{1,0:T(8,128)(2,1)S(1)} collective-permute-done((bf16[640,384]{1,0:T(8,128)(2,1)}, bf16[640,384]{1,0:T(8,128)(2,1)S(1)}, u32[]{:S(2)}, u32[]{:S(2)}) %collective-permute-start) | collective-permute-done | bytes 491552 | tf_op jit(solution)/shard_map/ppermute | solution.py:31
  14.2 0.7 %collective-permute-start.2 = (bf16[640,384]{1,0:T(8,128)(2,1)S(1)}, bf16[640,384]{1,0:T(8,128)(2,1)S(1)}, u32[]{:S(2)}, u32[]{:S(2)}) collective-permute-start(bf16[640,384]{1,0:T(8,128)(2,1)S(1)} %collective-permute-done), channel_id=1, source_target_pairs={{1,2},{2,1},{5,6},{6,5},{9,10},{10,9},{13,14},{14,13},{17,18},{18,... | collective-permute-start | bytes 1474568 | tf_op jit(solution)/shard_map/ppermute | solution.py:33
  14.9 0.7 %collective-permute-start.4 = (bf16[640,384]{1,0:T(8,128)(2,1)S(1)}, bf16[640,384]{1,0:T(8,128)(2,1)S(1)}, u32[]{:S(2)}, u32[]{:S(2)}) collective-permute-start(bf16[640,384]{1,0:T(8,128)(2,1)S(1)} %collective-permute-done), channel_id=1, source_target_pairs={{1,5},{2,6},{5,9},{6,10},{9,13},{10,14},{17,21},{18,22},{21,25},{2... | collective-permute-start | bytes 1474568 | tf_op jit(solution)/shard_map/ppermute | solution.py:40
  15.6 0.0 collective-permute-done.3
  15.6 0.1 constant_dynamic-update-slice_fusion.6
  15.7 0.2 constant_dynamic-update-slice_fusion
  15.8 0.0 collective-permute-done.1
  15.8 0.1 constant_dynamic-update-slice_fusion.2
  15.9 1.8 %fusion.2 = f32[768]{0:T(1024)S(1)} fusion(bf16[640,768]{1,0:T(8,128)(2,1)S(1)} %get-tuple-element.5, bf16[640,1152]{1,0:T(8,128)(2,1)S(1)} %constant_dynamic-update-slice_fusion.2), kind=kOutput, calls=%fused_computation.4 | convolution fusion | flops 1135115520 | bytes 2460672 | tf_op jit(solution)/shard_map/dot_general | solution.py:15
  17.8 0.0 collective-permute-done.4
  17.8 0.1 constant_dynamic-update-slice_fusion.5
  17.8 1.8 %fusion.3 = f32[768]{0:T(1024)S(1)} fusion(bf16[640,768]{1,0:T(8,128)(2,1)S(1)} %constant_dynamic-update-slice_fusion.5, bf16[640,1152]{1,0:T(8,128)(2,1)S(1)} %constant_dynamic-update-slice_fusion.2), kind=kOutput, calls=%fused_computation.5 | convolution fusion | flops 1135115520 | bytes 2460672 | tf_op jit(solution)/shard_map/dot_general | solution.py:15
  19.7 0.0 collective-permute-done.2
  19.7 0.7 %fusion.7 = f32[768]{0:T(1024)S(1)} fusion(bf16[640,768]{1,0:T(8,128)(2,1)S(1)} %constant_dynamic-update-slice_fusion.5, bf16[640,384]{1,0:T(8,128)(2,1)S(1)} %collective-permute-done.2), kind=kOutput, calls=%fused_computation.11 | convolution fusion | flops 378371328 | bytes 1477632 | tf_op jit(solution)/shard_map/dot_general | solution.py:15
  20.4 0.7 %collective-permute-start.5 = (f32[768]{0:T(1024)S(1)}, f32[768]{0:T(1024)S(1)}, u32[]{:S(2)}, u32[]{:S(2)}) collective-permute-start(f32[768]{0:T(1024)S(1)} %add.13), channel_id=1, source_target_pairs={{5,1},{6,2},{9,5},{10,6},{13,9},{14,10},{21,17},{22,18},{25,21},{2... | collective-permute-start | bytes 9224 | tf_op jit(solution)/shard_map/ppermute | solution.py:46
  21.1 0.7 %fusion.6 = f32[768]{0:T(1024)S(1)} fusion(bf16[640,768]{1,0:T(8,128)(2,1)S(1)} %get-tuple-element.5, bf16[640,384]{1,0:T(8,128)(2,1)S(1)} %collective-permute-done.2), kind=kOutput, calls=%fused_computation.10 | convolution fusion | flops 378371328 | bytes 1477632 | tf_op jit(solution)/shard_map/dot_general | solution.py:15
  21.8 0.0 collective-permute-done.5
  21.8 1.3 %collective-permute-start.6 = (f32[384]{0:T(512)S(1)}, f32[384]{0:T(512)S(1)}, u32[]{:S(2)}, u32[]{:S(2)}) collective-permute-start(f32[384]{0:T(512)S(1)} %slice_add_fusion), channel_id=1, source_target_pairs={{1,0},{2,3},{5,4},{6,7},{9,8},{10,11},{13,12},{14,15},{17,16},{18,... | collective-permute-start | bytes 4616 | tf_op jit(solution)/shard_map/ppermute | solution.py:49
  23.1 17.5 %collective-permute-done.6 = f32[384]{0:T(512)S(1)} collective-permute-done((f32[384]{0:T(512)S(1)}, f32[384]{0:T(512)S(1)}, u32[]{:S(2)}, u32[]{:S(2)}) %collective-permute-start.6) | collective-permute-done | bytes 1568 | tf_op jit(solution)/shard_map/ppermute | solution.py:49
  40.6 0.6 %add_select_fusion = f32[384]{0:T(512)} fusion(f32[384]{0:T(512)S(1)} %collective-permute-done.6, f32[768]{0:T(1024)S(1)} %collective-permute-done.5, f32[768]{0:T(1024)S(1)} %add.12, pred[]{:T(512)S(6)} %or.3), kind=kLoop, calls=%fused_computation.20 | loop fusion | flops 768 | bytes 6145 | tf_op jit(solution)/shard_map/jit(_where)/select_n | solution.py:51
  (3 shorter events, 0.0 us)
Async XLA Ops:
  0.0 14.2 %collective-permute-start = (bf16[640,384]{1,0:T(8,128)(2,1)}, bf16[640,384]{1,0:T(8,128)(2,1)S(1)}, u32[]{:S(2)}, u32[]{:S(2)}) collective-permute-start(bf16[640,384]{1,0:T(8,128)(2,1)} %param.1), channel_id=1, source_target_pairs={{0,1},{3,2},{4,5},{7,6},{8,9},{11,10},{12,13},{15,14},{16,17},{19,... | collective-permute-start | bytes 1474568 | tf_op jit(solution)/shard_map/ppermute | solution.py:31
  4.1 11.5 %collective-permute-start.3 = (bf16[640,384]{1,0:T(8,128)(2,1)}, bf16[640,384]{1,0:T(8,128)(2,1)S(1)}, u32[]{:S(2)}, u32[]{:S(2)}) collective-permute-start(bf16[640,384]{1,0:T(8,128)(2,1)} %param.1), channel_id=1, source_target_pairs={{1,5},{2,6},{5,9},{6,10},{9,13},{10,14},{17,21},{18,22},{21,25},{2... | collective-permute-start | bytes 1474568 | tf_op jit(solution)/shard_map/ppermute | solution.py:40
  4.8 11.1 %collective-permute-start.1 = (bf16[640,384]{1,0:T(8,128)(2,1)}, bf16[640,384]{1,0:T(8,128)(2,1)S(1)}, u32[]{:S(2)}, u32[]{:S(2)}) collective-permute-start(bf16[640,384]{1,0:T(8,128)(2,1)} %param.1), channel_id=1, source_target_pairs={{1,2},{2,1},{5,6},{6,5},{9,10},{10,9},{13,14},{14,13},{17,18},{18,... | collective-permute-start | bytes 1474568 | tf_op jit(solution)/shard_map/ppermute | solution.py:32
  14.2 5.5 %collective-permute-start.2 = (bf16[640,384]{1,0:T(8,128)(2,1)S(1)}, bf16[640,384]{1,0:T(8,128)(2,1)S(1)}, u32[]{:S(2)}, u32[]{:S(2)}) collective-permute-start(bf16[640,384]{1,0:T(8,128)(2,1)S(1)} %collective-permute-done), channel_id=1, source_target_pairs={{1,2},{2,1},{5,6},{6,5},{9,10},{10,9},{13,14},{14,13},{17,18},{18,... | collective-permute-start | bytes 1474568 | tf_op jit(solution)/shard_map/ppermute | solution.py:33
  14.9 2.9 %collective-permute-start.4 = (bf16[640,384]{1,0:T(8,128)(2,1)S(1)}, bf16[640,384]{1,0:T(8,128)(2,1)S(1)}, u32[]{:S(2)}, u32[]{:S(2)}) collective-permute-start(bf16[640,384]{1,0:T(8,128)(2,1)S(1)} %collective-permute-done), channel_id=1, source_target_pairs={{1,5},{2,6},{5,9},{6,10},{9,13},{10,14},{17,21},{18,22},{21,25},{2... | collective-permute-start | bytes 1474568 | tf_op jit(solution)/shard_map/ppermute | solution.py:40
  20.4 1.4 %collective-permute-start.5 = (f32[768]{0:T(1024)S(1)}, f32[768]{0:T(1024)S(1)}, u32[]{:S(2)}, u32[]{:S(2)}) collective-permute-start(f32[768]{0:T(1024)S(1)} %add.13), channel_id=1, source_target_pairs={{5,1},{6,2},{9,5},{10,6},{13,9},{14,10},{21,17},{22,18},{25,21},{2... | collective-permute-start | bytes 9224 | tf_op jit(solution)/shard_map/ppermute | solution.py:46
  21.8 18.8 %collective-permute-start.6 = (f32[384]{0:T(512)S(1)}, f32[384]{0:T(512)S(1)}, u32[]{:S(2)}, u32[]{:S(2)}) collective-permute-start(f32[384]{0:T(512)S(1)} %slice_add_fusion), channel_id=1, source_target_pairs={{1,0},{2,3},{5,4},{6,7},{9,8},{10,11},{13,12},{14,15},{17,16},{18,... | collective-permute-start | bytes 4616 | tf_op jit(solution)/shard_map/ppermute | solution.py:49

commit v9 on v8

--- a/solution.py
+++ b/solution.py
@@ -30,14 +30,24 @@
     own = genotypes
     adopt = lax.ppermute(own, "group", [(0, 1), (3, 2)])
     nbr = lax.ppermute(own, "group", [(1, 2), (2, 1)])
-    far = lax.ppermute(adopt, "group", [(1, 2), (2, 1)])
-    early = jnp.concatenate([own, adopt, nbr], axis=1)
 
     both = ("genome", "group")
     line = lax.axis_size("group")
-    onward = [(g * line + z, (g + 1) * line + z) for g in range(lax.axis_size("genome") - 1) for z in (1, 2)]
+    steps = range(lax.axis_size("genome") - 1)
+    crossing = [g for g in steps if g % 2 == 1]
+    hubs = (1, 2)
+    onward = [(g * line + z, (g + 1) * line + z) for g in steps for z in hubs]
     backward = [(b, a) for a, b in onward]
-    prev = [lax.ppermute(r, both, onward) for r in (own, adopt)]
+    ends_across = [(g * line + z, (g + 1) * line + z) for g in crossing for z in (0, line - 1)]
+    prev_own = lax.ppermute(own, both, onward + ends_across)
+    on_chip = [(g * line + z, (g + 1) * line + z) for g in steps if g % 2 == 0 for z in hubs]
+    relay, adopted_here = lax.optimization_barrier((prev_own, adopt))
+    far = lax.ppermute(adopted_here, "group", [(1, 2), (2, 1)])
+    early = jnp.concatenate([own, adopt, nbr], axis=1)
+    relayed = [((g + 1) * line, (g + 1) * line + 1) for g in crossing]
+    relayed += [((g + 1) * line + line - 1, (g + 1) * line + line - 2) for g in crossing]
+    prev_adopt = lax.ppermute(adopt, both, on_chip) + lax.ppermute(relay, both, relayed)
+    prev = [prev_own, prev_adopt]
     width = own.shape[1]
     sums = []
     for rows in (jnp.concatenate([own, adopt], axis=1), jnp.concatenate(prev, axis=1)):

time: 41.5 us -> 40.7 us (0.981)
  waiting for transfers between devices: 25.2 us -> 20.3 us
  starting transfers between devices: 8.76 us -> 12.7 us
    ppermute x3 -> x4, starting transfers between devices: 2.06 us -> 6.05 us  [the longest x1 3.99 us: hub_plan(): prev_own = lax.ppermute(own, both, onward + ends_across)]
    ppermute x1, waiting for transfers between devices: 7.64 us -> 4.34 us  [hub_plan(): adopt = lax.ppermute(own, 'group', [(0, 1), (3, 2)])]
    ppermute x1, waiting for transfers between devices: 17.5 us -> 16 us  [hub_plan(): at_end = lax.ppermute(adopted, 'group', [(1, 0), (2, 3)])]
    unnamed x2 -> x1, local copies, waits for them, and re-layouts: 1.17 us -> 1.12 us
  transfers between devices with their start and end apart: 7 -> 8, of which waited for: 2 -> 2; matrix products, arithmetic and copies ran while one was open for 14% -> 14% of each run, Pallas kernels for 0% -> 0%
where the time goes in v9:
time: 40.7 us; the launch traced here: 40.4 us
  waiting for transfers between devices  20.3 us (50%)
  starting transfers between devices  12.7 us (31%)
  matrix products  5.06 us (12%)
  local copies, waits for them, and re-layouts  1.35 us (3%)
  other arithmetic  0.73 us (2%)
    ppermute x1, waiting for transfers between devices, hub_plan(): at_end = lax.ppermute(adopted, 'group', [(1, 0), (2, 3)])  16 us
    dot_general x4, matrix products, row_squares(): lax.dot_general(rows, columns, (((0,), (0,)), ((), ())), preferred_elemen...  5.06 us
    ppermute x1, waiting for transfers between devices, hub_plan(): adopt = lax.ppermute(own, 'group', [(0, 1), (3, 2)])  4.34 us
    ppermute x1, starting transfers between devices, hub_plan(): adopt = lax.ppermute(own, 'group', [(0, 1), (3, 2)])  4.05 us
    ppermute x1, starting transfers between devices, hub_plan(): prev_own = lax.ppermute(own, both, onward + ends_across)  3.99 us
    ppermute x1, starting transfers between devices, hub_plan(): at_end = lax.ppermute(adopted, 'group', [(1, 0), (2, 3)])  1.29 us
    unnamed x1, local copies, waits for them, and re-layouts  1.12 us
  transfers between devices with their start and end apart: 8, of which 2 were waited for; matrix products, arithmetic and copies ran while one was open for 14% of the time, Pallas kernels for 0%

profile of v9, /device:TPU:1, one launch (start us, length us, event | category | flops | bytes accessed | tf_op | source)
XLA Modules:
  0.0 40.4 jit_solution(6898537619739683049)
XLA Ops:
  0.0 4.0 %collective-permute-start = (bf16[640,384]{1,0:T(8,128)(2,1)}, bf16[640,384]{1,0:T(8,128)(2,1)S(1)}, u32[]{:S(2)}, u32[]{:S(2)}) collective-permute-start(bf16[640,384]{1,0:T(8,128)(2,1)} %param.1), channel_id=1, source_target_pairs={{0,1},{3,2},{4,5},{7,6},{8,9},{11,10},{12,13},{15,14},{16,17},{19,... | collective-permute-start | bytes 1474568 | tf_op jit(solution)/shard_map/ppermute | solution.py:31
  4.1 4.0 %collective-permute-start.2 = (bf16[640,384]{1,0:T(8,128)(2,1)}, bf16[640,384]{1,0:T(8,128)(2,1)S(1)}, u32[]{:S(2)}, u32[]{:S(2)}) collective-permute-start(bf16[640,384]{1,0:T(8,128)(2,1)} %param.1), channel_id=1, source_target_pairs={{1,5},{2,6},{5,9},{6,10},{9,13},{10,14},{4,8},{7,11},{17,21},{18,2... | collective-permute-start | bytes 1474568 | tf_op jit(solution)/shard_map/ppermute | solution.py:42
  8.1 0.7 %collective-permute-start.1 = (bf16[640,384]{1,0:T(8,128)(2,1)}, bf16[640,384]{1,0:T(8,128)(2,1)S(1)}, u32[]{:S(2)}, u32[]{:S(2)}) collective-permute-start(bf16[640,384]{1,0:T(8,128)(2,1)} %param.1), channel_id=1, source_target_pairs={{1,2},{2,1},{5,6},{6,5},{9,10},{10,9},{13,14},{14,13},{17,18},{18,... | collective-permute-start | bytes 1474568 | tf_op jit(solution)/shard_map/ppermute | solution.py:32
  8.8 1.1 %constant_dynamic-update-slice_fusion.1 = (bf16[640,768]{1,0:T(8,128)(2,1)S(1)}, bf16[640,1152]{1,0:T(8,128)(2,1)S(1)}) fusion(bf16[640,384]{1,0:T(8,128)(2,1)} %param.1), kind=kLoop, calls=%fused_computation.14 | loop fusion | bytes 1474560
  9.9 4.3 %collective-permute-done = bf16[640,384]{1,0:T(8,128)(2,1)S(1)} collective-permute-done((bf16[640,384]{1,0:T(8,128)(2,1)}, bf16[640,384]{1,0:T(8,128)(2,1)S(1)}, u32[]{:S(2)}, u32[]{:S(2)}) %collective-permute-start) | collective-permute-done | bytes 491552 | tf_op jit(solution)/shard_map/ppermute | solution.py:31
  14.2 0.0 collective-permute-done.2
  14.2 0.7 %collective-permute-start.5 = (bf16[640,384]{1,0:T(8,128)(2,1)S(1)}, bf16[640,384]{1,0:T(8,128)(2,1)S(1)}, u32[]{:S(2)}, u32[]{:S(2)}) collective-permute-start(bf16[640,384]{1,0:T(8,128)(2,1)S(1)} %collective-permute-done.2), channel_id=1, source_target_pairs={{8,9},{11,10},{24,25},{27,26}} | collective-permute-start | bytes 1474568 | tf_op jit(solution)/shard_map/ppermute | solution.py:49
  14.9 0.7 %collective-permute-start.3 = (bf16[640,384]{1,0:T(8,128)(2,1)S(1)}, bf16[640,384]{1,0:T(8,128)(2,1)S(1)}, u32[]{:S(2)}, u32[]{:S(2)}) collective-permute-start(bf16[640,384]{1,0:T(8,128)(2,1)S(1)} %collective-permute-done), channel_id=1, source_target_pairs={{1,2},{2,1},{5,6},{6,5},{9,10},{10,9},{13,14},{14,13},{17,18},{18,... | collective-permute-start | bytes 1474568 | tf_op jit(solution)/shard_map/ppermute | solution.py:45
  15.6 0.7 %collective-permute-start.4 = (bf16[640,384]{1,0:T(8,128)(2,1)S(1)}, bf16[640,384]{1,0:T(8,128)(2,1)S(1)}, u32[]{:S(2)}, u32[]{:S(2)}) collective-permute-start(bf16[640,384]{1,0:T(8,128)(2,1)S(1)} %collective-permute-done), channel_id=1, source_target_pairs={{1,5},{2,6},{9,13},{10,14},{17,21},{18,22},{25,29},{26,30}} | collective-permute-start | bytes 1474568 | tf_op jit(solution)/shard_map/ppermute | solution.py:49
  16.3 0.2 constant_dynamic-update-slice_fusion
  16.5 0.0 collective-permute-done.1
  16.5 0.1 constant_dynamic-update-slice_fusion.2
  16.6 1.8 %fusion.2 = f32[768]{0:T(1024)S(1)} fusion(bf16[640,768]{1,0:T(8,128)(2,1)S(1)} %get-tuple-element.9, bf16[640,1152]{1,0:T(8,128)(2,1)S(1)} %constant_dynamic-update-slice_fusion.2), kind=kOutput, calls=%fused_computation.4 | convolution fusion | flops 1135115520 | bytes 2460672 | tf_op jit(solution)/shard_map/dot_general | solution.py:15
  18.4 0.0 collective-permute-done.4
  18.4 0.0 collective-permute-done.5
  18.4 0.1 add.16
  18.5 1.8 %fusion.3 = f32[768]{0:T(1024)S(1)} fusion(bf16[640,1152]{1,0:T(8,128)(2,1)S(1)} %constant_dynamic-update-slice_fusion.2, bf16[640,384]{1,0:T(8,128)(2,1)S(1)} %add.16, bf16[640,384]{1,0:T(8,128)(2,1)S(1)} %collective-permute-done.2), kind=kOutput, calls=%fused_computation.5 | convolution fusion | flops 1137081600 | bytes 2460672 | tf_op jit(solution)/shard_map/dot_general | solution.py:15
  20.4 0.0 collective-permute-done.3
  20.4 0.7 %fusion.7 = f32[768]{0:T(1024)S(1)} fusion(bf16[640,384]{1,0:T(8,128)(2,1)S(1)} %collective-permute-done.3, bf16[640,384]{1,0:T(8,128)(2,1)S(1)} %add.16, bf16[640,384]{1,0:T(8,128)(2,1)S(1)} %collective-permute-done.2), kind=kOutput, calls=%fused_computation.11 | convolution fusion | flops 380337408 | bytes 1477632 | tf_op jit(solution)/shard_map/dot_general | solution.py:15
  21.1 0.7 %collective-permute-start.6 = (f32[768]{0:T(1024)S(1)}, f32[768]{0:T(1024)S(1)}, u32[]{:S(2)}, u32[]{:S(2)}) collective-permute-start(f32[768]{0:T(1024)S(1)} %add.17), channel_id=1, source_target_pairs={{5,1},{6,2},{9,5},{10,6},{13,9},{14,10},{21,17},{22,18},{25,21},{2... | collective-permute-start | bytes 9224 | tf_op jit(solution)/shard_map/ppermute | solution.py:56
  21.8 0.7 %fusion.6 = f32[768]{0:T(1024)S(1)} fusion(bf16[640,768]{1,0:T(8,128)(2,1)S(1)} %get-tuple-element.9, bf16[640,384]{1,0:T(8,128)(2,1)S(1)} %collective-permute-done.3), kind=kOutput, calls=%fused_computation.10 | convolution fusion | flops 378371328 | bytes 1477632 | tf_op jit(solution)/shard_map/dot_general | solution.py:15
  22.5 0.0 collective-permute-done.6
  22.5 1.3 %collective-permute-start.7 = (f32[384]{0:T(512)S(1)}, f32[384]{0:T(512)S(1)}, u32[]{:S(2)}, u32[]{:S(2)}) collective-permute-start(f32[384]{0:T(512)S(1)} %slice_add_fusion), channel_id=1, source_target_pairs={{1,0},{2,3},{5,4},{6,7},{9,8},{10,11},{13,12},{14,15},{17,16},{18,... | collective-permute-start | bytes 4616 | tf_op jit(solution)/shard_map/ppermute | solution.py:59
  23.8 16.0 %collective-permute-done.7 = f32[384]{0:T(512)S(1)} collective-permute-done((f32[384]{0:T(512)S(1)}, f32[384]{0:T(512)S(1)}, u32[]{:S(2)}, u32[]{:S(2)}) %collective-permute-start.7) | collective-permute-done | bytes 1568 | tf_op jit(solution)/shard_map/ppermute | solution.py:59
  39.8 0.6 %add_select_fusion = f32[384]{0:T(512)} fusion(f32[384]{0:T(512)S(1)} %collective-permute-done.7, f32[768]{0:T(1024)S(1)} %collective-permute-done.6, f32[768]{0:T(1024)S(1)} %add.15, pred[]{:T(512)S(6)} %or.3), kind=kLoop, calls=%fused_computation.19 | loop fusion | flops 768 | bytes 6145 | tf_op jit(solution)/shard_map/jit(_where)/select_n | solution.py:61
  (3 shorter events, 0.0 us)
Async XLA Ops:
  0.0 14.2 %collective-permute-start = (bf16[640,384]{1,0:T(8,128)(2,1)}, bf16[640,384]{1,0:T(8,128)(2,1)S(1)}, u32[]{:S(2)}, u32[]{:S(2)}) collective-permute-start(bf16[640,384]{1,0:T(8,128)(2,1)} %param.1), channel_id=1, source_target_pairs={{0,1},{3,2},{4,5},{7,6},{8,9},{11,10},{12,13},{15,14},{16,17},{19,... | collective-permute-start | bytes 1474568 | tf_op jit(solution)/shard_map/ppermute | solution.py:31
  4.1 10.2 %collective-permute-start.2 = (bf16[640,384]{1,0:T(8,128)(2,1)}, bf16[640,384]{1,0:T(8,128)(2,1)S(1)}, u32[]{:S(2)}, u32[]{:S(2)}) collective-permute-start(bf16[640,384]{1,0:T(8,128)(2,1)} %param.1), channel_id=1, source_target_pairs={{1,5},{2,6},{5,9},{6,10},{9,13},{10,14},{4,8},{7,11},{17,21},{18,2... | collective-permute-start | bytes 1474568 | tf_op jit(solution)/shard_map/ppermute | solution.py:42
  8.1 8.4 %collective-permute-start.1 = (bf16[640,384]{1,0:T(8,128)(2,1)}, bf16[640,384]{1,0:T(8,128)(2,1)S(1)}, u32[]{:S(2)}, u32[]{:S(2)}) collective-permute-start(bf16[640,384]{1,0:T(8,128)(2,1)} %param.1), channel_id=1, source_target_pairs={{1,2},{2,1},{5,6},{6,5},{9,10},{10,9},{13,14},{14,13},{17,18},{18,... | collective-permute-start | bytes 1474568 | tf_op jit(solution)/shard_map/ppermute | solution.py:32
  14.2 4.2 %collective-permute-start.5 = (bf16[640,384]{1,0:T(8,128)(2,1)S(1)}, bf16[640,384]{1,0:T(8,128)(2,1)S(1)}, u32[]{:S(2)}, u32[]{:S(2)}) collective-permute-start(bf16[640,384]{1,0:T(8,128)(2,1)S(1)} %collective-permute-done.2), channel_id=1, source_target_pairs={{8,9},{11,10},{24,25},{27,26}} | collective-permute-start | bytes 1474568 | tf_op jit(solution)/shard_map/ppermute | solution.py:49
  14.9 5.5 %collective-permute-start.3 = (bf16[640,384]{1,0:T(8,128)(2,1)S(1)}, bf16[640,384]{1,0:T(8,128)(2,1)S(1)}, u32[]{:S(2)}, u32[]{:S(2)}) collective-permute-start(bf16[640,384]{1,0:T(8,128)(2,1)S(1)} %collective-permute-done), channel_id=1, source_target_pairs={{1,2},{2,1},{5,6},{6,5},{9,10},{10,9},{13,14},{14,13},{17,18},{18,... | collective-permute-start | bytes 1474568 | tf_op jit(solution)/shard_map/ppermute | solution.py:45
  15.6 2.8 %collective-permute-start.4 = (bf16[640,384]{1,0:T(8,128)(2,1)S(1)}, bf16[640,384]{1,0:T(8,128)(2,1)S(1)}, u32[]{:S(2)}, u32[]{:S(2)}) collective-permute-start(bf16[640,384]{1,0:T(8,128)(2,1)S(1)} %collective-permute-done), channel_id=1, source_target_pairs={{1,5},{2,6},{9,13},{10,14},{17,21},{18,22},{25,29},{26,30}} | collective-permute-start | bytes 1474568 | tf_op jit(solution)/shard_map/ppermute | solution.py:49
  21.1 1.4 %collective-permute-start.6 = (f32[768]{0:T(1024)S(1)}, f32[768]{0:T(1024)S(1)}, u32[]{:S(2)}, u32[]{:S(2)}) collective-permute-start(f32[768]{0:T(1024)S(1)} %add.17), channel_id=1, source_target_pairs={{5,1},{6,2},{9,5},{10,6},{13,9},{14,10},{21,17},{22,18},{25,21},{2... | collective-permute-start | bytes 9224 | tf_op jit(solution)/shard_map/ppermute | solution.py:56
  22.5 17.3 %collective-permute-start.7 = (f32[384]{0:T(512)S(1)}, f32[384]{0:T(512)S(1)}, u32[]{:S(2)}, u32[]{:S(2)}) collective-permute-start(f32[384]{0:T(512)S(1)} %slice_add_fusion), channel_id=1, source_target_pairs={{1,0},{2,3},{5,4},{6,7},{9,8},{10,11},{13,12},{14,15},{17,16},{18,... | collective-permute-start | bytes 4616 | tf_op jit(solution)/shard_map/ppermute | solution.py:59

commit v10 on v9

--- a/solution.py
+++ b/solution.py
@@ -53,7 +53,10 @@
     for rows in (jnp.concatenate([own, adopt], axis=1), jnp.concatenate(prev, axis=1)):
         total = row_squares(rows, early, scaling) + row_squares(rows, far, scaling)
         sums += [total[:width], total[width:]]
-    following = lax.ppermute(jnp.concatenate(sums[2:]), both, backward)
+    returned = jnp.concatenate(sums[2:])
+    back_within = [(a, b) for a, b in backward if (b // line) % 2 == 0]
+    back_across = [(a, b) for a, b in backward if (b // line) % 2 == 1]
+    following = lax.ppermute(returned, both, back_within) + lax.ppermute(returned, both, back_across)
     at_hub = sums[0] + following[:width]
     adopted = sums[1] + following[width:]
     at_end = lax.ppermute(adopted, "group", [(1, 0), (2, 3)])

time: 40.7 us -> 43.3 us (1.064)
  waiting for transfers between devices: 20.3 us -> 22.3 us
  starting transfers between devices: 12.7 us -> 13.4 us
    ppermute x1, waiting for transfers between devices: 16 us -> 17.9 us  [hub_plan(): at_end = lax.ppermute(adopted, 'group', [(1, 0), (2, 3)])]
    ppermute x1 -> x2, starting transfers between devices: 0.66 us -> 1.32 us  [the longest x1 0.66 us: hub_plan(): lax.ppermute(returned, both, back_within)]
  transfers between devices with their start and end apart: 8 -> 9, of which waited for: 2 -> 2; matrix products, arithmetic and copies ran while one was open for 14% -> 14% of each run, Pallas kernels for 0% -> 0%
where the time goes in v10:
time: 43.3 us; the launch traced here: 43 us
  waiting for transfers between devices  22.3 us (52%)
  starting transfers between devices  13.4 us (31%)
  matrix products  5.06 us (12%)
  local copies, waits for them, and re-layouts  1.35 us (3%)
  other arithmetic  0.73 us (2%)
    ppermute x1, waiting for transfers between devices, hub_plan(): at_end = lax.ppermute(adopted, 'group', [(1, 0), (2, 3)])  17.9 us
    dot_general x4, matrix products, row_squares(): lax.dot_general(rows, columns, (((0,), (0,)), ((), ())), preferred_elemen...  5.06 us
    ppermute x1, waiting for transfers between devices, hub_plan(): adopt = lax.ppermute(own, 'group', [(0, 1), (3, 2)])  4.34 us
    ppermute x1, starting transfers between devices, hub_plan(): adopt = lax.ppermute(own, 'group', [(0, 1), (3, 2)])  4.05 us
    ppermute x1, starting transfers between devices, hub_plan(): prev_own = lax.ppermute(own, both, onward + ends_across)  3.99 us
    ppermute x1, starting transfers between devices, hub_plan(): at_end = lax.ppermute(adopted, 'group', [(1, 0), (2, 3)])  1.29 us
    unnamed x1, local copies, waits for them, and re-layouts  1.12 us
  transfers between devices with their start and end apart: 9, of which 2 were waited for; matrix products, arithmetic and copies ran while one was open for 14% of the time, Pallas kernels for 0%

profile of v10, /device:TPU:1, one launch (start us, length us, event | category | flops | bytes accessed | tf_op | source)
XLA Modules:
  0.0 43.0 jit_solution(14825756051176290401)
XLA Ops:
  0.0 4.0 %collective-permute-start = (bf16[640,384]{1,0:T(8,128)(2,1)}, bf16[640,384]{1,0:T(8,128)(2,1)S(1)}, u32[]{:S(2)}, u32[]{:S(2)}) collective-permute-start(bf16[640,384]{1,0:T(8,128)(2,1)} %param.1), channel_id=1, source_target_pairs={{0,1},{3,2},{4,5},{7,6},{8,9},{11,10},{12,13},{15,14},{16,17},{19,... | collective-permute-start | bytes 1474568 | tf_op jit(solution)/shard_map/ppermute | solution.py:31
  4.1 4.0 %collective-permute-start.2 = (bf16[640,384]{1,0:T(8,128)(2,1)}, bf16[640,384]{1,0:T(8,128)(2,1)S(1)}, u32[]{:S(2)}, u32[]{:S(2)}) collective-permute-start(bf16[640,384]{1,0:T(8,128)(2,1)} %param.1), channel_id=1, source_target_pairs={{1,5},{2,6},{5,9},{6,10},{9,13},{10,14},{4,8},{7,11},{17,21},{18,2... | collective-permute-start | bytes 1474568 | tf_op jit(solution)/shard_map/ppermute | solution.py:42
  8.1 0.7 %collective-permute-start.1 = (bf16[640,384]{1,0:T(8,128)(2,1)}, bf16[640,384]{1,0:T(8,128)(2,1)S(1)}, u32[]{:S(2)}, u32[]{:S(2)}) collective-permute-start(bf16[640,384]{1,0:T(8,128)(2,1)} %param.1), channel_id=1, source_target_pairs={{1,2},{2,1},{5,6},{6,5},{9,10},{10,9},{13,14},{14,13},{17,18},{18,... | collective-permute-start | bytes 1474568 | tf_op jit(solution)/shard_map/ppermute | solution.py:32
  8.8 1.1 %constant_dynamic-update-slice_fusion.1 = (bf16[640,768]{1,0:T(8,128)(2,1)S(1)}, bf16[640,1152]{1,0:T(8,128)(2,1)S(1)}) fusion(bf16[640,384]{1,0:T(8,128)(2,1)} %param.1), kind=kLoop, calls=%fused_computation.14 | loop fusion | bytes 1474560
  9.9 4.3 %collective-permute-done = bf16[640,384]{1,0:T(8,128)(2,1)S(1)} collective-permute-done((bf16[640,384]{1,0:T(8,128)(2,1)}, bf16[640,384]{1,0:T(8,128)(2,1)S(1)}, u32[]{:S(2)}, u32[]{:S(2)}) %collective-permute-start) | collective-permute-done | bytes 491552 | tf_op jit(solution)/shard_map/ppermute | solution.py:31
  14.2 0.0 collective-permute-done.2
  14.2 0.7 %collective-permute-start.5 = (bf16[640,384]{1,0:T(8,128)(2,1)S(1)}, bf16[640,384]{1,0:T(8,128)(2,1)S(1)}, u32[]{:S(2)}, u32[]{:S(2)}) collective-permute-start(bf16[640,384]{1,0:T(8,128)(2,1)S(1)} %collective-permute-done.2), channel_id=1, source_target_pairs={{8,9},{11,10},{24,25},{27,26}} | collective-permute-start | bytes 1474568 | tf_op jit(solution)/shard_map/ppermute | solution.py:49
  14.9 0.7 %collective-permute-start.3 = (bf16[640,384]{1,0:T(8,128)(2,1)S(1)}, bf16[640,384]{1,0:T(8,128)(2,1)S(1)}, u32[]{:S(2)}, u32[]{:S(2)}) collective-permute-start(bf16[640,384]{1,0:T(8,128)(2,1)S(1)} %collective-permute-done), channel_id=1, source_target_pairs={{1,2},{2,1},{5,6},{6,5},{9,10},{10,9},{13,14},{14,13},{17,18},{18,... | collective-permute-start | bytes 1474568 | tf_op jit(solution)/shard_map/ppermute | solution.py:45
  15.6 0.7 %collective-permute-start.4 = (bf16[640,384]{1,0:T(8,128)(2,1)S(1)}, bf16[640,384]{1,0:T(8,128)(2,1)S(1)}, u32[]{:S(2)}, u32[]{:S(2)}) collective-permute-start(bf16[640,384]{1,0:T(8,128)(2,1)S(1)} %collective-permute-done), channel_id=1, source_target_pairs={{1,5},{2,6},{9,13},{10,14},{17,21},{18,22},{25,29},{26,30}} | collective-permute-start | bytes 1474568 | tf_op jit(solution)/shard_map/ppermute | solution.py:49
  16.3 0.2 constant_dynamic-update-slice_fusion
  16.5 0.0 collective-permute-done.1
  16.5 0.1 constant_dynamic-update-slice_fusion.2
  16.6 1.8 %fusion.2 = f32[768]{0:T(1024)S(1)} fusion(bf16[640,768]{1,0:T(8,128)(2,1)S(1)} %get-tuple-element.9, bf16[640,1152]{1,0:T(8,128)(2,1)S(1)} %constant_dynamic-update-slice_fusion.2), kind=kOutput, calls=%fused_computation.4 | convolution fusion | flops 1135115520 | bytes 2460672 | tf_op jit(solution)/shard_map/dot_general | solution.py:15
  18.4 0.0 collective-permute-done.4
  18.4 0.0 collective-permute-done.5
  18.4 0.1 add.19
  18.5 1.8 %fusion.3 = f32[768]{0:T(1024)S(1)} fusion(bf16[640,1152]{1,0:T(8,128)(2,1)S(1)} %constant_dynamic-update-slice_fusion.2, bf16[640,384]{1,0:T(8,128)(2,1)S(1)} %add.19, bf16[640,384]{1,0:T(8,128)(2,1)S(1)} %collective-permute-done.2), kind=kOutput, calls=%fused_computation.5 | convolution fusion | flops 1137081600 | bytes 2460672 | tf_op jit(solution)/shard_map/dot_general | solution.py:15
  20.4 0.0 collective-permute-done.3
  20.4 0.7 %fusion.7 = f32[768]{0:T(1024)S(1)} fusion(bf16[640,384]{1,0:T(8,128)(2,1)S(1)} %collective-permute-done.3, bf16[640,384]{1,0:T(8,128)(2,1)S(1)} %add.19, bf16[640,384]{1,0:T(8,128)(2,1)S(1)} %collective-permute-done.2), kind=kOutput, calls=%fused_computation.11 | convolution fusion | flops 380337408 | bytes 1477632 | tf_op jit(solution)/shard_map/dot_general | solution.py:15
  21.1 0.7 %collective-permute-start.6 = (f32[768]{0:T(1024)S(1)}, f32[768]{0:T(1024)S(1)}, u32[]{:S(2)}, u32[]{:S(2)}) collective-permute-start(f32[768]{0:T(1024)S(1)} %add.20), channel_id=1, source_target_pairs={{5,1},{6,2},{13,9},{14,10},{21,17},{22,18},{29,25},{30,26}} | collective-permute-start | bytes 9224 | tf_op jit(solution)/shard_map/ppermute | solution.py:59
  21.8 0.7 %collective-permute-start.7 = (f32[768]{0:T(1024)S(1)}, f32[768]{0:T(1024)S(1)}, u32[]{:S(2)}, u32[]{:S(2)}) collective-permute-start(f32[768]{0:T(1024)S(1)} %add.20), channel_id=1, source_target_pairs={{9,5},{10,6},{25,21},{26,22}} | collective-permute-start | bytes 9224 | tf_op jit(solution)/shard_map/ppermute | solution.py:59
  22.4 0.7 %fusion.6 = f32[768]{0:T(1024)S(1)} fusion(bf16[640,768]{1,0:T(8,128)(2,1)S(1)} %get-tuple-element.9, bf16[640,384]{1,0:T(8,128)(2,1)S(1)} %collective-permute-done.3), kind=kOutput, calls=%fused_computation.10 | convolution fusion | flops 378371328 | bytes 1477632 | tf_op jit(solution)/shard_map/dot_general | solution.py:15
  23.2 0.0 collective-permute-done.6
  23.2 0.0 collective-permute-done.7
  23.2 1.3 %collective-permute-start.8 = (f32[384]{0:T(512)S(1)}, f32[384]{0:T(512)S(1)}, u32[]{:S(2)}, u32[]{:S(2)}) collective-permute-start(f32[384]{0:T(512)S(1)} %slice_add_fusion), channel_id=1, source_target_pairs={{1,0},{2,3},{5,4},{6,7},{9,8},{10,11},{13,12},{14,15},{17,16},{18,... | collective-permute-start | bytes 4616 | tf_op jit(solution)/shard_map/ppermute | solution.py:62
  24.5 17.9 %collective-permute-done.8 = f32[384]{0:T(512)S(1)} collective-permute-done((f32[384]{0:T(512)S(1)}, f32[384]{0:T(512)S(1)}, u32[]{:S(2)}, u32[]{:S(2)}) %collective-permute-start.8) | collective-permute-done | bytes 1568 | tf_op jit(solution)/shard_map/ppermute | solution.py:62
  42.4 0.6 %add_select_fusion = f32[384]{0:T(512)} fusion(f32[384]{0:T(512)S(1)} %collective-permute-done.8, f32[768]{0:T(1024)S(1)} %add.21, f32[768]{0:T(1024)S(1)} %add.18, pred[]{:T(512)S(6)} %or.3), kind=kLoop, calls=%fused_computation.19 | loop fusion | flops 768 | bytes 6145 | tf_op jit(solution)/shard_map/jit(_where)/select_n | solution.py:64
  (4 shorter events, 0.0 us)
Async XLA Ops:
  0.0 14.2 %collective-permute-start = (bf16[640,384]{1,0:T(8,128)(2,1)}, bf16[640,384]{1,0:T(8,128)(2,1)S(1)}, u32[]{:S(2)}, u32[]{:S(2)}) collective-permute-start(bf16[640,384]{1,0:T(8,128)(2,1)} %param.1), channel_id=1, source_target_pairs={{0,1},{3,2},{4,5},{7,6},{8,9},{11,10},{12,13},{15,14},{16,17},{19,... | collective-permute-start | bytes 1474568 | tf_op jit(solution)/shard_map/ppermute | solution.py:31
  4.1 10.2 %collective-permute-start.2 = (bf16[640,384]{1,0:T(8,128)(2,1)}, bf16[640,384]{1,0:T(8,128)(2,1)S(1)}, u32[]{:S(2)}, u32[]{:S(2)}) collective-permute-start(bf16[640,384]{1,0:T(8,128)(2,1)} %param.1), channel_id=1, source_target_pairs={{1,5},{2,6},{5,9},{6,10},{9,13},{10,14},{4,8},{7,11},{17,21},{18,2... | collective-permute-start | bytes 1474568 | tf_op jit(solution)/shard_map/ppermute | solution.py:42
  8.1 8.4 %collective-permute-start.1 = (bf16[640,384]{1,0:T(8,128)(2,1)}, bf16[640,384]{1,0:T(8,128)(2,1)S(1)}, u32[]{:S(2)}, u32[]{:S(2)}) collective-permute-start(bf16[640,384]{1,0:T(8,128)(2,1)} %param.1), channel_id=1, source_target_pairs={{1,2},{2,1},{5,6},{6,5},{9,10},{10,9},{13,14},{14,13},{17,18},{18,... | collective-permute-start | bytes 1474568 | tf_op jit(solution)/shard_map/ppermute | solution.py:32
  14.2 4.2 %collective-permute-start.5 = (bf16[640,384]{1,0:T(8,128)(2,1)S(1)}, bf16[640,384]{1,0:T(8,128)(2,1)S(1)}, u32[]{:S(2)}, u32[]{:S(2)}) collective-permute-start(bf16[640,384]{1,0:T(8,128)(2,1)S(1)} %collective-permute-done.2), channel_id=1, source_target_pairs={{8,9},{11,10},{24,25},{27,26}} | collective-permute-start | bytes 1474568 | tf_op jit(solution)/shard_map/ppermute | solution.py:49
  14.9 5.5 %collective-permute-start.3 = (bf16[640,384]{1,0:T(8,128)(2,1)S(1)}, bf16[640,384]{1,0:T(8,128)(2,1)S(1)}, u32[]{:S(2)}, u32[]{:S(2)}) collective-permute-start(bf16[640,384]{1,0:T(8,128)(2,1)S(1)} %collective-permute-done), channel_id=1, source_target_pairs={{1,2},{2,1},{5,6},{6,5},{9,10},{10,9},{13,14},{14,13},{17,18},{18,... | collective-permute-start | bytes 1474568 | tf_op jit(solution)/shard_map/ppermute | solution.py:45
  15.6 2.8 %collective-permute-start.4 = (bf16[640,384]{1,0:T(8,128)(2,1)S(1)}, bf16[640,384]{1,0:T(8,128)(2,1)S(1)}, u32[]{:S(2)}, u32[]{:S(2)}) collective-permute-start(bf16[640,384]{1,0:T(8,128)(2,1)S(1)} %collective-permute-done), channel_id=1, source_target_pairs={{1,5},{2,6},{9,13},{10,14},{17,21},{18,22},{25,29},{26,30}} | collective-permute-start | bytes 1474568 | tf_op jit(solution)/shard_map/ppermute | solution.py:49
  21.1 2.1 %collective-permute-start.6 = (f32[768]{0:T(1024)S(1)}, f32[768]{0:T(1024)S(1)}, u32[]{:S(2)}, u32[]{:S(2)}) collective-permute-start(f32[768]{0:T(1024)S(1)} %add.20), channel_id=1, source_target_pairs={{5,1},{6,2},{13,9},{14,10},{21,17},{22,18},{29,25},{30,26}} | collective-permute-start | bytes 9224 | tf_op jit(solution)/shard_map/ppermute | solution.py:59
  21.8 1.4 %collective-permute-start.7 = (f32[768]{0:T(1024)S(1)}, f32[768]{0:T(1024)S(1)}, u32[]{:S(2)}, u32[]{:S(2)}) collective-permute-start(f32[768]{0:T(1024)S(1)} %add.20), channel_id=1, source_target_pairs={{9,5},{10,6},{25,21},{26,22}} | collective-permute-start | bytes 9224 | tf_op jit(solution)/shard_map/ppermute | solution.py:59
  23.2 19.2 %collective-permute-start.8 = (f32[384]{0:T(512)S(1)}, f32[384]{0:T(512)S(1)}, u32[]{:S(2)}, u32[]{:S(2)}) collective-permute-start(f32[384]{0:T(512)S(1)} %slice_add_fusion), channel_id=1, source_target_pairs={{1,0},{2,3},{5,4},{6,7},{9,8},{10,11},{13,12},{14,15},{17,16},{18,... | collective-permute-start | bytes 4616 | tf_op jit(solution)/shard_map/ppermute | solution.py:62

commit v11 on v9

--- a/solution.py
+++ b/solution.py
@@ -53,10 +53,10 @@
     for rows in (jnp.concatenate([own, adopt], axis=1), jnp.concatenate(prev, axis=1)):
         total = row_squares(rows, early, scaling) + row_squares(rows, far, scaling)
         sums += [total[:width], total[width:]]
-    following = lax.ppermute(jnp.concatenate(sums[2:]), both, backward)
-    at_hub = sums[0] + following[:width]
-    adopted = sums[1] + following[width:]
-    at_end = lax.ppermute(adopted, "group", [(1, 0), (2, 3)])
+    to_end = [((g + 1) * line + 1, g * line) for g in steps]
+    to_end += [((g + 1) * line + line - 2, g * line + line - 1) for g in steps]
+    at_hub = sums[0] + lax.ppermute(sums[2], both, backward)
+    at_end = lax.ppermute(sums[1], "group", [(1, 0), (2, 3)]) + lax.ppermute(sums[3], both, to_end)
     place = lax.axis_index("group")
     return jnp.where((place == 1) | (place == 2), at_hub, at_end)
 

time: 40.7 us -> 40.9 us (level)
  starting transfers between devices: 12.7 us -> 14 us
  waiting for transfers between devices: 20.3 us -> 19.2 us
    ppermute x2 -> x3, starting transfers between devices: 1.95 us -> 3.25 us  [the longest x1 1.29 us: hub_plan(): lax.ppermute(sums[3], both, to_end)]
    ppermute x2 -> x3, waiting for transfers between devices: 16 us -> 14.8 us  [the longest x1 8.75 us: hub_plan(): lax.ppermute(sums[1], 'group', [(1, 0), (2, 3)])]
    unnamed x1 -> x2, local copies, waits for them, and re-layouts: 1.12 us -> 1.27 us
  transfers between devices with their start and end apart: 8 -> 9, of which waited for: 2 -> 3; matrix products, arithmetic and copies ran while one was open for 14% -> 16% of each run, Pallas kernels for 0% -> 0%
where the time goes in v11:
time: 40.9 us; the launch traced here: 40.5 us
  waiting for transfers between devices  19.2 us (47%)
  starting transfers between devices  14 us (34%)
  matrix products  5.05 us (12%)
  local copies, waits for them, and re-layouts  1.36 us (3%)
  other arithmetic  0.72 us (2%)
    ppermute x1, waiting for transfers between devices, hub_plan(): lax.ppermute(sums[1], 'group', [(1, 0), (2, 3)])  8.75 us
    ppermute x1, waiting for transfers between devices, hub_plan(): lax.ppermute(sums[3], both, to_end)  6.05 us
    dot_general x4, matrix products, row_squares(): lax.dot_general(rows, columns, (((0,), (0,)), ((), ())), preferred_elemen...  5.05 us
    ppermute x1, waiting for transfers between devices, hub_plan(): adopt = lax.ppermute(own, 'group', [(0, 1), (3, 2)])  4.34 us
    ppermute x1, starting transfers between devices, hub_plan(): adopt = lax.ppermute(own, 'group', [(0, 1), (3, 2)])  4.05 us
    ppermute x1, starting transfers between devices, hub_plan(): prev_own = lax.ppermute(own, both, onward + ends_across)  3.99 us
    ppermute x1, starting transfers between devices, hub_plan(): lax.ppermute(sums[3], both, to_end)  1.29 us
    ppermute x1, starting transfers between devices, hub_plan(): lax.ppermute(sums[1], 'group', [(1, 0), (2, 3)])  1.29 us
  transfers between devices with their start and end apart: 9, of which 3 were waited for; matrix products, arithmetic and copies ran while one was open for 16% of the time, Pallas kernels for 0%

profile of v11, /device:TPU:1, one launch (start us, length us, event | category | flops | bytes accessed | tf_op | source)
XLA Modules:
  0.0 40.5 jit_solution(15883425716728598224)
XLA Ops:
  0.0 4.0 %collective-permute-start = (bf16[640,384]{1,0:T(8,128)(2,1)}, bf16[640,384]{1,0:T(8,128)(2,1)S(1)}, u32[]{:S(2)}, u32[]{:S(2)}) collective-permute-start(bf16[640,384]{1,0:T(8,128)(2,1)} %param.1), channel_id=1, source_target_pairs={{0,1},{3,2},{4,5},{7,6},{8,9},{11,10},{12,13},{15,14},{16,17},{19,... | collective-permute-start | bytes 1474568 | tf_op jit(solution)/shard_map/ppermute | solution.py:31
  4.1 4.0 %collective-permute-start.2 = (bf16[640,384]{1,0:T(8,128)(2,1)}, bf16[640,384]{1,0:T(8,128)(2,1)S(1)}, u32[]{:S(2)}, u32[]{:S(2)}) collective-permute-start(bf16[640,384]{1,0:T(8,128)(2,1)} %param.1), channel_id=1, source_target_pairs={{1,5},{2,6},{5,9},{6,10},{9,13},{10,14},{4,8},{7,11},{17,21},{18,2... | collective-permute-start | bytes 1474568 | tf_op jit(solution)/shard_map/ppermute | solution.py:42
  8.1 0.7 %collective-permute-start.1 = (bf16[640,384]{1,0:T(8,128)(2,1)}, bf16[640,384]{1,0:T(8,128)(2,1)S(1)}, u32[]{:S(2)}, u32[]{:S(2)}) collective-permute-start(bf16[640,384]{1,0:T(8,128)(2,1)} %param.1), channel_id=1, source_target_pairs={{1,2},{2,1},{5,6},{6,5},{9,10},{10,9},{13,14},{14,13},{17,18},{18,... | collective-permute-start | bytes 1474568 | tf_op jit(solution)/shard_map/ppermute | solution.py:32
  8.8 1.1 %constant_dynamic-update-slice_fusion.4 = (bf16[640,1152]{1,0:T(8,128)(2,1)S(1)}, bf16[640,768]{1,0:T(8,128)(2,1)S(1)}) fusion(bf16[640,384]{1,0:T(8,128)(2,1)} %param.1), kind=kLoop, calls=%fused_computation.17 | loop fusion | bytes 1474560
  9.9 4.3 %collective-permute-done = bf16[640,384]{1,0:T(8,128)(2,1)S(1)} collective-permute-done((bf16[640,384]{1,0:T(8,128)(2,1)}, bf16[640,384]{1,0:T(8,128)(2,1)S(1)}, u32[]{:S(2)}, u32[]{:S(2)}) %collective-permute-start) | collective-permute-done | bytes 491552 | tf_op jit(solution)/shard_map/ppermute | solution.py:31
  14.2 0.0 collective-permute-done.2
  14.2 0.7 %collective-permute-start.3 = (bf16[640,384]{1,0:T(8,128)(2,1)S(1)}, bf16[640,384]{1,0:T(8,128)(2,1)S(1)}, u32[]{:S(2)}, u32[]{:S(2)}) collective-permute-start(bf16[640,384]{1,0:T(8,128)(2,1)S(1)} %collective-permute-done), channel_id=1, source_target_pairs={{1,2},{2,1},{5,6},{6,5},{9,10},{10,9},{13,14},{14,13},{17,18},{18,... | collective-permute-start | bytes 1474568 | tf_op jit(solution)/shard_map/ppermute | solution.py:45
  14.9 0.7 %collective-permute-start.5 = (bf16[640,384]{1,0:T(8,128)(2,1)S(1)}, bf16[640,384]{1,0:T(8,128)(2,1)S(1)}, u32[]{:S(2)}, u32[]{:S(2)}) collective-permute-start(bf16[640,384]{1,0:T(8,128)(2,1)S(1)} %collective-permute-done.2), channel_id=1, source_target_pairs={{8,9},{11,10},{24,25},{27,26}} | collective-permute-start | bytes 1474568 | tf_op jit(solution)/shard_map/ppermute | solution.py:49
  15.6 0.7 %collective-permute-start.4 = (bf16[640,384]{1,0:T(8,128)(2,1)S(1)}, bf16[640,384]{1,0:T(8,128)(2,1)S(1)}, u32[]{:S(2)}, u32[]{:S(2)}) collective-permute-start(bf16[640,384]{1,0:T(8,128)(2,1)S(1)} %collective-permute-done), channel_id=1, source_target_pairs={{1,5},{2,6},{9,13},{10,14},{17,21},{18,22},{25,29},{26,30}} | collective-permute-start | bytes 1474568 | tf_op jit(solution)/shard_map/ppermute | solution.py:49
  16.3 0.2 constant_dynamic-update-slice_fusion.3
  16.5 0.0 collective-permute-done.1
  16.5 0.1 constant_dynamic-update-slice_fusion.2
  16.6 1.8 %fusion.2 = f32[768]{0:T(1024)S(1)} fusion(bf16[640,768]{1,0:T(8,128)(2,1)S(1)} %get-tuple-element.10, bf16[640,1152]{1,0:T(8,128)(2,1)S(1)} %constant_dynamic-update-slice_fusion.2), kind=kOutput, calls=%fused_computation.4 | convolution fusion | flops 1135115520 | bytes 2460672 | tf_op jit(solution)/shard_map/dot_general | solution.py:15
  18.4 0.0 collective-permute-done.3
  18.4 0.7 %fusion.6 = f32[768]{0:T(1024)S(1)} fusion(bf16[640,768]{1,0:T(8,128)(2,1)S(1)} %get-tuple-element.10, bf16[640,384]{1,0:T(8,128)(2,1)S(1)} %collective-permute-done.3), kind=kOutput, calls=%fused_computation.10 | convolution fusion | flops 378371328 | bytes 1477632 | tf_op jit(solution)/shard_map/dot_general | solution.py:15
  19.1 1.3 %collective-permute-start.7 = (f32[384]{0:T(512)S(1)}, f32[384]{0:T(512)S(1)}, u32[]{:S(2)}, u32[]{:S(2)}) collective-permute-start(f32[384]{0:T(512)S(1)} %slice.14), channel_id=1, source_target_pairs={{1,0},{2,3},{5,4},{6,7},{9,8},{10,11},{13,12},{14,15},{17,16},{18,... | collective-permute-start | bytes 4616 | tf_op jit(solution)/shard_map/ppermute | solution.py:59
  20.4 0.0 collective-permute-done.4
  20.4 0.0 collective-permute-done.5
  20.4 0.1 add.16
  20.6 1.8 %fusion.3 = f32[768]{0:T(1024)S(1)} fusion(bf16[640,1152]{1,0:T(8,128)(2,1)S(1)} %constant_dynamic-update-slice_fusion.2, bf16[640,384]{1,0:T(8,128)(2,1)S(1)} %add.16, bf16[640,384]{1,0:T(8,128)(2,1)S(1)} %collective-permute-done.2), kind=kOutput, calls=%fused_computation.5 | convolution fusion | flops 1137081600 | bytes 2460672 | tf_op jit(solution)/shard_map/dot_general | solution.py:15
  22.4 0.7 %fusion.7 = f32[768]{0:T(1024)S(1)} fusion(bf16[640,384]{1,0:T(8,128)(2,1)S(1)} %collective-permute-done.3, bf16[640,384]{1,0:T(8,128)(2,1)S(1)} %add.16, bf16[640,384]{1,0:T(8,128)(2,1)S(1)} %collective-permute-done.2), kind=kOutput, calls=%fused_computation.11 | convolution fusion | flops 380337408 | bytes 1477632 | tf_op jit(solution)/shard_map/dot_general | solution.py:15
  23.1 1.3 %collective-permute-start.8 = (f32[384]{0:T(512)S(1)}, f32[384]{0:T(512)S(1)}, u32[]{:S(2)}, u32[]{:S(2)}) collective-permute-start(f32[384]{0:T(512)S(1)} %get-tuple-element.14), channel_id=1, source_target_pairs={{5,0},{9,4},{13,8},{6,3},{10,7},{14,11},{21,16},{25,20},{29,24},{2... | collective-permute-start | bytes 4616 | tf_op jit(solution)/shard_map/ppermute | solution.py:59
  24.4 0.7 %collective-permute-start.6 = (f32[384]{0:T(512)S(1)}, f32[384]{0:T(512)S(1)}, u32[]{:S(2)}, u32[]{:S(2)}) collective-permute-start(f32[384]{0:T(512)S(1)} %get-tuple-element.13), channel_id=1, source_target_pairs={{5,1},{6,2},{9,5},{10,6},{13,9},{14,10},{21,17},{22,18},{25,21},{2... | collective-permute-start | bytes 4616 | tf_op jit(solution)/shard_map/ppermute | solution.py:58
  25.1 8.8 %collective-permute-done.7 = f32[384]{0:T(512)S(1)} collective-permute-done((f32[384]{0:T(512)S(1)}, f32[384]{0:T(512)S(1)}, u32[]{:S(2)}, u32[]{:S(2)}) %collective-permute-start.7) | collective-permute-done | bytes 1568 | tf_op jit(solution)/shard_map/ppermute | solution.py:59
  33.9 6.1 %collective-permute-done.8 = f32[384]{0:T(512)S(1)} collective-permute-done((f32[384]{0:T(512)S(1)}, f32[384]{0:T(512)S(1)}, u32[]{:S(2)}, u32[]{:S(2)}) %collective-permute-start.8) | collective-permute-done | bytes 1568 | tf_op jit(solution)/shard_map/ppermute | solution.py:59
  39.9 0.0 collective-permute-done.6
  39.9 0.6 %add_select_fusion = f32[384]{0:T(512)} fusion(f32[384]{0:T(512)S(1)} %collective-permute-done.7, f32[384]{0:T(512)S(1)} %collective-permute-done.8, f32[384]{0:T(512)S(1)} %collective-permute-done.6, f32[768]{0:T(1024)S(1)} %add.15, pred[]{:T(512)S(6)} %or.3), kind=kLoop, calls=%fused_computation.18 | loop fusion | flops 1152 | bytes 7681 | tf_op jit(solution)/shard_map/jit(_where)/select_n | solution.py:61
  (4 shorter events, 0.0 us)
Async XLA Ops:
  0.0 14.2 %collective-permute-start = (bf16[640,384]{1,0:T(8,128)(2,1)}, bf16[640,384]{1,0:T(8,128)(2,1)S(1)}, u32[]{:S(2)}, u32[]{:S(2)}) collective-permute-start(bf16[640,384]{1,0:T(8,128)(2,1)} %param.1), channel_id=1, source_target_pairs={{0,1},{3,2},{4,5},{7,6},{8,9},{11,10},{12,13},{15,14},{16,17},{19,... | collective-permute-start | bytes 1474568 | tf_op jit(solution)/shard_map/ppermute | solution.py:31
  4.1 10.2 %collective-permute-start.2 = (bf16[640,384]{1,0:T(8,128)(2,1)}, bf16[640,384]{1,0:T(8,128)(2,1)S(1)}, u32[]{:S(2)}, u32[]{:S(2)}) collective-permute-start(bf16[640,384]{1,0:T(8,128)(2,1)} %param.1), channel_id=1, source_target_pairs={{1,5},{2,6},{5,9},{6,10},{9,13},{10,14},{4,8},{7,11},{17,21},{18,2... | collective-permute-start | bytes 1474568 | tf_op jit(solution)/shard_map/ppermute | solution.py:42
  8.1 8.4 %collective-permute-start.1 = (bf16[640,384]{1,0:T(8,128)(2,1)}, bf16[640,384]{1,0:T(8,128)(2,1)S(1)}, u32[]{:S(2)}, u32[]{:S(2)}) collective-permute-start(bf16[640,384]{1,0:T(8,128)(2,1)} %param.1), channel_id=1, source_target_pairs={{1,2},{2,1},{5,6},{6,5},{9,10},{10,9},{13,14},{14,13},{17,18},{18,... | collective-permute-start | bytes 1474568 | tf_op jit(solution)/shard_map/ppermute | solution.py:32
  14.2 4.2 %collective-permute-start.3 = (bf16[640,384]{1,0:T(8,128)(2,1)S(1)}, bf16[640,384]{1,0:T(8,128)(2,1)S(1)}, u32[]{:S(2)}, u32[]{:S(2)}) collective-permute-start(bf16[640,384]{1,0:T(8,128)(2,1)S(1)} %collective-permute-done), channel_id=1, source_target_pairs={{1,2},{2,1},{5,6},{6,5},{9,10},{10,9},{13,14},{14,13},{17,18},{18,... | collective-permute-start | bytes 1474568 | tf_op jit(solution)/shard_map/ppermute | solution.py:45
  14.9 5.5 %collective-permute-start.5 = (bf16[640,384]{1,0:T(8,128)(2,1)S(1)}, bf16[640,384]{1,0:T(8,128)(2,1)S(1)}, u32[]{:S(2)}, u32[]{:S(2)}) collective-permute-start(bf16[640,384]{1,0:T(8,128)(2,1)S(1)} %collective-permute-done.2), channel_id=1, source_target_pairs={{8,9},{11,10},{24,25},{27,26}} | collective-permute-start | bytes 1474568 | tf_op jit(solution)/shard_map/ppermute | solution.py:49
  15.6 4.8 %collective-permute-start.4 = (bf16[640,384]{1,0:T(8,128)(2,1)S(1)}, bf16[640,384]{1,0:T(8,128)(2,1)S(1)}, u32[]{:S(2)}, u32[]{:S(2)}) collective-permute-start(bf16[640,384]{1,0:T(8,128)(2,1)S(1)} %collective-permute-done), channel_id=1, source_target_pairs={{1,5},{2,6},{9,13},{10,14},{17,21},{18,22},{25,29},{26,30}} | collective-permute-start | bytes 1474568 | tf_op jit(solution)/shard_map/ppermute | solution.py:49
  19.1 14.7 %collective-permute-start.7 = (f32[384]{0:T(512)S(1)}, f32[384]{0:T(512)S(1)}, u32[]{:S(2)}, u32[]{:S(2)}) collective-permute-start(f32[384]{0:T(512)S(1)} %slice.14), channel_id=1, source_target_pairs={{1,0},{2,3},{5,4},{6,7},{9,8},{10,11},{13,12},{14,15},{17,16},{18,... | collective-permute-start | bytes 4616 | tf_op jit(solution)/shard_map/ppermute | solution.py:59
  23.1 16.8 %collective-permute-start.8 = (f32[384]{0:T(512)S(1)}, f32[384]{0:T(512)S(1)}, u32[]{:S(2)}, u32[]{:S(2)}) collective-permute-start(f32[384]{0:T(512)S(1)} %get-tuple-element.14), channel_id=1, source_target_pairs={{5,0},{9,4},{13,8},{6,3},{10,7},{14,11},{21,16},{25,20},{29,24},{2... | collective-permute-start | bytes 4616 | tf_op jit(solution)/shard_map/ppermute | solution.py:59
  24.4 15.5 %collective-permute-start.6 = (f32[384]{0:T(512)S(1)}, f32[384]{0:T(512)S(1)}, u32[]{:S(2)}, u32[]{:S(2)}) collective-permute-start(f32[384]{0:T(512)S(1)} %get-tuple-element.13), channel_id=1, source_target_pairs={{5,1},{6,2},{9,5},{10,6},{13,9},{14,10},{21,17},{22,18},{25,21},{2... | collective-permute-start | bytes 4616 | tf_op jit(solution)/shard_map/ppermute | solution.py:58

commit v12 on v9

--- a/solution.py
+++ b/solution.py
@@ -41,7 +41,8 @@
     ends_across = [(g * line + z, (g + 1) * line + z) for g in crossing for z in (0, line - 1)]
     prev_own = lax.ppermute(own, both, onward + ends_across)
     on_chip = [(g * line + z, (g + 1) * line + z) for g in steps if g % 2 == 0 for z in hubs]
-    relay, adopted_here = lax.optimization_barrier((prev_own, adopt))
+    adopted_here, nbr = lax.optimization_barrier((adopt, nbr))
+    relay, _ = lax.optimization_barrier((prev_own, adopted_here))
     far = lax.ppermute(adopted_here, "group", [(1, 2), (2, 1)])
     early = jnp.concatenate([own, adopt, nbr], axis=1)
     relayed = [((g + 1) * line, (g + 1) * line + 1) for g in crossing]

time: 40.7 us -> 43.5 us (1.069)
  waiting for transfers between devices: 20.3 us -> 23.1 us
    ppermute x1, waiting for transfers between devices: 16 us -> 18.8 us  [hub_plan(): at_end = lax.ppermute(adopted, 'group', [(1, 0), (2, 3)])]
where the time goes in v12:
time: 43.5 us; the launch traced here: 43.2 us
  waiting for transfers between devices  23.1 us (53%)
  starting transfers between devices  12.7 us (29%)
  matrix products  5.06 us (12%)
  local copies, waits for them, and re-layouts  1.37 us (3%)
  other arithmetic  0.73 us (2%)
    ppermute x1, waiting for transfers between devices, hub_plan(): at_end = lax.ppermute(adopted, 'group', [(1, 0), (2, 3)])  18.8 us
    dot_general x4, matrix products, row_squares(): lax.dot_general(rows, columns, (((0,), (0,)), ((), ())), preferred_elemen...  5.06 us
    ppermute x1, waiting for transfers between devices, hub_plan(): adopt = lax.ppermute(own, 'group', [(0, 1), (3, 2)])  4.32 us
    ppermute x1, starting transfers between devices, hub_plan(): adopt = lax.ppermute(own, 'group', [(0, 1), (3, 2)])  4.05 us
    ppermute x1, starting transfers between devices, hub_plan(): prev_own = lax.ppermute(own, both, onward + ends_across)  3.99 us
    ppermute x1, starting transfers between devices, hub_plan(): at_end = lax.ppermute(adopted, 'group', [(1, 0), (2, 3)])  1.29 us
    unnamed x1, local copies, waits for them, and re-layouts  1.14 us
  transfers between devices with their start and end apart: 8, of which 2 were waited for; matrix products, arithmetic and copies ran while one was open for 14% of the time, Pallas kernels for 0%

profile of v12, /device:TPU:1, one launch (start us, length us, event | category | flops | bytes accessed | tf_op | source)
XLA Modules:
  0.0 43.2 jit_solution(6485843510483587327)
XLA Ops:
  0.0 4.0 %collective-permute-start = (bf16[640,384]{1,0:T(8,128)(2,1)}, bf16[640,384]{1,0:T(8,128)(2,1)S(1)}, u32[]{:S(2)}, u32[]{:S(2)}) collective-permute-start(bf16[640,384]{1,0:T(8,128)(2,1)} %param.1), channel_id=1, source_target_pairs={{0,1},{3,2},{4,5},{7,6},{8,9},{11,10},{12,13},{15,14},{16,17},{19,... | collective-permute-start | bytes 1474568 | tf_op jit(solution)/shard_map/ppermute | solution.py:31
  4.1 0.7 %collective-permute-start.1 = (bf16[640,384]{1,0:T(8,128)(2,1)}, bf16[640,384]{1,0:T(8,128)(2,1)S(1)}, u32[]{:S(2)}, u32[]{:S(2)}) collective-permute-start(bf16[640,384]{1,0:T(8,128)(2,1)} %param.1), channel_id=1, source_target_pairs={{1,2},{2,1},{5,6},{6,5},{9,10},{10,9},{13,14},{14,13},{17,18},{18,... | collective-permute-start | bytes 1474568 | tf_op jit(solution)/shard_map/ppermute | solution.py:32
  4.8 4.0 %collective-permute-start.3 = (bf16[640,384]{1,0:T(8,128)(2,1)}, bf16[640,384]{1,0:T(8,128)(2,1)S(1)}, u32[]{:S(2)}, u32[]{:S(2)}) collective-permute-start(bf16[640,384]{1,0:T(8,128)(2,1)} %param.1), channel_id=1, source_target_pairs={{1,5},{2,6},{5,9},{6,10},{9,13},{10,14},{4,8},{7,11},{17,21},{18,2... | collective-permute-start | bytes 1474568 | tf_op jit(solution)/shard_map/ppermute | solution.py:42
  8.8 1.1 %constant_dynamic-update-slice_fusion.1 = (bf16[640,768]{1,0:T(8,128)(2,1)S(1)}, bf16[640,1152]{1,0:T(8,128)(2,1)S(1)}) fusion(bf16[640,384]{1,0:T(8,128)(2,1)} %param.1), kind=kLoop, calls=%fused_computation.14 | loop fusion | bytes 1474560
  9.9 4.3 %collective-permute-done = bf16[640,384]{1,0:T(8,128)(2,1)S(1)} collective-permute-done((bf16[640,384]{1,0:T(8,128)(2,1)}, bf16[640,384]{1,0:T(8,128)(2,1)S(1)}, u32[]{:S(2)}, u32[]{:S(2)}) %collective-permute-start) | collective-permute-done | bytes 491552 | tf_op jit(solution)/shard_map/ppermute | solution.py:31
  14.2 0.0 collective-permute-done.1
  14.2 0.7 %collective-permute-start.2 = (bf16[640,384]{1,0:T(8,128)(2,1)S(1)}, bf16[640,384]{1,0:T(8,128)(2,1)S(1)}, u32[]{:S(2)}, u32[]{:S(2)}) collective-permute-start(bf16[640,384]{1,0:T(8,128)(2,1)S(1)} %collective-permute-done), channel_id=1, source_target_pairs={{1,2},{2,1},{5,6},{6,5},{9,10},{10,9},{13,14},{14,13},{17,18},{18,... | collective-permute-start | bytes 1474568 | tf_op jit(solution)/shard_map/ppermute | solution.py:46
  14.9 0.0 collective-permute-done.3
  14.9 0.7 %collective-permute-start.5 = (bf16[640,384]{1,0:T(8,128)(2,1)S(1)}, bf16[640,384]{1,0:T(8,128)(2,1)S(1)}, u32[]{:S(2)}, u32[]{:S(2)}) collective-permute-start(bf16[640,384]{1,0:T(8,128)(2,1)S(1)} %collective-permute-done.3), channel_id=1, source_target_pairs={{8,9},{11,10},{24,25},{27,26}} | collective-permute-start | bytes 1474568 | tf_op jit(solution)/shard_map/ppermute | solution.py:50
  15.6 0.7 %collective-permute-start.4 = (bf16[640,384]{1,0:T(8,128)(2,1)S(1)}, bf16[640,384]{1,0:T(8,128)(2,1)S(1)}, u32[]{:S(2)}, u32[]{:S(2)}) collective-permute-start(bf16[640,384]{1,0:T(8,128)(2,1)S(1)} %collective-permute-done), channel_id=1, source_target_pairs={{1,5},{2,6},{9,13},{10,14},{17,21},{18,22},{25,29},{26,30}} | collective-permute-start | bytes 1474568 | tf_op jit(solution)/shard_map/ppermute | solution.py:50
  16.3 0.2 constant_dynamic-update-slice_fusion
  16.5 0.1 constant_dynamic-update-slice_fusion.2
  16.6 1.8 %fusion.2 = f32[768]{0:T(1024)S(1)} fusion(bf16[640,768]{1,0:T(8,128)(2,1)S(1)} %get-tuple-element.11, bf16[640,1152]{1,0:T(8,128)(2,1)S(1)} %constant_dynamic-update-slice_fusion.2), kind=kOutput, calls=%fused_computation.4 | convolution fusion | flops 1135115520 | bytes 2460672 | tf_op jit(solution)/shard_map/dot_general | solution.py:15
  18.4 0.0 collective-permute-done.5
  18.4 0.0 collective-permute-done.4
  18.4 0.1 add.16
  18.5 1.8 %fusion.3 = f32[768]{0:T(1024)S(1)} fusion(bf16[640,1152]{1,0:T(8,128)(2,1)S(1)} %constant_dynamic-update-slice_fusion.2, bf16[640,384]{1,0:T(8,128)(2,1)S(1)} %add.16, bf16[640,384]{1,0:T(8,128)(2,1)S(1)} %collective-permute-done.3), kind=kOutput, calls=%fused_computation.5 | convolution fusion | flops 1137081600 | bytes 2460672 | tf_op jit(solution)/shard_map/dot_general | solution.py:15
  20.4 0.0 collective-permute-done.2
  20.4 0.7 %fusion.7 = f32[768]{0:T(1024)S(1)} fusion(bf16[640,384]{1,0:T(8,128)(2,1)S(1)} %collective-permute-done.2, bf16[640,384]{1,0:T(8,128)(2,1)S(1)} %add.16, bf16[640,384]{1,0:T(8,128)(2,1)S(1)} %collective-permute-done.3), kind=kOutput, calls=%fused_computation.11 | convolution fusion | flops 380337408 | bytes 1477632 | tf_op jit(solution)/shard_map/dot_general | solution.py:15
  21.1 0.7 %collective-permute-start.6 = (f32[768]{0:T(1024)S(1)}, f32[768]{0:T(1024)S(1)}, u32[]{:S(2)}, u32[]{:S(2)}) collective-permute-start(f32[768]{0:T(1024)S(1)} %add.17), channel_id=1, source_target_pairs={{5,1},{6,2},{9,5},{10,6},{13,9},{14,10},{21,17},{22,18},{25,21},{2... | collective-permute-start | bytes 9224 | tf_op jit(solution)/shard_map/ppermute | solution.py:57
  21.8 0.7 %fusion.6 = f32[768]{0:T(1024)S(1)} fusion(bf16[640,768]{1,0:T(8,128)(2,1)S(1)} %get-tuple-element.11, bf16[640,384]{1,0:T(8,128)(2,1)S(1)} %collective-permute-done.2), kind=kOutput, calls=%fused_computation.10 | convolution fusion | flops 378371328 | bytes 1477632 | tf_op jit(solution)/shard_map/dot_general | solution.py:15
  22.5 0.0 collective-permute-done.6
  22.5 1.3 %collective-permute-start.7 = (f32[384]{0:T(512)S(1)}, f32[384]{0:T(512)S(1)}, u32[]{:S(2)}, u32[]{:S(2)}) collective-permute-start(f32[384]{0:T(512)S(1)} %slice_add_fusion), channel_id=1, source_target_pairs={{1,0},{2,3},{5,4},{6,7},{9,8},{10,11},{13,12},{14,15},{17,16},{18,... | collective-permute-start | bytes 4616 | tf_op jit(solution)/shard_map/ppermute | solution.py:60
  23.8 18.8 %collective-permute-done.7 = f32[384]{0:T(512)S(1)} collective-permute-done((f32[384]{0:T(512)S(1)}, f32[384]{0:T(512)S(1)}, u32[]{:S(2)}, u32[]{:S(2)}) %collective-permute-start.7) | collective-permute-done | bytes 1568 | tf_op jit(solution)/shard_map/ppermute | solution.py:60
  42.6 0.6 %add_select_fusion = f32[384]{0:T(512)} fusion(f32[384]{0:T(512)S(1)} %collective-permute-done.7, f32[768]{0:T(1024)S(1)} %collective-permute-done.6, f32[768]{0:T(1024)S(1)} %add.15, pred[]{:T(512)S(6)} %or.3), kind=kLoop, calls=%fused_computation.19 | loop fusion | flops 768 | bytes 6145 | tf_op jit(solution)/shard_map/jit(_where)/select_n | solution.py:62
  (3 shorter events, 0.0 us)
Async XLA Ops:
  0.0 14.2 %collective-permute-start = (bf16[640,384]{1,0:T(8,128)(2,1)}, bf16[640,384]{1,0:T(8,128)(2,1)S(1)}, u32[]{:S(2)}, u32[]{:S(2)}) collective-permute-start(bf16[640,384]{1,0:T(8,128)(2,1)} %param.1), channel_id=1, source_target_pairs={{0,1},{3,2},{4,5},{7,6},{8,9},{11,10},{12,13},{15,14},{16,17},{19,... | collective-permute-start | bytes 1474568 | tf_op jit(solution)/shard_map/ppermute | solution.py:31
  4.1 10.2 %collective-permute-start.1 = (bf16[640,384]{1,0:T(8,128)(2,1)}, bf16[640,384]{1,0:T(8,128)(2,1)S(1)}, u32[]{:S(2)}, u32[]{:S(2)}) collective-permute-start(bf16[640,384]{1,0:T(8,128)(2,1)} %param.1), channel_id=1, source_target_pairs={{1,2},{2,1},{5,6},{6,5},{9,10},{10,9},{13,14},{14,13},{17,18},{18,... | collective-permute-start | bytes 1474568 | tf_op jit(solution)/shard_map/ppermute | solution.py:32
  4.8 10.2 %collective-permute-start.3 = (bf16[640,384]{1,0:T(8,128)(2,1)}, bf16[640,384]{1,0:T(8,128)(2,1)S(1)}, u32[]{:S(2)}, u32[]{:S(2)}) collective-permute-start(bf16[640,384]{1,0:T(8,128)(2,1)} %param.1), channel_id=1, source_target_pairs={{1,5},{2,6},{5,9},{6,10},{9,13},{10,14},{4,8},{7,11},{17,21},{18,2... | collective-permute-start | bytes 1474568 | tf_op jit(solution)/shard_map/ppermute | solution.py:42
  14.2 6.2 %collective-permute-start.2 = (bf16[640,384]{1,0:T(8,128)(2,1)S(1)}, bf16[640,384]{1,0:T(8,128)(2,1)S(1)}, u32[]{:S(2)}, u32[]{:S(2)}) collective-permute-start(bf16[640,384]{1,0:T(8,128)(2,1)S(1)} %collective-permute-done), channel_id=1, source_target_pairs={{1,2},{2,1},{5,6},{6,5},{9,10},{10,9},{13,14},{14,13},{17,18},{18,... | collective-permute-start | bytes 1474568 | tf_op jit(solution)/shard_map/ppermute | solution.py:46
  14.9 3.5 %collective-permute-start.5 = (bf16[640,384]{1,0:T(8,128)(2,1)S(1)}, bf16[640,384]{1,0:T(8,128)(2,1)S(1)}, u32[]{:S(2)}, u32[]{:S(2)}) collective-permute-start(bf16[640,384]{1,0:T(8,128)(2,1)S(1)} %collective-permute-done.3), channel_id=1, source_target_pairs={{8,9},{11,10},{24,25},{27,26}} | collective-permute-start | bytes 1474568 | tf_op jit(solution)/shard_map/ppermute | solution.py:50
  15.6 2.8 %collective-permute-start.4 = (bf16[640,384]{1,0:T(8,128)(2,1)S(1)}, bf16[640,384]{1,0:T(8,128)(2,1)S(1)}, u32[]{:S(2)}, u32[]{:S(2)}) collective-permute-start(bf16[640,384]{1,0:T(8,128)(2,1)S(1)} %collective-permute-done), channel_id=1, source_target_pairs={{1,5},{2,6},{9,13},{10,14},{17,21},{18,22},{25,29},{26,30}} | collective-permute-start | bytes 1474568 | tf_op jit(solution)/shard_map/ppermute | solution.py:50
  21.1 1.4 %collective-permute-start.6 = (f32[768]{0:T(1024)S(1)}, f32[768]{0:T(1024)S(1)}, u32[]{:S(2)}, u32[]{:S(2)}) collective-permute-start(f32[768]{0:T(1024)S(1)} %add.17), channel_id=1, source_target_pairs={{5,1},{6,2},{9,5},{10,6},{13,9},{14,10},{21,17},{22,18},{25,21},{2... | collective-permute-start | bytes 9224 | tf_op jit(solution)/shard_map/ppermute | solution.py:57
  22.5 20.1 %collective-permute-start.7 = (f32[384]{0:T(512)S(1)}, f32[384]{0:T(512)S(1)}, u32[]{:S(2)}, u32[]{:S(2)}) collective-permute-start(f32[384]{0:T(512)S(1)} %slice_add_fusion), channel_id=1, source_target_pairs={{1,0},{2,3},{5,4},{6,7},{9,8},{10,11},{13,12},{14,15},{17,16},{18,... | collective-permute-start | bytes 4616 | tf_op jit(solution)/shard_map/ppermute | solution.py:60

commit v13 on v11

--- a/solution.py
+++ b/solution.py
@@ -49,9 +49,12 @@
     prev_adopt = lax.ppermute(adopt, both, on_chip) + lax.ppermute(relay, both, relayed)
     prev = [prev_own, prev_adopt]
     width = own.shape[1]
+    pair, prev_rows = jnp.concatenate([own, adopt], axis=1), jnp.concatenate(prev, axis=1)
+    before = [row_squares(pair, early, scaling), row_squares(prev_rows, early, scaling)]
+    far, before[1] = lax.optimization_barrier((far, before[1]))
     sums = []
-    for rows in (jnp.concatenate([own, adopt], axis=1), jnp.concatenate(prev, axis=1)):
-        total = row_squares(rows, early, scaling) + row_squares(rows, far, scaling)
+    for rows, part in zip((pair, prev_rows), before):
+        total = part + row_squares(rows, far, scaling)
         sums += [total[:width], total[width:]]
     to_end = [((g + 1) * line + 1, g * line) for g in steps]
     to_end += [((g + 1) * line + line - 2, g * line + line - 1) for g in steps]

time: 40.9 us -> 41.3 us (level)
  transfers between devices with their start and end apart: 9 -> 9, of which waited for: 3 -> 3; matrix products, arithmetic and copies ran while one was open for 16% -> 14% of each run, Pallas kernels for 0% -> 0%
where the time goes in v13:
time: 41.3 us; the launch traced here: 40.9 us
  waiting for transfers between devices  19.5 us (47%)
  starting transfers between devices  14 us (34%)
  matrix products  5.04 us (12%)
  local copies, waits for them, and re-layouts  1.36 us (3%)
  other arithmetic  0.72 us (2%)
    ppermute x1, waiting for transfers between devices, hub_plan(): lax.ppermute(sums[1], 'group', [(1, 0), (2, 3)])  8.78 us
    ppermute x1, waiting for transfers between devices, hub_plan(): lax.ppermute(sums[3], both, to_end)  6.41 us
    dot_general x4, matrix products, row_squares(): lax.dot_general(rows, columns, (((0,), (0,)), ((), ())), preferred_elemen...  5.04 us
    ppermute x1, waiting for transfers between devices, hub_plan(): adopt = lax.ppermute(own, 'group', [(0, 1), (3, 2)])  4.34 us
    ppermute x1, starting transfers between devices, hub_plan(): adopt = lax.ppermute(own, 'group', [(0, 1), (3, 2)])  4.05 us
    ppermute x1, starting transfers between devices, hub_plan(): prev_own = lax.ppermute(own, both, onward + ends_across)  3.99 us
    ppermute x1, starting transfers between devices, hub_plan(): lax.ppermute(sums[1], 'group', [(1, 0), (2, 3)])  1.29 us
    ppermute x1, starting transfers between devices, hub_plan(): lax.ppermute(sums[3], both, to_end)  1.29 us
  transfers between devices with their start and end apart: 9, of which 3 were waited for; matrix products, arithmetic and copies ran while one was open for 14% of the time, Pallas kernels for 0%

profile of v13, /device:TPU:1, one launch (start us, length us, event | category | flops | bytes accessed | tf_op | source)
XLA Modules:
  0.0 40.9 jit_solution(10075155172218810077)
XLA Ops:
  0.0 4.0 %collective-permute-start = (bf16[640,384]{1,0:T(8,128)(2,1)}, bf16[640,384]{1,0:T(8,128)(2,1)S(1)}, u32[]{:S(2)}, u32[]{:S(2)}) collective-permute-start(bf16[640,384]{1,0:T(8,128)(2,1)} %param.1), channel_id=1, source_target_pairs={{0,1},{3,2},{4,5},{7,6},{8,9},{11,10},{12,13},{15,14},{16,17},{19,... | collective-permute-start | bytes 1474568 | tf_op jit(solution)/shard_map/ppermute | solution.py:31
  4.1 4.0 %collective-permute-start.2 = (bf16[640,384]{1,0:T(8,128)(2,1)}, bf16[640,384]{1,0:T(8,128)(2,1)S(1)}, u32[]{:S(2)}, u32[]{:S(2)}) collective-permute-start(bf16[640,384]{1,0:T(8,128)(2,1)} %param.1), channel_id=1, source_target_pairs={{1,5},{2,6},{5,9},{6,10},{9,13},{10,14},{4,8},{7,11},{17,21},{18,2... | collective-permute-start | bytes 1474568 | tf_op jit(solution)/shard_map/ppermute | solution.py:42
  8.1 0.7 %collective-permute-start.1 = (bf16[640,384]{1,0:T(8,128)(2,1)}, bf16[640,384]{1,0:T(8,128)(2,1)S(1)}, u32[]{:S(2)}, u32[]{:S(2)}) collective-permute-start(bf16[640,384]{1,0:T(8,128)(2,1)} %param.1), channel_id=1, source_target_pairs={{1,2},{2,1},{5,6},{6,5},{9,10},{10,9},{13,14},{14,13},{17,18},{18,... | collective-permute-start | bytes 1474568 | tf_op jit(solution)/shard_map/ppermute | solution.py:32
  8.8 1.1 %constant_dynamic-update-slice_fusion.4 = (bf16[640,1152]{1,0:T(8,128)(2,1)S(1)}, bf16[640,768]{1,0:T(8,128)(2,1)S(1)}) fusion(bf16[640,384]{1,0:T(8,128)(2,1)} %param.1), kind=kLoop, calls=%fused_computation.17 | loop fusion | bytes 1474560
  9.9 4.3 %collective-permute-done = bf16[640,384]{1,0:T(8,128)(2,1)S(1)} collective-permute-done((bf16[640,384]{1,0:T(8,128)(2,1)}, bf16[640,384]{1,0:T(8,128)(2,1)S(1)}, u32[]{:S(2)}, u32[]{:S(2)}) %collective-permute-start) | collective-permute-done | bytes 491552 | tf_op jit(solution)/shard_map/ppermute | solution.py:31
  14.2 0.0 collective-permute-done.2
  14.2 0.7 %collective-permute-start.3 = (bf16[640,384]{1,0:T(8,128)(2,1)S(1)}, bf16[640,384]{1,0:T(8,128)(2,1)S(1)}, u32[]{:S(2)}, u32[]{:S(2)}) collective-permute-start(bf16[640,384]{1,0:T(8,128)(2,1)S(1)} %collective-permute-done), channel_id=1, source_target_pairs={{1,2},{2,1},{5,6},{6,5},{9,10},{10,9},{13,14},{14,13},{17,18},{18,... | collective-permute-start | bytes 1474568 | tf_op jit(solution)/shard_map/ppermute | solution.py:45
  14.9 0.7 %collective-permute-start.5 = (bf16[640,384]{1,0:T(8,128)(2,1)S(1)}, bf16[640,384]{1,0:T(8,128)(2,1)S(1)}, u32[]{:S(2)}, u32[]{:S(2)}) collective-permute-start(bf16[640,384]{1,0:T(8,128)(2,1)S(1)} %collective-permute-done.2), channel_id=1, source_target_pairs={{8,9},{11,10},{24,25},{27,26}} | collective-permute-start | bytes 1474568 | tf_op jit(solution)/shard_map/ppermute | solution.py:49
  15.6 0.7 %collective-permute-start.4 = (bf16[640,384]{1,0:T(8,128)(2,1)S(1)}, bf16[640,384]{1,0:T(8,128)(2,1)S(1)}, u32[]{:S(2)}, u32[]{:S(2)}) collective-permute-start(bf16[640,384]{1,0:T(8,128)(2,1)S(1)} %collective-permute-done), channel_id=1, source_target_pairs={{1,5},{2,6},{9,13},{10,14},{17,21},{18,22},{25,29},{26,30}} | collective-permute-start | bytes 1474568 | tf_op jit(solution)/shard_map/ppermute | solution.py:49
  16.3 0.2 constant_dynamic-update-slice_fusion.3
  16.5 0.0 collective-permute-done.1
  16.5 0.1 constant_dynamic-update-slice_fusion.2
  16.6 1.8 %fusion.2 = f32[768]{0:T(1024)S(1)} fusion(bf16[640,768]{1,0:T(8,128)(2,1)S(1)} %get-tuple-element.14, bf16[640,1152]{1,0:T(8,128)(2,1)S(1)} %constant_dynamic-update-slice_fusion.2), kind=kOutput, calls=%fused_computation.4 | convolution fusion | flops 1135115520 | bytes 2460672 | tf_op jit(solution)/shard_map/dot_general | solution.py:15
  18.4 0.0 collective-permute-done.4
  18.4 0.0 collective-permute-done.5
  18.4 0.1 add.15
  18.5 1.8 %fusion.3 = f32[768]{0:T(1024)S(1)} fusion(bf16[640,1152]{1,0:T(8,128)(2,1)S(1)} %constant_dynamic-update-slice_fusion.2, bf16[640,384]{1,0:T(8,128)(2,1)S(1)} %add.15, bf16[640,384]{1,0:T(8,128)(2,1)S(1)} %collective-permute-done.2), kind=kOutput, calls=%fused_computation.5 | convolution fusion | flops 1137081600 | bytes 2460672 | tf_op jit(solution)/shard_map/dot_general | solution.py:15
  20.4 0.0 collective-permute-done.3
  20.4 0.7 %fusion.6 = f32[768]{0:T(1024)S(1)} fusion(bf16[640,768]{1,0:T(8,128)(2,1)S(1)} %get-tuple-element.14, bf16[640,384]{1,0:T(8,128)(2,1)S(1)} %collective-permute-done.3), kind=kOutput, calls=%fused_computation.10 | convolution fusion | flops 378371328 | bytes 1477632 | tf_op jit(solution)/shard_map/dot_general | solution.py:15
  21.1 1.3 %collective-permute-start.7 = (f32[384]{0:T(512)S(1)}, f32[384]{0:T(512)S(1)}, u32[]{:S(2)}, u32[]{:S(2)}) collective-permute-start(f32[384]{0:T(512)S(1)} %slice.14), channel_id=1, source_target_pairs={{1,0},{2,3},{5,4},{6,7},{9,8},{10,11},{13,12},{14,15},{17,16},{18,... | collective-permute-start | bytes 4616 | tf_op jit(solution)/shard_map/ppermute | solution.py:62
  22.4 0.7 %fusion.7 = f32[768]{0:T(1024)S(1)} fusion(bf16[640,384]{1,0:T(8,128)(2,1)S(1)} %collective-permute-done.3, bf16[640,384]{1,0:T(8,128)(2,1)S(1)} %add.15, bf16[640,384]{1,0:T(8,128)(2,1)S(1)} %collective-permute-done.2), kind=kOutput, calls=%fused_computation.11 | convolution fusion | flops 380337408 | bytes 1477632 | tf_op jit(solution)/shard_map/dot_general | solution.py:15
  23.1 1.3 %collective-permute-start.8 = (f32[384]{0:T(512)S(1)}, f32[384]{0:T(512)S(1)}, u32[]{:S(2)}, u32[]{:S(2)}) collective-permute-start(f32[384]{0:T(512)S(1)} %get-tuple-element.18), channel_id=1, source_target_pairs={{5,0},{9,4},{13,8},{6,3},{10,7},{14,11},{21,16},{25,20},{29,24},{2... | collective-permute-start | bytes 4616 | tf_op jit(solution)/shard_map/ppermute | solution.py:62
  24.4 0.7 %collective-permute-start.6 = (f32[384]{0:T(512)S(1)}, f32[384]{0:T(512)S(1)}, u32[]{:S(2)}, u32[]{:S(2)}) collective-permute-start(f32[384]{0:T(512)S(1)} %get-tuple-element.17), channel_id=1, source_target_pairs={{5,1},{6,2},{9,5},{10,6},{13,9},{14,10},{21,17},{22,18},{25,21},{2... | collective-permute-start | bytes 4616 | tf_op jit(solution)/shard_map/ppermute | solution.py:61
  25.1 8.8 %collective-permute-done.7 = f32[384]{0:T(512)S(1)} collective-permute-done((f32[384]{0:T(512)S(1)}, f32[384]{0:T(512)S(1)}, u32[]{:S(2)}, u32[]{:S(2)}) %collective-permute-start.7) | collective-permute-done | bytes 1568 | tf_op jit(solution)/shard_map/ppermute | solution.py:62
  33.9 6.4 %collective-permute-done.8 = f32[384]{0:T(512)S(1)} collective-permute-done((f32[384]{0:T(512)S(1)}, f32[384]{0:T(512)S(1)}, u32[]{:S(2)}, u32[]{:S(2)}) %collective-permute-start.8) | collective-permute-done | bytes 1568 | tf_op jit(solution)/shard_map/ppermute | solution.py:62
  40.3 0.0 collective-permute-done.6
  40.3 0.6 %add_select_fusion = f32[384]{0:T(512)} fusion(f32[384]{0:T(512)S(1)} %collective-permute-done.7, f32[384]{0:T(512)S(1)} %collective-permute-done.8, f32[384]{0:T(512)S(1)} %collective-permute-done.6, f32[768]{0:T(1024)S(1)} %add.16, pred[]{:T(512)S(6)} %or.3), kind=kLoop, calls=%fused_computation.18 | loop fusion | flops 1152 | bytes 7681 | tf_op jit(solution)/shard_map/jit(_where)/select_n | solution.py:64
  (4 shorter events, 0.0 us)
Async XLA Ops:
  0.0 14.2 %collective-permute-start = (bf16[640,384]{1,0:T(8,128)(2,1)}, bf16[640,384]{1,0:T(8,128)(2,1)S(1)}, u32[]{:S(2)}, u32[]{:S(2)}) collective-permute-start(bf16[640,384]{1,0:T(8,128)(2,1)} %param.1), channel_id=1, source_target_pairs={{0,1},{3,2},{4,5},{7,6},{8,9},{11,10},{12,13},{15,14},{16,17},{19,... | collective-permute-start | bytes 1474568 | tf_op jit(solution)/shard_map/ppermute | solution.py:31
  4.1 10.2 %collective-permute-start.2 = (bf16[640,384]{1,0:T(8,128)(2,1)}, bf16[640,384]{1,0:T(8,128)(2,1)S(1)}, u32[]{:S(2)}, u32[]{:S(2)}) collective-permute-start(bf16[640,384]{1,0:T(8,128)(2,1)} %param.1), channel_id=1, source_target_pairs={{1,5},{2,6},{5,9},{6,10},{9,13},{10,14},{4,8},{7,11},{17,21},{18,2... | collective-permute-start | bytes 1474568 | tf_op jit(solution)/shard_map/ppermute | solution.py:42
  8.1 8.4 %collective-permute-start.1 = (bf16[640,384]{1,0:T(8,128)(2,1)}, bf16[640,384]{1,0:T(8,128)(2,1)S(1)}, u32[]{:S(2)}, u32[]{:S(2)}) collective-permute-start(bf16[640,384]{1,0:T(8,128)(2,1)} %param.1), channel_id=1, source_target_pairs={{1,2},{2,1},{5,6},{6,5},{9,10},{10,9},{13,14},{14,13},{17,18},{18,... | collective-permute-start | bytes 1474568 | tf_op jit(solution)/shard_map/ppermute | solution.py:32
  14.2 6.2 %collective-permute-start.3 = (bf16[640,384]{1,0:T(8,128)(2,1)S(1)}, bf16[640,384]{1,0:T(8,128)(2,1)S(1)}, u32[]{:S(2)}, u32[]{:S(2)}) collective-permute-start(bf16[640,384]{1,0:T(8,128)(2,1)S(1)} %collective-permute-done), channel_id=1, source_target_pairs={{1,2},{2,1},{5,6},{6,5},{9,10},{10,9},{13,14},{14,13},{17,18},{18,... | collective-permute-start | bytes 1474568 | tf_op jit(solution)/shard_map/ppermute | solution.py:45
  14.9 3.5 %collective-permute-start.5 = (bf16[640,384]{1,0:T(8,128)(2,1)S(1)}, bf16[640,384]{1,0:T(8,128)(2,1)S(1)}, u32[]{:S(2)}, u32[]{:S(2)}) collective-permute-start(bf16[640,384]{1,0:T(8,128)(2,1)S(1)} %collective-permute-done.2), channel_id=1, source_target_pairs={{8,9},{11,10},{24,25},{27,26}} | collective-permute-start | bytes 1474568 | tf_op jit(solution)/shard_map/ppermute | solution.py:49
  15.6 2.8 %collective-permute-start.4 = (bf16[640,384]{1,0:T(8,128)(2,1)S(1)}, bf16[640,384]{1,0:T(8,128)(2,1)S(1)}, u32[]{:S(2)}, u32[]{:S(2)}) collective-permute-start(bf16[640,384]{1,0:T(8,128)(2,1)S(1)} %collective-permute-done), channel_id=1, source_target_pairs={{1,5},{2,6},{9,13},{10,14},{17,21},{18,22},{25,29},{26,30}} | collective-permute-start | bytes 1474568 | tf_op jit(solution)/shard_map/ppermute | solution.py:49
  21.1 12.8 %collective-permute-start.7 = (f32[384]{0:T(512)S(1)}, f32[384]{0:T(512)S(1)}, u32[]{:S(2)}, u32[]{:S(2)}) collective-permute-start(f32[384]{0:T(512)S(1)} %slice.14), channel_id=1, source_target_pairs={{1,0},{2,3},{5,4},{6,7},{9,8},{10,11},{13,12},{14,15},{17,16},{18,... | collective-permute-start | bytes 4616 | tf_op jit(solution)/shard_map/ppermute | solution.py:62
  23.1 17.2 %collective-permute-start.8 = (f32[384]{0:T(512)S(1)}, f32[384]{0:T(512)S(1)}, u32[]{:S(2)}, u32[]{:S(2)}) collective-permute-start(f32[384]{0:T(512)S(1)} %get-tuple-element.18), channel_id=1, source_target_pairs={{5,0},{9,4},{13,8},{6,3},{10,7},{14,11},{21,16},{25,20},{29,24},{2... | collective-permute-start | bytes 4616 | tf_op jit(solution)/shard_map/ppermute | solution.py:62
  24.4 15.9 %collective-permute-start.6 = (f32[384]{0:T(512)S(1)}, f32[384]{0:T(512)S(1)}, u32[]{:S(2)}, u32[]{:S(2)}) collective-permute-start(f32[384]{0:T(512)S(1)} %get-tuple-element.17), channel_id=1, source_target_pairs={{5,1},{6,2},{9,5},{10,6},{13,9},{14,10},{21,17},{22,18},{25,21},{2... | collective-permute-start | bytes 4616 | tf_op jit(solution)/shard_map/ppermute | solution.py:61
